TPU v7x, 128 devices: a whole 4x4x4 slice. The times are simulated.
128 devices in a mesh: dp: 8 (over z, core), ctx: 16 (over y, x).
Axes of the slice: x: 4, y: 4, z: 4, core: 2. Of those that a mesh axis runs over, the one named last changes fastest.
Arguments:
- queries: bfloat16 [8, 2048, 6144], P('dp', 'ctx'), may hold values from -6 to 6
- kv_proj: bfloat16 [8, 4096, 1024], P('dp', 'ctx'), may hold values from -6 to 6
- hidden: bfloat16 [8, 4096, 12288], P('dp', 'ctx'), may hold values from -0.119628906 to 0.119628906
- grad_out: bfloat16 [8, 2048, 6144], P('dp', 'ctx'), may hold values from -6 to 6
- doc_lengths: int32 [8, 256], P('dp'), may hold values from 1 to 8192, 262144 in all within a row
- slab_offsets: int32 [8], P('dp'), may hold values from 0 to 260096
Outputs:
- attended: bfloat16 [8, 2048, 6144], P('dp', 'ctx')
- grad_queries: bfloat16 [8, 2048, 6144], P('dp', 'ctx')
- grad_kv: bfloat16 [8, 4096, 1024], P('dp', 'ctx')
- grad_weight: float32 [12288, 1024], P('ctx', 'dp')
All inputs are finite; a program needn't handle non-finite values.
Results may differ from a plain program's by a relative error of at most 0.025.
Values may be sent and summed in bfloat16 or wider, within the bound.
No kernel may reach another device: no remote copies, remote signals or barrier semaphores. Data moves between devices by JAX's collectives and lax.ppermute only.
A program may use at most 192 MiB of HBM per device.

v0:
```python
import jax
import jax.numpy as jnp
from jax import lax
from jax.sharding import PartitionSpec as P

HEAD_FEATURES = 128
KEY_VALUE_HEADS = 4
WINDOW = 2048


def doc_index(positions, bounds):
    return jnp.sum(
        (bounds[None, :] <= positions[:, None]).astype(jnp.int32), axis=1, dtype=jnp.int32
    )


def band_mask(anchor, row_count, key_span, offset, bounds):
    query_index = anchor + jnp.arange(row_count, dtype=jnp.int32)
    key_index = anchor + jnp.arange(key_span, dtype=jnp.int32)
    query_pos = offset + query_index
    key_pos = offset - WINDOW + key_index
    same_doc = doc_index(query_pos, bounds)[:, None] == doc_index(key_pos, bounds)[None, :]
    after_query = key_index[None, :] > query_index[:, None]
    within = key_index[None, :] <= query_index[:, None] + WINDOW
    return after_query & within & (key_pos >= 0)[None, :] & same_doc


def band_block(query_block, key_block, value_block, upstream_gradient, allowed):
    factor = HEAD_FEATURES ** (-0.5)
    f32 = jnp.float32
    scores = (
        jnp.einsum("qhgd,khd->hgqk", query_block, key_block, preferred_element_type=f32) * factor
    )
    scores = jnp.where(allowed[None, None], scores, -1e30)
    maxima = jnp.max(scores, axis=-1, keepdims=True)
    raised = jnp.exp(scores - maxima)
    weights = raised / jnp.sum(raised, axis=-1, keepdims=True)
    weights_low = weights.astype(jnp.bfloat16)
    attended = jnp.einsum(
        "hgqk,khd->qhgd", weights_low, value_block, preferred_element_type=f32
    ).astype(jnp.bfloat16)
    grad_probs = jnp.einsum(
        "qhgd,khd->hgqk", upstream_gradient, value_block, preferred_element_type=f32
    )
    deltas = jnp.einsum("qhgd,qhgd->hgq", upstream_gradient, attended, preferred_element_type=f32)
    grad_scores = (weights * (grad_probs - deltas[..., None]) * factor).astype(jnp.bfloat16)
    grad_query = jnp.einsum(
        "hgqk,khd->qhgd", grad_scores, key_block, preferred_element_type=f32
    ).astype(jnp.bfloat16)
    grad_key = jnp.einsum("hgqk,qhgd->khd", grad_scores, query_block, preferred_element_type=f32)
    grad_value = jnp.einsum(
        "hgqk,qhgd->khd", weights_low, upstream_gradient, preferred_element_type=f32
    )
    return (attended, grad_query, jnp.stack([grad_key, grad_value], axis=2))


def band_attention(query_all, upstream_all, pair_all, anchor, offset, bounds, block_rows):
    query_total_count = query_all.shape[0]
    key_total_count = pair_all.shape[0]
    head_count = query_all.shape[1]
    key_span = block_rows + WINDOW

    def step(running, block_index):
        first_row = block_index * block_rows
        query_block = lax.dynamic_slice_in_dim(query_all, first_row, block_rows, 0)
        upstream_gradient = lax.dynamic_slice_in_dim(upstream_all, first_row, block_rows, 0)
        pair_block = lax.dynamic_slice_in_dim(pair_all, first_row, key_span, 0)
        allowed = band_mask(anchor + first_row, block_rows, key_span, offset, bounds)
        attended, grad_query, grad_pair = band_block(
            query_block, pair_block[:, :, 0], pair_block[:, :, 1], upstream_gradient, allowed
        )
        previous = lax.dynamic_slice_in_dim(running, first_row, key_span, 0)
        running = lax.dynamic_update_slice_in_dim(running, previous + grad_pair, first_row, 0)
        return (running, (attended, grad_query))

    initial = jnp.zeros((key_total_count, head_count, 2, HEAD_FEATURES), jnp.float32)
    grads, outputs = lax.scan(
        step, initial, jnp.arange(query_total_count // block_rows, dtype=jnp.int32)
    )
    attended, grad_query = outputs
    return (
        attended.reshape(query_total_count, -1),
        grad_query.reshape(query_total_count, -1),
        grads.reshape(key_total_count, -1),
    )


def head_attention(head_queries, head_upstream, head_keys, offset, bounds):
    row_count = head_queries.shape[0]
    heads_here = head_queries.shape[1] // HEAD_FEATURES
    return band_attention(
        head_queries.reshape(row_count, 1, heads_here, HEAD_FEATURES),
        head_upstream.reshape(row_count, 1, heads_here, HEAD_FEATURES),
        head_keys.reshape(head_keys.shape[0], 1, 2, HEAD_FEATURES),
        0,
        offset,
        bounds,
        min(512, row_count),
    )


def local(queries, kv_proj, hidden, grad_out, doc_lengths, slab_offsets):
    query_matrix_rows = queries[0]
    upstream_gradient = grad_out[0]
    key_matrix_rows = kv_proj[0]
    hidden_rows = hidden[0]
    bounds = jnp.cumsum(doc_lengths[0], dtype=jnp.int32)
    offset = slab_offsets[0]
    key_value_width = 2 * KEY_VALUE_HEADS * HEAD_FEATURES
    hidden_cols = lax.all_to_all(hidden_rows, "ctx", split_axis=1, concat_axis=0, tiled=True)
    repeat_heads = lax.axis_size("ctx") // KEY_VALUE_HEADS
    key_total_count = key_matrix_rows.shape[0]
    copies = jnp.broadcast_to(
        key_matrix_rows.reshape(key_total_count, KEY_VALUE_HEADS, 1, 2 * HEAD_FEATURES),
        (key_total_count, KEY_VALUE_HEADS, repeat_heads, 2 * HEAD_FEATURES),
    ).reshape(key_total_count, KEY_VALUE_HEADS * repeat_heads * 2 * HEAD_FEATURES)
    head_queries, head_upstream, head_keys = (
        lax.all_to_all(query_matrix_rows, "ctx", split_axis=1, concat_axis=0, tiled=True),
        lax.all_to_all(upstream_gradient, "ctx", split_axis=1, concat_axis=0, tiled=True),
        lax.all_to_all(copies, "ctx", split_axis=1, concat_axis=0, tiled=True),
    )
    attended_heads, grad_query_heads, grad_head = head_attention(
        head_queries, head_upstream, head_keys, offset, bounds
    )
    attended, grad_query = (
        lax.all_to_all(attended_heads, "ctx", split_axis=0, concat_axis=1, tiled=True),
        lax.all_to_all(grad_query_heads, "ctx", split_axis=0, concat_axis=1, tiled=True),
    )
    partial_sums = lax.all_to_all(grad_head, "ctx", split_axis=0, concat_axis=1, tiled=True)
    grad_keys = jnp.sum(
        partial_sums.reshape(
            partial_sums.shape[0], KEY_VALUE_HEADS, repeat_heads, 2 * HEAD_FEATURES
        ),
        axis=2,
    ).reshape(partial_sums.shape[0], key_value_width)
    grad_low = grad_keys.astype(jnp.bfloat16)
    local_weight = jnp.einsum(
        "kd,kc->dc",
        hidden_cols,
        lax.all_gather(grad_low, "ctx", axis=0, tiled=True),
        preferred_element_type=jnp.float32,
    )
    summed = lax.psum(local_weight.astype(jnp.bfloat16), "dp").astype(jnp.float32)
    columns_dp = key_value_width // lax.axis_size("dp")
    grad_weight = lax.dynamic_slice_in_dim(summed, lax.axis_index("dp") * columns_dp, columns_dp, 1)
    return (attended[None], grad_query[None], grad_low[None], grad_weight)


def solution(mesh):
    in_specs = (
        P("dp", "ctx", None),
        P("dp", "ctx", None),
        P("dp", "ctx", None),
        P("dp", "ctx", None),
        P("dp", None),
        P("dp"),
    )
    out_specs = (P("dp", "ctx", None), P("dp", "ctx", None), P("dp", "ctx", None), P("ctx", "dp"))
    return jax.shard_map(local, mesh=mesh, in_specs=in_specs, out_specs=out_specs, check_vma=False)
```

profile of v0, /device:TPU:0, one launch (start us, length us, event | category | flops | bytes accessed | tf_op | source)
XLA Modules:
  0.0 690.2 jit_solution(8261273656922120973)
XLA Ops:
  9.9 7.1 %all-to-all-start = ((bf16[128,16,384]{0,2,1:T(8,128)(2,1)}), bf16[128,16,384]{0,2,1:T(8,128)(2,1)S(1)}, u32[]{:S(2)}, u32[]{:S(2)}) async-start(bf16[128,16,384]{0,2,1:T(8,128)(2,1)} %bitcast.36), calls=%async_computation | async-start | bytes 3145728 | tf_op jit(solution)/shard_map/all_to_all | solution.py:118
  18.6 22.9 %all-to-all-done = bf16[128,16,384]{0,2,1:T(8,128)(2,1)S(1)} async-done(((bf16[128,16,384]{0,2,1:T(8,128)(2,1)}), bf16[128,16,384]{0,2,1:T(8,128)(2,1)S(1)}, u32[]{:S(2)}, u32[]{:S(2)}) %all-to-all-start) | async-done | bytes 1572896 | tf_op jit(solution)/shard_map/all_to_all | solution.py:118
  41.5 3.7 all-to-all-start.2
  47.3 21.2 %all-to-all-done.2 = bf16[128,16,384]{0,2,1:T(8,128)(2,1)S(1)} async-done(((bf16[128,16,384]{0,2,1:T(8,128)(2,1)}), bf16[128,16,384]{0,2,1:T(8,128)(2,1)S(1)}, u32[]{:S(2)}, u32[]{:S(2)}) %all-to-all-start.2) | async-done | bytes 1572896 | tf_op jit(solution)/shard_map/all_to_all | solution.py:119
  71.5 3.7 all-to-all-start.1
  76.5 3.6 copy.126
  80.2 3.7 reshape.310
  83.9 3.6 copy.130
  87.4 3.7 reshape.314
  91.2 14.8 %all-to-all-done.1 = bf16[256,16,256]{0,2,1:T(8,128)(2,1)S(1)} async-done(((bf16[256,16,256]{0,2,1:T(8,128)(2,1)}), bf16[256,16,256]{0,2,1:T(8,128)(2,1)S(1)}, u32[]{:S(2)}, u32[]{:S(2)}) %all-to-all-start.1) | async-done | bytes 2097184 | tf_op jit(solution)/shard_map/all_to_all | solution.py:120
  108.5 4.2 reshape.313
  115.2 260.2 %while.16 = (s32[]{:T(128)}, f32[4096,1,2,128]{0,3,2,1:T(8,128)}, bf16[4,512,1,3,128]{1,4,3,2,0:T(8,128)(2,1)}, bf16[4,512,1,3,128]{1,4,3,2,0:T(8,128)(2,1)}, s3...) while((s32[]{:T(128)}, f32[4096,1,2,128]{0,3,2,1:T(8,128)}, ...), condition=%wide.region_7.8_spmd, body=%wide.region_2.7_spmd.sunk | while | flops 6150822912 | bytes 191393264 | solution.py:77
  135.4 9.8 %fusion.74 = (f32[3,512]{1,0:T(4,128)S(1)}, f32[2560,512,3]{1,0,2:T(8,128)}) fusion(pred[512,2560]{0,1:T(8,128)(4,1)S(1)} %compare_and_fusion.2, bf16[2048,1,3,128]{0,3,2,1:T(8,128)(2,1)} %get-tuple-element.361, s32[]{:T(128)S(6)} %select_n.55, bf16[4096,1,2,128]{0,3,2,1:T(8,128)(2,1)} %get-tuple-element.365, s32[]{:T(128)S(6)} %select_n.54), kind=kOutput, calls=%fused_computation.8.clone.1 | convolution fusion | flops 1018427904 | bytes 18094088 | tf_op jit(solution)/shard_map/while/body/eval_jaxpr/qhgd,khd->hgqk/dot_general | solution.py:32
  145.2 8.9 %fusion.75 = f32[3,512]{1,0:T(4,128)S(1)} fusion(f32[2560,512,3]{1,0,2:T(8,128)} %get-tuple-element.318, f32[3,512]{1,0:T(4,128)S(1)} %get-tuple-element.319, pred[512,2560]{0,1:T(8,128)(4,1)S(1)} %compare_and_fusion.2), kind=kLoop, calls=%fused_computation.7.clone.1 | loop fusion | flops 15727104 | bytes 17051648 | tf_op jit(solution)/shard_map/while/body/eval_jaxpr/reduce_sum | solution.py:37
  154.1 9.7 %fusion.76 = f32[2560,1,1,128]{0,3,2,1:T(8,128)} fusion(bf16[512,1,3,128]{0,3,2,1:T(8,128)(2,1)S(1)} %constant_dynamic-slice_fusion.2, f32[3,512]{1,0:T(4,128)S(1)} %fusion.75, f32[3,512]{1,0:T(4,128)S(1)} %get-tuple-element.319, f32[2560,512,3]{1,0,2:T(8,128)} %get-tuple-element.318, pred[512,2560]{0,1:T(8,128)(4,1)S(1)} %compare_and_fusion.2), kind=kOutput, calls=%fused_computation.19.clone.1 | convolution fusion | flops 1026293760 | bytes 18755584 | tf_op jit(solution)/shard_map/while/body/eval_jaxpr/hgqk,qhgd->khd/dot_general | solution.py:51
  164.3 8.6 %multiply_reduce_fusion.2 = (f32[3,512]{1,0:T(4,128)S(1)}, bf16[128,3,512]{2,0,1:T(8,128)(2,1)S(1)}) fusion(f32[3,512,128]{1,2,0:T(8,128)S(1)} %copy.176, f32[3,512]{1,0:T(4,128)S(1)} %fusion.75, f32[3,512]{1,0:T(4,128)S(1)} %get-tuple-element.319, f32[2560,512,3]{1,0,2:T(8,128)} %get-tuple-element.318, ...), kind=kOutput, calls=%fused_computation.28.clone.1 | convolution fusion | flops 1027078656 | bytes 18892808 | tf_op jit(solution)/shard_map/while/body/eval_jaxpr/hgqk,khd->qhgd/dot_general | solution.py:39
  172.9 9.5 %fusion.77 = bf16[1,3,512,2560]{2,3,1,0:T(8,128)(2,1)S(1)} fusion(f32[3,512]{1,0:T(4,128)S(1)} %get-tuple-element.320, f32[3,512]{1,0:T(4,128)S(1)} %fusion.75, f32[3,512]{1,0:T(4,128)S(1)} %get-tuple-element.319, f32[2560,512,3]{1,0,2:T(8,128)} %get-tuple-element.318, pred[512,2560]{0,1:T(8,128)(4,1)S(1)} %compare_and_fusion.2, ...), kind=kOutput, calls=%fused_computation.3.clone.1 | convolution fusion | flops 1038090240 | bytes 25976840 | tf_op jit(solution)/shard_map/while/body/eval_jaxpr/qhgd,khd->hgqk/dot_general | solution.py:42
  182.5 3.7 fusion.78
  197.2 9.8 %fusion.74 = (f32[3,512]{1,0:T(4,128)S(1)}, f32[2560,512,3]{1,0,2:T(8,128)}) fusion(pred[512,2560]{0,1:T(8,128)(4,1)S(1)} %compare_and_fusion.2, bf16[2048,1,3,128]{0,3,2,1:T(8,128)(2,1)} %get-tuple-element.361, s32[]{:T(128)S(6)} %select_n.55, bf16[4096,1,2,128]{0,3,2,1:T(8,128)(2,1)} %get-tuple-element.365, s32[]{:T(128)S(6)} %select_n.54), kind=kOutput, calls=%fused_computation.8.clone.1 | convolution fusion | flops 1018427904 | bytes 18094088 | tf_op jit(solution)/shard_map/while/body/eval_jaxpr/qhgd,khd->hgqk/dot_general | solution.py:32
  207.0 8.9 %fusion.75 = f32[3,512]{1,0:T(4,128)S(1)} fusion(f32[2560,512,3]{1,0,2:T(8,128)} %get-tuple-element.318, f32[3,512]{1,0:T(4,128)S(1)} %get-tuple-element.319, pred[512,2560]{0,1:T(8,128)(4,1)S(1)} %compare_and_fusion.2), kind=kLoop, calls=%fused_computation.7.clone.1 | loop fusion | flops 15727104 | bytes 17051648 | tf_op jit(solution)/shard_map/while/body/eval_jaxpr/reduce_sum | solution.py:37
  215.8 9.7 %fusion.76 = f32[2560,1,1,128]{0,3,2,1:T(8,128)} fusion(bf16[512,1,3,128]{0,3,2,1:T(8,128)(2,1)S(1)} %constant_dynamic-slice_fusion.2, f32[3,512]{1,0:T(4,128)S(1)} %fusion.75, f32[3,512]{1,0:T(4,128)S(1)} %get-tuple-element.319, f32[2560,512,3]{1,0,2:T(8,128)} %get-tuple-element.318, pred[512,2560]{0,1:T(8,128)(4,1)S(1)} %compare_and_fusion.2), kind=kOutput, calls=%fused_computation.19.clone.1 | convolution fusion | flops 1026293760 | bytes 18755584 | tf_op jit(solution)/shard_map/while/body/eval_jaxpr/hgqk,qhgd->khd/dot_general | solution.py:51
  226.1 8.6 %multiply_reduce_fusion.2 = (f32[3,512]{1,0:T(4,128)S(1)}, bf16[128,3,512]{2,0,1:T(8,128)(2,1)S(1)}) fusion(f32[3,512,128]{1,2,0:T(8,128)S(1)} %copy.176, f32[3,512]{1,0:T(4,128)S(1)} %fusion.75, f32[3,512]{1,0:T(4,128)S(1)} %get-tuple-element.319, f32[2560,512,3]{1,0,2:T(8,128)} %get-tuple-element.318, ...), kind=kOutput, calls=%fused_computation.28.clone.1 | convolution fusion | flops 1027078656 | bytes 18892808 | tf_op jit(solution)/shard_map/while/body/eval_jaxpr/hgqk,khd->qhgd/dot_general | solution.py:39
  234.7 9.5 %fusion.77 = bf16[1,3,512,2560]{2,3,1,0:T(8,128)(2,1)S(1)} fusion(f32[3,512]{1,0:T(4,128)S(1)} %get-tuple-element.320, f32[3,512]{1,0:T(4,128)S(1)} %fusion.75, f32[3,512]{1,0:T(4,128)S(1)} %get-tuple-element.319, f32[2560,512,3]{1,0,2:T(8,128)} %get-tuple-element.318, pred[512,2560]{0,1:T(8,128)(4,1)S(1)} %compare_and_fusion.2, ...), kind=kOutput, calls=%fused_computation.3.clone.1 | convolution fusion | flops 1038090240 | bytes 25976840 | tf_op jit(solution)/shard_map/while/body/eval_jaxpr/qhgd,khd->hgqk/dot_general | solution.py:42
  244.2 3.7 fusion.78
  258.9 9.8 %fusion.74 = (f32[3,512]{1,0:T(4,128)S(1)}, f32[2560,512,3]{1,0,2:T(8,128)}) fusion(pred[512,2560]{0,1:T(8,128)(4,1)S(1)} %compare_and_fusion.2, bf16[2048,1,3,128]{0,3,2,1:T(8,128)(2,1)} %get-tuple-element.361, s32[]{:T(128)S(6)} %select_n.55, bf16[4096,1,2,128]{0,3,2,1:T(8,128)(2,1)} %get-tuple-element.365, s32[]{:T(128)S(6)} %select_n.54), kind=kOutput, calls=%fused_computation.8.clone.1 | convolution fusion | flops 1018427904 | bytes 18094088 | tf_op jit(solution)/shard_map/while/body/eval_jaxpr/qhgd,khd->hgqk/dot_general | solution.py:32
  268.7 8.9 %fusion.75 = f32[3,512]{1,0:T(4,128)S(1)} fusion(f32[2560,512,3]{1,0,2:T(8,128)} %get-tuple-element.318, f32[3,512]{1,0:T(4,128)S(1)} %get-tuple-element.319, pred[512,2560]{0,1:T(8,128)(4,1)S(1)} %compare_and_fusion.2), kind=kLoop, calls=%fused_computation.7.clone.1 | loop fusion | flops 15727104 | bytes 17051648 | tf_op jit(solution)/shard_map/while/body/eval_jaxpr/reduce_sum | solution.py:37
  277.6 9.7 %fusion.76 = f32[2560,1,1,128]{0,3,2,1:T(8,128)} fusion(bf16[512,1,3,128]{0,3,2,1:T(8,128)(2,1)S(1)} %constant_dynamic-slice_fusion.2, f32[3,512]{1,0:T(4,128)S(1)} %fusion.75, f32[3,512]{1,0:T(4,128)S(1)} %get-tuple-element.319, f32[2560,512,3]{1,0,2:T(8,128)} %get-tuple-element.318, pred[512,2560]{0,1:T(8,128)(4,1)S(1)} %compare_and_fusion.2), kind=kOutput, calls=%fused_computation.19.clone.1 | convolution fusion | flops 1026293760 | bytes 18755584 | tf_op jit(solution)/shard_map/while/body/eval_jaxpr/hgqk,qhgd->khd/dot_general | solution.py:51
  287.9 8.6 %multiply_reduce_fusion.2 = (f32[3,512]{1,0:T(4,128)S(1)}, bf16[128,3,512]{2,0,1:T(8,128)(2,1)S(1)}) fusion(f32[3,512,128]{1,2,0:T(8,128)S(1)} %copy.176, f32[3,512]{1,0:T(4,128)S(1)} %fusion.75, f32[3,512]{1,0:T(4,128)S(1)} %get-tuple-element.319, f32[2560,512,3]{1,0,2:T(8,128)} %get-tuple-element.318, ...), kind=kOutput, calls=%fused_computation.28.clone.1 | convolution fusion | flops 1027078656 | bytes 18892808 | tf_op jit(solution)/shard_map/while/body/eval_jaxpr/hgqk,khd->qhgd/dot_general | solution.py:39
  296.4 9.5 %fusion.77 = bf16[1,3,512,2560]{2,3,1,0:T(8,128)(2,1)S(1)} fusion(f32[3,512]{1,0:T(4,128)S(1)} %get-tuple-element.320, f32[3,512]{1,0:T(4,128)S(1)} %fusion.75, f32[3,512]{1,0:T(4,128)S(1)} %get-tuple-element.319, f32[2560,512,3]{1,0,2:T(8,128)} %get-tuple-element.318, pred[512,2560]{0,1:T(8,128)(4,1)S(1)} %compare_and_fusion.2, ...), kind=kOutput, calls=%fused_computation.3.clone.1 | convolution fusion | flops 1038090240 | bytes 25976840 | tf_op jit(solution)/shard_map/while/body/eval_jaxpr/qhgd,khd->hgqk/dot_general | solution.py:42
  306.0 3.7 fusion.78
  320.7 9.8 %fusion.74 = (f32[3,512]{1,0:T(4,128)S(1)}, f32[2560,512,3]{1,0,2:T(8,128)}) fusion(pred[512,2560]{0,1:T(8,128)(4,1)S(1)} %compare_and_fusion.2, bf16[2048,1,3,128]{0,3,2,1:T(8,128)(2,1)} %get-tuple-element.361, s32[]{:T(128)S(6)} %select_n.55, bf16[4096,1,2,128]{0,3,2,1:T(8,128)(2,1)} %get-tuple-element.365, s32[]{:T(128)S(6)} %select_n.54), kind=kOutput, calls=%fused_computation.8.clone.1 | convolution fusion | flops 1018427904 | bytes 18094088 | tf_op jit(solution)/shard_map/while/body/eval_jaxpr/qhgd,khd->hgqk/dot_general | solution.py:32
  330.5 8.9 %fusion.75 = f32[3,512]{1,0:T(4,128)S(1)} fusion(f32[2560,512,3]{1,0,2:T(8,128)} %get-tuple-element.318, f32[3,512]{1,0:T(4,128)S(1)} %get-tuple-element.319, pred[512,2560]{0,1:T(8,128)(4,1)S(1)} %compare_and_fusion.2), kind=kLoop, calls=%fused_computation.7.clone.1 | loop fusion | flops 15727104 | bytes 17051648 | tf_op jit(solution)/shard_map/while/body/eval_jaxpr/reduce_sum | solution.py:37
  339.4 9.7 %fusion.76 = f32[2560,1,1,128]{0,3,2,1:T(8,128)} fusion(bf16[512,1,3,128]{0,3,2,1:T(8,128)(2,1)S(1)} %constant_dynamic-slice_fusion.2, f32[3,512]{1,0:T(4,128)S(1)} %fusion.75, f32[3,512]{1,0:T(4,128)S(1)} %get-tuple-element.319, f32[2560,512,3]{1,0,2:T(8,128)} %get-tuple-element.318, pred[512,2560]{0,1:T(8,128)(4,1)S(1)} %compare_and_fusion.2), kind=kOutput, calls=%fused_computation.19.clone.1 | convolution fusion | flops 1026293760 | bytes 18755584 | tf_op jit(solution)/shard_map/while/body/eval_jaxpr/hgqk,qhgd->khd/dot_general | solution.py:51
  349.6 8.6 %multiply_reduce_fusion.2 = (f32[3,512]{1,0:T(4,128)S(1)}, bf16[128,3,512]{2,0,1:T(8,128)(2,1)S(1)}) fusion(f32[3,512,128]{1,2,0:T(8,128)S(1)} %copy.176, f32[3,512]{1,0:T(4,128)S(1)} %fusion.75, f32[3,512]{1,0:T(4,128)S(1)} %get-tuple-element.319, f32[2560,512,3]{1,0,2:T(8,128)} %get-tuple-element.318, ...), kind=kOutput, calls=%fused_computation.28.clone.1 | convolution fusion | flops 1027078656 | bytes 18892808 | tf_op jit(solution)/shard_map/while/body/eval_jaxpr/hgqk,khd->qhgd/dot_general | solution.py:39
  358.2 9.5 %fusion.77 = bf16[1,3,512,2560]{2,3,1,0:T(8,128)(2,1)S(1)} fusion(f32[3,512]{1,0:T(4,128)S(1)} %get-tuple-element.320, f32[3,512]{1,0:T(4,128)S(1)} %fusion.75, f32[3,512]{1,0:T(4,128)S(1)} %get-tuple-element.319, f32[2560,512,3]{1,0,2:T(8,128)} %get-tuple-element.318, pred[512,2560]{0,1:T(8,128)(4,1)S(1)} %compare_and_fusion.2, ...), kind=kOutput, calls=%fused_computation.3.clone.1 | convolution fusion | flops 1038090240 | bytes 25976840 | tf_op jit(solution)/shard_map/while/body/eval_jaxpr/qhgd,khd->hgqk/dot_general | solution.py:42
  367.8 3.7 fusion.78
  375.3 3.9 copy.171
  381.7 53.9 %all_to_all.115 = f32[16,256,256]{1,2,0:T(8,128)S(1)} all-to-all(f32[16,256,256]{1,2,0:T(8,128)S(1)} %copy.138), channel_id=1, replica_groups=mesh['dp'=8,'ctx'=16] {'ctx'}, dimensions={0} | all-to-all | bytes 8388608 | tf_op jit(solution)/shard_map/all_to_all | solution.py:129
  436.8 8.7 %copy.142 = bf16[1,256,12288]{1,2,0:T(8,128)(2,1)} copy(bf16[1,256,12288]{2,1,0:T(8,128)(2,1)} %param.10) | data formatting | bytes 12582912 | tf_op args[2]
  445.5 4.8 all-to-all-start.6
  453.7 102.6 %all-to-all-done.6 = bf16[256,16,768]{0,2,1:T(8,128)(2,1)} async-done(((bf16[256,16,768]{0,2,1:T(8,128)(2,1)}), bf16[256,16,768]{0,2,1:T(8,128)(2,1)}, u32[]{:S(2)}, u32[]{:S(2)}) %all-to-all-start.6) | async-done | bytes 6291488 | tf_op jit(solution)/shard_map/all_to_all | solution.py:110
  556.4 5.1 all-to-all-start.3
  569.2 8.7 %copy.143 = bf16[16,256,768]{2,1,0:T(8,128)(2,1)} copy(bf16[16,256,768]{1,2,0:T(8,128)(2,1)} %bitcast.55) | data formatting | bytes 12582912 | tf_op jit(solution)/shard_map/all_to_all | solution.py:110
  577.8 19.9 %all-to-all-done.3 = bf16[16,128,384]{1,2,0:T(8,128)(2,1)S(1)} async-done(((bf16[16,128,384]{1,2,0:T(8,128)(2,1)}), bf16[16,128,384]{1,2,0:T(8,128)(2,1)S(1)}, u32[]{:S(2)}, u32[]{:S(2)}) %all-to-all-start.3) | async-done | bytes 1572896 | tf_op jit(solution)/shard_map/all_to_all | solution.py:126
  597.8 3.7 all-to-all-start.4
  601.6 12.0 %fusion.50 = bf16[768,1024]{0,1:T(8,128)(2,1)} fusion(bf16[4096,1024]{0,1:T(8,128)(2,1)} %all-gather.2.cloned.1.call-done, bf16[4096,768]{1,0:T(8,128)(2,1)} %bitcast.232), kind=kOutput, calls=%fused_computation.55 | convolution fusion | flops 6443237376 | bytes 16252928 | tf_op jit(solution)/shard_map/kd,kc->dc/dot_general | solution.py:137
  615.2 6.8 all-to-all-done.4
  625.6 55.5 %all-reduce.2.cloned.1.call-done = bf16[768,1024]{0,1:T(8,128)(2,1)} async-done(((bf16[768,1024]{0,1:T(8,128)(2,1)}), bf16[768,1024]{0,1:T(8,128)(2,1)}) %all-reduce.2.cloned.1.call-update) | async-done | bytes 1572880 | tf_op jit(solution)/shard_map/psum | solution.py:143
  (150 shorter events, 79.7 us)
Async XLA Ops:
  7.2 9.9 %copy-start.6 = (bf16[1,128,6144]{2,1,0:T(8,128)(2,1)S(1)}, bf16[1,128,6144]{2,1,0:T(8,128)(2,1)}, u32[]{:S(2)}) copy-start(bf16[1,128,6144]{2,1,0:T(8,128)(2,1)} %param.11) | copy-start | bytes 4718596
  9.9 31.7 %all-to-all-start = ((bf16[128,16,384]{0,2,1:T(8,128)(2,1)}), bf16[128,16,384]{0,2,1:T(8,128)(2,1)S(1)}, u32[]{:S(2)}, u32[]{:S(2)}) async-start(bf16[128,16,384]{0,2,1:T(8,128)(2,1)} %bitcast.36), calls=%async_computation | async-start | bytes 3145728 | tf_op jit(solution)/shard_map/all_to_all | solution.py:118
  41.5 29.9 %copy-start.4 = (bf16[128,16,384]{0,2,1:T(8,128)(2,1)}, bf16[128,16,384]{0,2,1:T(8,128)(2,1)S(1)}, u32[]{:S(2)}) copy-start(bf16[128,16,384]{0,2,1:T(8,128)(2,1)S(1)} %all-to-all-done) | copy-start | bytes 4718596
  41.5 27.0 %all-to-all-start.2 = ((bf16[128,16,384]{0,2,1:T(8,128)(2,1)}), bf16[128,16,384]{0,2,1:T(8,128)(2,1)S(1)}, u32[]{:S(2)}, u32[]{:S(2)}) async-start(bf16[128,16,384]{0,2,1:T(8,128)(2,1)} %bitcast.237), calls=%async_computation.2 | async-start | bytes 3145728 | tf_op jit(solution)/shard_map/all_to_all | solution.py:119
  45.3 30.6 %copy-start.10 = (s32[1,256]{1,0:T(1,128)S(1)}, s32[1,256]{1,0:T(1,128)}, u32[]{:S(2)}) copy-start(s32[1,256]{1,0:T(1,128)} %param.12) | copy-start | bytes 3076
  68.5 2.9 copy-start.5
  71.5 34.5 %all-to-all-start.1 = ((bf16[256,16,256]{0,2,1:T(8,128)(2,1)}), bf16[256,16,256]{0,2,1:T(8,128)(2,1)S(1)}, u32[]{:S(2)}, u32[]{:S(2)}) async-start(bf16[256,16,256]{0,2,1:T(8,128)(2,1)} %bitcast.42), calls=%async_computation.1 | async-start | bytes 4194304 | tf_op jit(solution)/shard_map/all_to_all | solution.py:120
  75.2 526.4 %all-gather.2.cloned.1.call-start = ((), (), s32[]{:S(2)}) async-start(), calls=%async_computation.7 | async-start | bytes 8912896 | tf_op jit(solution)/shard_map/all_gather | solution.py:140
  164.3 8.6 %copy-start.3 = (bf16[4096,1,2,128]{0,3,2,1:T(8,128)(2,1)S(1)}, bf16[4096,1,2,128]{0,3,2,1:T(8,128)(2,1)}, u32[]{:S(2)}) copy-start(bf16[4096,1,2,128]{0,3,2,1:T(8,128)(2,1)} %get-tuple-element.365) | copy-start | bytes 6291460 | tf_op jit(solution)/shard_map/while
  182.4 3.8 copy-start
  182.5 3.8 copy-start.2
  186.2 1.4 copy-start.8
  186.7 2.1 copy-start.1
  188.9 1.1 copy-start.9
  226.1 8.6 %copy-start.3 = (bf16[4096,1,2,128]{0,3,2,1:T(8,128)(2,1)S(1)}, bf16[4096,1,2,128]{0,3,2,1:T(8,128)(2,1)}, u32[]{:S(2)}) copy-start(bf16[4096,1,2,128]{0,3,2,1:T(8,128)(2,1)} %get-tuple-element.365) | copy-start | bytes 6291460 | tf_op jit(solution)/shard_map/while
  244.2 3.8 copy-start
  244.2 3.8 copy-start.2
  248.0 1.4 copy-start.8
  248.5 2.1 copy-start.1
  250.6 1.1 copy-start.9
  287.8 8.6 %copy-start.3 = (bf16[4096,1,2,128]{0,3,2,1:T(8,128)(2,1)S(1)}, bf16[4096,1,2,128]{0,3,2,1:T(8,128)(2,1)}, u32[]{:S(2)}) copy-start(bf16[4096,1,2,128]{0,3,2,1:T(8,128)(2,1)} %get-tuple-element.365) | copy-start | bytes 6291460 | tf_op jit(solution)/shard_map/while
  306.0 3.8 copy-start
  306.0 3.8 copy-start.2
  309.8 1.4 copy-start.8
  310.3 2.1 copy-start.1
  312.4 1.1 copy-start.9
  349.6 8.6 %copy-start.3 = (bf16[4096,1,2,128]{0,3,2,1:T(8,128)(2,1)S(1)}, bf16[4096,1,2,128]{0,3,2,1:T(8,128)(2,1)}, u32[]{:S(2)}) copy-start(bf16[4096,1,2,128]{0,3,2,1:T(8,128)(2,1)} %get-tuple-element.365) | copy-start | bytes 6291460 | tf_op jit(solution)/shard_map/while
  367.8 3.8 copy-start
  367.8 3.8 copy-start.2
  371.6 1.4 copy-start.8
  372.1 2.1 copy-start.1
  374.2 1.1 copy-start.9
  445.5 4.8 copy-start.7
  445.5 110.9 %all-to-all-start.6 = ((bf16[256,16,768]{0,2,1:T(8,128)(2,1)}), bf16[256,16,768]{0,2,1:T(8,128)(2,1)}, u32[]{:S(2)}, u32[]{:S(2)}) async-start(bf16[256,16,768]{0,2,1:T(8,128)(2,1)} %bitcast.229), calls=%async_computation.6 | async-start | bytes 12582912 | tf_op jit(solution)/shard_map/all_to_all | solution.py:110
  556.4 41.4 %all-to-all-start.3 = ((bf16[16,128,384]{1,2,0:T(8,128)(2,1)}), bf16[16,128,384]{1,2,0:T(8,128)(2,1)S(1)}, u32[]{:S(2)}, u32[]{:S(2)}) async-start(bf16[16,128,384]{1,2,0:T(8,128)(2,1)} %copy.135), calls=%async_computation.3 | async-start | bytes 3145728 | tf_op jit(solution)/shard_map/all_to_all | solution.py:126
  597.8 24.3 %all-to-all-start.4 = ((bf16[16,128,384]{1,2,0:T(8,128)(2,1)}), bf16[16,128,384]{1,2,0:T(8,128)(2,1)S(1)}, u32[]{:S(2)}, u32[]{:S(2)}) async-start(bf16[16,128,384]{1,2,0:T(8,128)(2,1)} %copy.137), calls=%async_computation.4 | async-start | bytes 3145728 | tf_op jit(solution)/shard_map/all_to_all | solution.py:127
  601.5 79.6 %all-reduce.2.cloned.1.call-start = ((), (), s32[]{:S(2)}) async-start(), calls=%async_computation.8 | async-start | bytes 3145728 | tf_op jit(solution)/shard_map/psum | solution.py:143
Sparse Core Ops, SparseCore 0:
  436.9 162.5 all-gather.1
  613.7 67.3 all-reduce.1
where the time goes:
time: 697 us; the launch traced here: 690 us
  waiting for transfers between devices  244 us (35%)
  matrix products  182 us (26%)
  local copies, waits for them, and re-layouts  90.8 us (13%)
  other arithmetic  59.5 us (9%)
  blocking collectives  53.9 us (8%)
  starting transfers between devices  28.3 us (4%)
  loops' own time  16.4 us (2%)
  between operations  15.3 us (2%)
    all_to_all x1, waiting for transfers between devices, local(): lax.all_to_all(hidden_rows, 'ctx', split_axis=1, concat_axis=0, tiled=True)  103 us
    psum x1, waiting for transfers between devices, local(): lax.psum(local_weight.astype(jnp.bfloat16), 'dp').astype(jnp.float32)  55.5 us
    all_to_all x1, blocking collectives, local(): lax.all_to_all(grad_head, 'ctx', split_axis=0, concat_axis=1, tiled=True)  53.9 us
    dot_general x4, matrix products, band_block(): jnp.einsum('qhgd,khd->hgqk', query_block, key_block, preferred_element_ty...  39.3 us
    dot_general x4, matrix products, band_block(): jnp.einsum('hgqk,qhgd->khd', weights_low, upstream_gradient, preferred_el...  38.7 us
    dot_general x4, matrix products, band_block(): jnp.einsum('qhgd,khd->hgqk', upstream_gradient, value_block, preferred_el...  38.1 us
    reduce_sum x4, other arithmetic, band_block(): weights = raised / jnp.sum(raised, axis=-1, keepdims=True)  35.5 us
    dot_general x4, matrix products, band_block(): jnp.einsum('hgqk,khd->qhgd', weights_low, value_block, preferred_element_...  34.3 us
  transfers between devices with their start and end apart: 8, of which 7 were waited for; matrix products, arithmetic and copies ran while one was open for 9% of the time, Pallas kernels for 0%

commit v1 on v0

v1 whole, which is shorter than its diff:
```python
import functools

import jax
import jax.numpy as jnp
from jax import lax
from jax.experimental import pallas as pl
from jax.experimental.pallas import tpu as pltpu
from jax.sharding import PartitionSpec as P

HEAD_FEATURES = 128
KEY_VALUE_HEADS = 4
WINDOW = 2048
BLOCK_QUERIES = 256


def doc_index(positions, bounds):
    return jnp.sum(
        (bounds[None, :] <= positions[:, None]).astype(jnp.int32), axis=1, dtype=jnp.int32
    )


def attention_kernel(qdoc_ref, kdoc_ref, q_ref, go_ref, kv_ref, att_ref, dq_ref, dkv_ref, *, bq, span):
    qb = pl.program_id(0)
    h = pl.program_id(1)
    f32 = jnp.float32
    bf16 = jnp.bfloat16
    factor = HEAD_FEATURES ** (-0.5)

    @pl.when((qb == 0) & (h == 0))
    def _():
        dkv_ref[...] = jnp.zeros_like(dkv_ref)

    start = pl.multiple_of(qb * bq, bq)
    k = kv_ref[pl.ds(start, span), 0:HEAD_FEATURES]
    v = kv_ref[pl.ds(start, span), HEAD_FEATURES : 2 * HEAD_FEATURES]
    q = q_ref[...]
    go = go_ref[...]
    nt = (((1,), (1,)), ((), ()))
    tn = (((0,), (0,)), ((), ()))
    scores = lax.dot_general(q, k, nt, preferred_element_type=f32) * factor
    row = lax.broadcasted_iota(jnp.int32, (bq, span), 0)
    col = lax.broadcasted_iota(jnp.int32, (bq, span), 1)
    same_doc = qdoc_ref[...] == kdoc_ref[:, pl.ds(start, span)]
    allowed = (col > row) & (col <= row + WINDOW) & same_doc
    scores = jnp.where(allowed, scores, -1e30)
    maxima = jnp.max(scores, axis=1, keepdims=True)
    raised = jnp.exp(scores - maxima)
    weights = raised / jnp.sum(raised, axis=1, keepdims=True)
    weights_low = weights.astype(bf16)
    att = jnp.dot(weights_low, v, preferred_element_type=f32).astype(bf16)
    att_ref[...] = att
    grad_probs = lax.dot_general(go, v, nt, preferred_element_type=f32)
    deltas = jnp.sum(go.astype(f32) * att.astype(f32), axis=1, keepdims=True)
    grad_scores = (weights * (grad_probs - deltas) * factor).astype(bf16)
    dq_ref[...] = jnp.dot(grad_scores, k, preferred_element_type=f32).astype(bf16)
    dk = lax.dot_general(grad_scores, q, tn, preferred_element_type=f32)
    dv = lax.dot_general(weights_low, go, tn, preferred_element_type=f32)
    dkv_ref[pl.ds(start, span), 0:HEAD_FEATURES] += dk
    dkv_ref[pl.ds(start, span), HEAD_FEATURES : 2 * HEAD_FEATURES] += dv


def head_attention(head_queries, head_upstream, head_keys, q_doc, k_doc):
    rows = head_queries.shape[0]
    keys = head_keys.shape[0]
    heads_here = head_queries.shape[1] // HEAD_FEATURES
    bq = min(BLOCK_QUERIES, rows)
    span = bq + WINDOW
    grid = (rows // bq, heads_here)
    kernel = functools.partial(attention_kernel, bq=bq, span=span)
    flops = 12 * heads_here * rows * span * HEAD_FEATURES
    bytes_accessed = 2 * (4 * rows * heads_here * HEAD_FEATURES + keys * 2 * HEAD_FEATURES) + 4 * keys * 2 * HEAD_FEATURES
    return pl.pallas_call(
        kernel,
        grid=grid,
        in_specs=[
            pl.BlockSpec((bq, 1), lambda i, h: (i, 0)),
            pl.BlockSpec((1, keys), lambda i, h: (0, 0)),
            pl.BlockSpec((bq, HEAD_FEATURES), lambda i, h: (i, h)),
            pl.BlockSpec((bq, HEAD_FEATURES), lambda i, h: (i, h)),
            pl.BlockSpec((keys, 2 * HEAD_FEATURES), lambda i, h: (0, 0)),
        ],
        out_specs=[
            pl.BlockSpec((bq, HEAD_FEATURES), lambda i, h: (i, h)),
            pl.BlockSpec((bq, HEAD_FEATURES), lambda i, h: (i, h)),
            pl.BlockSpec((keys, 2 * HEAD_FEATURES), lambda i, h: (0, 0)),
        ],
        out_shape=[
            jax.ShapeDtypeStruct(head_queries.shape, jnp.bfloat16),
            jax.ShapeDtypeStruct(head_queries.shape, jnp.bfloat16),
            jax.ShapeDtypeStruct((keys, 2 * HEAD_FEATURES), jnp.float32),
        ],
        compiler_params=pltpu.CompilerParams(
            dimension_semantics=("arbitrary", "arbitrary"), vmem_limit_bytes=60 * 1024 * 1024
        ),
        cost_estimate=pl.CostEstimate(
            flops=flops, transcendentals=heads_here * rows * span, bytes_accessed=bytes_accessed
        ),
        name="band_attention",
    )(q_doc.reshape(rows, 1), k_doc.reshape(1, keys), head_queries, head_upstream, head_keys)


def local(queries, kv_proj, hidden, grad_out, doc_lengths, slab_offsets):
    query_matrix_rows = queries[0]
    upstream_gradient = grad_out[0]
    key_matrix_rows = kv_proj[0]
    hidden_rows = hidden[0]
    bounds = jnp.cumsum(doc_lengths[0], dtype=jnp.int32)
    offset = slab_offsets[0]
    key_value_width = 2 * KEY_VALUE_HEADS * HEAD_FEATURES
    hidden_cols = lax.all_to_all(hidden_rows, "ctx", split_axis=1, concat_axis=0, tiled=True)
    repeat_heads = lax.axis_size("ctx") // KEY_VALUE_HEADS
    key_total_count = key_matrix_rows.shape[0]
    copies = jnp.broadcast_to(
        key_matrix_rows.reshape(key_total_count, KEY_VALUE_HEADS, 1, 2 * HEAD_FEATURES),
        (key_total_count, KEY_VALUE_HEADS, repeat_heads, 2 * HEAD_FEATURES),
    ).reshape(key_total_count, KEY_VALUE_HEADS * repeat_heads * 2 * HEAD_FEATURES)
    head_queries, head_upstream, head_keys = (
        lax.all_to_all(query_matrix_rows, "ctx", split_axis=1, concat_axis=0, tiled=True),
        lax.all_to_all(upstream_gradient, "ctx", split_axis=1, concat_axis=0, tiled=True),
        lax.all_to_all(copies, "ctx", split_axis=1, concat_axis=0, tiled=True),
    )
    rows = head_queries.shape[0]
    keys = head_keys.shape[0]
    query_pos = offset + jnp.arange(rows, dtype=jnp.int32)
    key_pos = offset - WINDOW + jnp.arange(keys, dtype=jnp.int32)
    q_doc = doc_index(query_pos, bounds)
    k_doc = jnp.where(key_pos >= 0, doc_index(key_pos, bounds), -1)
    attended_heads, grad_query_heads, grad_head = head_attention(
        head_queries, head_upstream, head_keys, q_doc, k_doc
    )
    attended, grad_query = (
        lax.all_to_all(attended_heads, "ctx", split_axis=0, concat_axis=1, tiled=True),
        lax.all_to_all(grad_query_heads, "ctx", split_axis=0, concat_axis=1, tiled=True),
    )
    partial_sums = lax.all_to_all(
        grad_head.astype(jnp.bfloat16), "ctx", split_axis=0, concat_axis=1, tiled=True
    )
    grad_keys = jnp.sum(
        partial_sums.reshape(
            partial_sums.shape[0], KEY_VALUE_HEADS, repeat_heads, 2 * HEAD_FEATURES
        ).astype(jnp.float32),
        axis=2,
    ).reshape(partial_sums.shape[0], key_value_width)
    grad_low = grad_keys.astype(jnp.bfloat16)
    local_weight = jnp.einsum(
        "kd,kc->dc",
        hidden_cols,
        lax.all_gather(grad_low, "ctx", axis=0, tiled=True),
        preferred_element_type=jnp.float32,
    )
    grad_weight = lax.psum_scatter(
        local_weight.astype(jnp.bfloat16), "dp", scatter_dimension=1, tiled=True
    ).astype(jnp.float32)
    return (attended[None], grad_query[None], grad_low[None], grad_weight)


def solution(mesh):
    in_specs = (
        P("dp", "ctx", None),
        P("dp", "ctx", None),
        P("dp", "ctx", None),
        P("dp", "ctx", None),
        P("dp", None),
        P("dp"),
    )
    out_specs = (P("dp", "ctx", None), P("dp", "ctx", None), P("dp", "ctx", None), P("ctx", "dp"))
    return jax.shard_map(local, mesh=mesh, in_specs=in_specs, out_specs=out_specs, check_vma=False)
```

time: 697 us -> 420 us (0.60)
  matrix products: 182 us -> 11.8 us
  waiting for transfers between devices: 244 us -> 108 us
  blocking collectives: 53.9 us -> 146 us
  Pallas kernels: 0 us -> 73.4 us
  other arithmetic: 59.5 us -> 5.66 us
  local copies, waits for them, and re-layouts: 90.8 us -> 40.6 us
  loops' own time: 16.4 us -> 0 us
  starting transfers between devices: 28.3 us -> 19.3 us
    dot_general x24 -> x0, matrix products: 170 us -> none  [the longest x4 39.3 us: band_block(): jnp.einsum('qhgd,khd->hgqk', query_block, key_block, preferred_element_ty...]
    all_to_all x2 -> x0, waiting for transfers between devices: 109 us -> none  [the longest x1 103 us: local(): lax.all_to_all(hidden_rows, 'ctx', split_axis=1, concat_axis=0, tiled=True)]
    all_to_all x1 -> x3, blocking collectives: 53.9 us -> 146 us  [the longest x1 87.7 us: local(): lax.all_to_all(hidden_rows, 'ctx', split_axis=1, concat_axis=0, tiled=True)]
    pallas_call x0 -> x1, Pallas kernels: none -> 73.4 us  [head_attention(): pl.pallas_call(kernel, grid=grid, in_specs=[pl.BlockSpec((bq, 1), lambda...]
    psum x1 -> x0, waiting for transfers between devices: 55.5 us -> none  [local(): lax.psum(local_weight.astype(jnp.bfloat16), 'dp').astype(jnp.float32)]
    reduce_sum x4 -> x0, other arithmetic: 35.5 us -> none  [band_block(): weights = raised / jnp.sum(raised, axis=-1, keepdims=True)]
    all_gather x1, waiting for transfers between devices: 0.02 us -> 23.3 us  [local(): lax.all_gather(grad_low, 'ctx', axis=0, tiled=True)]
    another operation x1 -> x0, loops' own time: 16.4 us -> none  [band_attention(): lax.scan(step, initial, jnp.arange(query_total_count // block_rows, dtype...]
  transfers between devices with their start and end apart: 8 -> 6, of which waited for: 7 -> 5; matrix products, arithmetic and copies ran while one was open for 9% -> 8% of each run, Pallas kernels for 0% -> 0%
where the time goes in v1:
time: 420 us; the launch traced here: 419 us
  blocking collectives  146 us (35%)
  waiting for transfers between devices  108 us (26%)
  Pallas kernels  73.4 us (17%)
  local copies, waits for them, and re-layouts  40.6 us (10%)
  starting transfers between devices  19.3 us (5%)
  between operations  14.8 us (4%)
  matrix products  11.8 us (3%)
  other arithmetic  5.66 us (1%)
    all_to_all x1, blocking collectives, local(): lax.all_to_all(hidden_rows, 'ctx', split_axis=1, concat_axis=0, tiled=True)  87.7 us
    pallas_call x1, Pallas kernels, head_attention(): pl.pallas_call(kernel, grid=grid, in_specs=[pl.BlockSpec((bq, 1), lambda...  73.4 us
    all_to_all x1, blocking collectives, local(): lax.all_to_all(grad_head.astype(jnp.bfloat16), 'ctx', split_axis=0, conca...  31.4 us
    all_to_all x1, blocking collectives, local(): lax.all_to_all(grad_query_heads, 'ctx', split_axis=0, concat_axis=1, tile...  26.9 us
    all_to_all x1, waiting for transfers between devices, local(): lax.all_to_all(copies, 'ctx', split_axis=1, concat_axis=0, tiled=True)  23.7 us
    all_gather x1, waiting for transfers between devices, local(): lax.all_gather(grad_low, 'ctx', axis=0, tiled=True)  23.3 us
    all_to_all x1, waiting for transfers between devices, local(): lax.all_to_all(query_matrix_rows, 'ctx', split_axis=1, concat_axis=0, til...  22.7 us
    all_to_all x1, waiting for transfers between devices, local(): lax.all_to_all(upstream_gradient, 'ctx', split_axis=1, concat_axis=0, til...  21.7 us
  transfers between devices with their start and end apart: 6, of which 5 were waited for; matrix products, arithmetic and copies ran while one was open for 8% of the time, Pallas kernels for 0%

profile of v1, /device:TPU:0, one launch (start us, length us, event | category | flops | bytes accessed | tf_op | source)
XLA Modules:
  0.0 419.1 jit_solution(11063051099842079050)
XLA Ops:
  7.2 1.7 copy.65
  8.9 1.5 copy.53
  10.4 7.3 %all-to-all-start = ((bf16[128,16,384]{2,0,1:T(8,128)(2,1)}), bf16[128,16,384]{2,0,1:T(8,128)(2,1)S(1)}, u32[]{:S(2)}, u32[]{:S(2)}) async-start(bf16[128,16,384]{2,0,1:T(8,128)(2,1)} %copy.53), calls=%async_computation | async-start | bytes 3145728 | tf_op jit(solution)/shard_map/all_to_all | solution.py:118
  17.7 0.0 copy-done.2
  17.7 0.3 copy.66
  18.0 1.5 copy.54
  19.5 22.7 %all-to-all-done = bf16[128,16,384]{2,0,1:T(8,128)(2,1)S(1)} async-done(((bf16[128,16,384]{2,0,1:T(8,128)(2,1)}), bf16[128,16,384]{2,0,1:T(8,128)(2,1)S(1)}, u32[]{:S(2)}, u32[]{:S(2)}) %all-to-all-start) | async-done | bytes 1572896 | tf_op jit(solution)/shard_map/all_to_all | solution.py:118
  42.2 4.4 %all-to-all-start.1 = ((bf16[128,16,384]{2,0,1:T(8,128)(2,1)}), bf16[128,16,384]{2,0,1:T(8,128)(2,1)}, u32[]{:S(2)}, u32[]{:S(2)}) async-start(bf16[128,16,384]{2,0,1:T(8,128)(2,1)} %copy.54), calls=%async_computation.1 | async-start | bytes 3145728 | tf_op jit(solution)/shard_map/all_to_all | solution.py:119
  46.6 0.4 broadcast_in_dim.23
  47.0 0.1 copy.55
  47.1 21.7 %all-to-all-done.1 = bf16[128,16,384]{2,0,1:T(8,128)(2,1)} async-done(((bf16[128,16,384]{2,0,1:T(8,128)(2,1)}), bf16[128,16,384]{2,0,1:T(8,128)(2,1)}, u32[]{:S(2)}, u32[]{:S(2)}) %all-to-all-start.1) | async-done | bytes 1572896 | tf_op jit(solution)/shard_map/all_to_all | solution.py:119
  68.8 1.5 broadcast_in_dim.24
  70.4 3.8 all-to-all-start.2
  74.2 0.0 all-gather.2.cloned.1.call-start
  74.9 0.3 reduce-window.9
  75.2 0.1 slice.7
  75.3 0.1 slice_reduce_fusion
  75.5 0.1 add_bitcast_fusion
  75.5 0.6 convert_reduce_fusion.1
  76.2 1.5 copy.56.qdoc_ref
  77.6 1.3 convert_reduce_fusion
  78.9 0.6 compare_select_fusion.kdoc_ref
  79.5 23.7 %all-to-all-done.2 = bf16[256,16,256]{2,0,1:T(8,128)(2,1)S(1)} async-done(((bf16[256,16,256]{2,0,1:T(8,128)(2,1)}), bf16[256,16,256]{2,0,1:T(8,128)(2,1)S(1)}, u32[]{:S(2)}, u32[]{:S(2)}) %all-to-all-start.2) | async-done | bytes 2097184 | tf_op jit(solution)/shard_map/all_to_all | solution.py:120
  103.3 1.3 copy-done.1
  104.6 73.4 %band_attention.1 = (bf16[2048,384]{1,0:T(8,128)(2,1)}, bf16[2048,384]{1,0:T(8,128)(2,1)}, f32[4096,256]{1,0:T(8,128)}) custom-call(s32[2048,1]{1,0:T(8,128)} %copy.56.qdoc_ref, s32[1,4096]{1,0:T(1,128)} %compare_select_fusion.kdoc_ref, bf16[2048,384]{1,0:T(8,128)(2,1)} %bitcast.55, bf16[2048,384]{1,0:T(8,128)(2,1)} %bitcast.8.go_ref, bf16[4096,256]{1,0:T(8,128)(2,1)} %bitcast.52), custom_call_target="tpu_custom_call" | custom-call | flops 21743271936 | bytes 12582912 | tf_op jit(solution)/shard_map/band_attention/pallas_call | solution.py:72
  178.0 2.4 convert_element_type.45
  180.4 31.4 %all_to_all.121 = bf16[16,256,256]{2,1,0:T(8,128)(2,1)S(1)} all-to-all(bf16[16,256,256]{2,1,0:T(8,128)(2,1)S(1)} %bitcast.44), channel_id=1, replica_groups=mesh['dp'=8,'ctx'=16] {'ctx'}, dimensions={0} | all-to-all | bytes 4194304 | tf_op jit(solution)/shard_map/all_to_all | solution.py:135
  211.7 0.3 bitcast_reduce_fusion
  212.1 1.0 copy.59
  213.1 0.0 all-gather.2.cloned.1.call-update
  213.1 0.0 reduce-scatter.2.cloned.1.call-start
  213.1 8.6 %copy.61 = bf16[1,256,12288]{1,2,0:T(8,128)(2,1)} copy(bf16[1,256,12288]{2,1,0:T(8,128)(2,1)} %param.8) | data formatting | bytes 12582912 | tf_op args[2]
  221.7 87.7 %all_to_all.122 = bf16[256,16,768]{0,2,1:T(8,128)(2,1)} all-to-all(bf16[256,16,768]{0,2,1:T(8,128)(2,1)} %bitcast.43), channel_id=1, replica_groups=mesh['dp'=8,'ctx'=16] {'ctx'}, dimensions={1} | all-to-all | bytes 12582912 | tf_op jit(solution)/shard_map/all_to_all | solution.py:110
  309.4 8.6 %copy.62 = bf16[16,256,768]{2,1,0:T(8,128)(2,1)} copy(bf16[16,256,768]{1,2,0:T(8,128)(2,1)} %bitcast.42) | data formatting | bytes 12582912 | tf_op jit(solution)/shard_map/all_to_all | solution.py:110
  318.0 23.3 %all-gather.2.cloned.1.call-done = bf16[4096,1024]{0,1:T(8,128)(2,1)} async-done(((bf16[256,1024]{0,1:T(8,128)(2,1)}), bf16[4096,1024]{0,1:T(8,128)(2,1)}) %all-gather.2.cloned.1.call-update) | async-done | bytes 8388624 | tf_op jit(solution)/shard_map/all_gather | solution.py:148
  341.3 11.8 %fusion = bf16[768,1024]{0,1:T(8,128)(2,1)} fusion(bf16[4096,1024]{0,1:T(8,128)(2,1)} %all-gather.2.cloned.1.call-done, bf16[4096,768]{1,0:T(8,128)(2,1)} %bitcast.45), kind=kOutput, calls=%fused_computation.4 | convolution fusion | flops 6443237376 | bytes 16252928 | tf_op jit(solution)/shard_map/kd,kc->dc/dot_general | solution.py:145
  353.1 0.0 reduce-scatter.2.cloned.1.call-update
  353.1 1.4 copy-done.4
  354.5 26.9 %all_to_all.123 = bf16[16,128,384]{2,1,0:T(8,128)(2,1)S(1)} all-to-all(bf16[16,128,384]{2,1,0:T(8,128)(2,1)S(1)} %bitcast.57), channel_id=1, replica_groups=mesh['dp'=8,'ctx'=16] {'ctx'}, dimensions={0} | all-to-all | bytes 3145728 | tf_op jit(solution)/shard_map/all_to_all | solution.py:133
  381.4 3.7 all-to-all-start.3
  385.1 2.1 copy.58
  387.2 3.6 broadcast_in_dim.26
  390.8 16.1 %all-to-all-done.3 = bf16[16,128,384]{2,1,0:T(8,128)(2,1)S(1)} async-done(((bf16[16,128,384]{2,1,0:T(8,128)(2,1)}), bf16[16,128,384]{2,1,0:T(8,128)(2,1)S(1)}, u32[]{:S(2)}, u32[]{:S(2)}) %all-to-all-start.3) | async-done | bytes 1572896 | tf_op jit(solution)/shard_map/all_to_all | solution.py:132
  406.9 0.9 copy.57
  407.8 0.0 copy-start
  407.8 1.6 broadcast_in_dim.25
  409.4 1.0 copy.63
  410.4 1.8 copy.64
  (14 shorter events, 0.1 us)
Async XLA Ops:
  10.4 7.3 %copy-start.2 = (bf16[1,128,6144]{2,1,0:T(8,128)(2,1)S(1)}, bf16[1,128,6144]{2,1,0:T(8,128)(2,1)}, u32[]{:S(2)}) copy-start(bf16[1,128,6144]{2,1,0:T(8,128)(2,1)} %param.9) | copy-start | bytes 4718596
  10.4 31.8 %all-to-all-start = ((bf16[128,16,384]{2,0,1:T(8,128)(2,1)}), bf16[128,16,384]{2,0,1:T(8,128)(2,1)S(1)}, u32[]{:S(2)}, u32[]{:S(2)}) async-start(bf16[128,16,384]{2,0,1:T(8,128)(2,1)} %copy.53), calls=%async_computation | async-start | bytes 3145728 | tf_op jit(solution)/shard_map/all_to_all | solution.py:118
  19.5 27.1 %copy-start.5 = (bf16[1,256,1024]{2,1,0:T(8,128)(2,1)S(1)}, bf16[1,256,1024]{2,1,0:T(8,128)(2,1)}, u32[]{:S(2)}) copy-start(bf16[1,256,1024]{2,1,0:T(8,128)(2,1)} %param.7) | copy-start | bytes 1572868
  42.2 4.8 %copy-start.3 = (bf16[128,16,384]{2,0,1:T(8,128)(2,1)}, bf16[128,16,384]{2,0,1:T(8,128)(2,1)S(1)}, u32[]{:S(2)}) copy-start(bf16[128,16,384]{2,0,1:T(8,128)(2,1)S(1)} %all-to-all-done) | copy-start | bytes 4718596
  42.2 26.6 %all-to-all-start.1 = ((bf16[128,16,384]{2,0,1:T(8,128)(2,1)}), bf16[128,16,384]{2,0,1:T(8,128)(2,1)}, u32[]{:S(2)}, u32[]{:S(2)}) async-start(bf16[128,16,384]{2,0,1:T(8,128)(2,1)} %copy.54), calls=%async_computation.1 | async-start | bytes 3145728 | tf_op jit(solution)/shard_map/all_to_all | solution.py:119
  70.4 4.6 %copy-start.6 = (s32[1,256]{1,0:T(1,128)S(1)}, s32[1,256]{1,0:T(1,128)}, u32[]{:S(2)}) copy-start(s32[1,256]{1,0:T(1,128)} %param.10) | copy-start | bytes 3076
  70.4 32.9 %all-to-all-start.2 = ((bf16[256,16,256]{2,0,1:T(8,128)(2,1)}), bf16[256,16,256]{2,0,1:T(8,128)(2,1)S(1)}, u32[]{:S(2)}, u32[]{:S(2)}) async-start(bf16[256,16,256]{2,0,1:T(8,128)(2,1)} %bitcast.9), calls=%async_computation.2 | async-start | bytes 4194304 | tf_op jit(solution)/shard_map/all_to_all | solution.py:120
  74.2 267.1 %all-gather.2.cloned.1.call-start = ((), (), s32[]{:S(2)}) async-start(), calls=%async_computation.8 | async-start | bytes 8912896 | tf_op jit(solution)/shard_map/all_gather | solution.py:148
  103.3 1.3 copy-start.1
  213.1 197.4 %reduce-scatter.2.cloned.1.call-start = ((), (), s32[]{:S(2)}) async-start(), calls=%async_computation.9 | async-start | bytes 1769472 | tf_op jit(solution)/shard_map/reduce_scatter | solution.py:151
  353.1 1.4 copy-start.4
  381.4 25.5 %all-to-all-start.3 = ((bf16[16,128,384]{2,1,0:T(8,128)(2,1)}), bf16[16,128,384]{2,1,0:T(8,128)(2,1)S(1)}, u32[]{:S(2)}, u32[]{:S(2)}) async-start(bf16[16,128,384]{2,1,0:T(8,128)(2,1)} %bitcast.56), calls=%async_computation.3 | async-start | bytes 3145728 | tf_op jit(solution)/shard_map/all_to_all | solution.py:132
  407.8 1.6 copy-start
Sparse Core Ops, SparseCore 0:
  213.2 128.0 all-gather.1
  353.3 34.0 reduce-scatter.1

commit v2 on v1

--- a/solution.py
+++ b/solution.py
@@ -6,6 +6,7 @@
 from jax.experimental import pallas as pl
 from jax.experimental.pallas import tpu as pltpu
 from jax.sharding import PartitionSpec as P
+
 
 HEAD_FEATURES = 128
 KEY_VALUE_HEADS = 4
@@ -99,7 +100,31 @@
     )(q_doc.reshape(rows, 1), k_doc.reshape(1, keys), head_queries, head_upstream, head_keys)
 
 
-def local(queries, kv_proj, hidden, grad_out, doc_lengths, slab_offsets):
+def weight_gradient(hidden_rows, grad_low):
+    dp = lax.axis_size("dp")
+    ctx = lax.axis_size("ctx")
+    rows, features = hidden_rows.shape
+    piece = features // (ctx * dp)
+    width = features // dp
+    me = lax.axis_index("dp")
+    interleaved = hidden_rows.reshape(rows, ctx, dp, piece).transpose(2, 0, 1, 3).reshape(dp, rows, width)
+    received = [lax.dynamic_index_in_dim(interleaved, me, 0, keepdims=False)]
+    for shift in range(1, dp):
+        outgoing = lax.dynamic_index_in_dim(interleaved, (me + shift) % dp, 0, keepdims=False)
+        pairs = [(i, (i + shift) % dp) for i in range(dp)]
+        received.append(lax.ppermute(outgoing, "dp", pairs))
+    hidden_dp = jnp.concatenate(received, axis=0)
+    grad_all = lax.all_gather(grad_low, "dp", axis=0, tiled=False)
+    grad_dp = jnp.concatenate(
+        [lax.dynamic_index_in_dim(grad_all, (me - shift) % dp, 0, keepdims=False) for shift in range(dp)],
+        axis=0,
+    )
+    partial = jnp.einsum("kd,kc->dc", hidden_dp, grad_dp, preferred_element_type=jnp.float32)
+    reduced = lax.psum_scatter(partial, "ctx", scatter_dimension=0, tiled=True)
+    return lax.all_to_all(reduced, "dp", split_axis=1, concat_axis=0, tiled=True)
+
+
+def local_body(queries, kv_proj, hidden, grad_out, doc_lengths, slab_offsets):
     query_matrix_rows = queries[0]
     upstream_gradient = grad_out[0]
     key_matrix_rows = kv_proj[0]
@@ -107,7 +132,6 @@
     bounds = jnp.cumsum(doc_lengths[0], dtype=jnp.int32)
     offset = slab_offsets[0]
     key_value_width = 2 * KEY_VALUE_HEADS * HEAD_FEATURES
-    hidden_cols = lax.all_to_all(hidden_rows, "ctx", split_axis=1, concat_axis=0, tiled=True)
     repeat_heads = lax.axis_size("ctx") // KEY_VALUE_HEADS
     key_total_count = key_matrix_rows.shape[0]
     copies = jnp.broadcast_to(
@@ -125,9 +149,7 @@
     key_pos = offset - WINDOW + jnp.arange(keys, dtype=jnp.int32)
     q_doc = doc_index(query_pos, bounds)
     k_doc = jnp.where(key_pos >= 0, doc_index(key_pos, bounds), -1)
-    attended_heads, grad_query_heads, grad_head = head_attention(
-        head_queries, head_upstream, head_keys, q_doc, k_doc
-    )
+    attended_heads, grad_query_heads, grad_head = head_attention(head_queries, head_upstream, head_keys, q_doc, k_doc)
     attended, grad_query = (
         lax.all_to_all(attended_heads, "ctx", split_axis=0, concat_axis=1, tiled=True),
         lax.all_to_all(grad_query_heads, "ctx", split_axis=0, concat_axis=1, tiled=True),
@@ -142,15 +164,7 @@
         axis=2,
     ).reshape(partial_sums.shape[0], key_value_width)
     grad_low = grad_keys.astype(jnp.bfloat16)
-    local_weight = jnp.einsum(
-        "kd,kc->dc",
-        hidden_cols,
-        lax.all_gather(grad_low, "ctx", axis=0, tiled=True),
-        preferred_element_type=jnp.float32,
-    )
-    grad_weight = lax.psum_scatter(
-        local_weight.astype(jnp.bfloat16), "dp", scatter_dimension=1, tiled=True
-    ).astype(jnp.float32)
+    grad_weight = weight_gradient(hidden_rows, grad_low)
     return (attended[None], grad_query[None], grad_low[None], grad_weight)
 
 
@@ -164,4 +178,4 @@
         P("dp"),
     )
     out_specs = (P("dp", "ctx", None), P("dp", "ctx", None), P("dp", "ctx", None), P("ctx", "dp"))
-    return jax.shard_map(local, mesh=mesh, in_specs=in_specs, out_specs=out_specs, check_vma=False)
+    return jax.shard_map(local_body, mesh=mesh, in_specs=in_specs, out_specs=out_specs, check_vma=False)

time: 420 us -> 460 us (1.095)
  blocking collectives: 146 us -> 63.4 us
  waiting for transfers between devices: 108 us -> 181 us
  starting transfers between devices: 19.3 us -> 47.2 us
  local copies, waits for them, and re-layouts: 40.6 us -> 62.1 us
    all_to_all x3 -> x2, blocking collectives: 146 us -> 63.4 us  [the longest x1 32.1 us: local_body(): lax.all_to_all(attended_heads, 'ctx', split_axis=0, concat_axis=1, tiled=...]
    reduce_scatter x1, waiting for transfers between devices: 0.01 us -> 71.8 us  [weight_gradient(): reduced = lax.psum_scatter(partial, 'ctx', scatter_dimension=0, tiled=True)]
    ppermute x0 -> x7, waiting for transfers between devices: none -> 39.9 us  [weight_gradient(): received.append(lax.ppermute(outgoing, 'dp', pairs))]
    ppermute x0 -> x7, starting transfers between devices: none -> 23.7 us  [weight_gradient(): received.append(lax.ppermute(outgoing, 'dp', pairs))]
    all_gather x1, waiting for transfers between devices: 23.3 us -> 0.01 us  [weight_gradient(): grad_all = lax.all_gather(grad_low, 'dp', axis=0, tiled=False)]
    unnamed x19 -> x33, local copies, waits for them, and re-layouts: 16.1 us -> 33.8 us
    all_to_all x4 -> x5, waiting for transfers between devices: 84.2 us -> 68.9 us  [the longest x1 23.7 us: local_body(): lax.all_to_all(copies, 'ctx', split_axis=1, concat_axis=0, tiled=True)]
    all_to_all x5, local copies, waits for them, and re-layouts: 14.6 us -> 7.76 us  [the longest x1 2.06 us: local_body(): lax.all_to_all(attended_heads, 'ctx', split_axis=0, concat_axis=1, tiled=...]
  transfers between devices with their start and end apart: 6 -> 14, of which waited for: 5 -> 8; matrix products, arithmetic and copies ran while one was open for 8% -> 11% of each run, Pallas kernels for 0% -> 0%
where the time goes in v2:
time: 460 us; the launch traced here: 458 us
  waiting for transfers between devices  181 us (39%)
  Pallas kernels  73.4 us (16%)
  blocking collectives  63.4 us (14%)
  local copies, waits for them, and re-layouts  62.1 us (14%)
  starting transfers between devices  47.2 us (10%)
  between operations  15 us (3%)
  matrix products  10.4 us (2%)
  other arithmetic  5.66 us (1%)
    pallas_call x1, Pallas kernels, head_attention(): pl.pallas_call(kernel, grid=grid, in_specs=[pl.BlockSpec((bq, 1), lambda...  73.4 us
    reduce_scatter x1, waiting for transfers between devices, weight_gradient(): reduced = lax.psum_scatter(partial, 'ctx', scatter_dimension=0, tiled=True)  71.8 us
    ppermute x7, waiting for transfers between devices, weight_gradient(): received.append(lax.ppermute(outgoing, 'dp', pairs))  39.9 us
    unnamed x33, local copies, waits for them, and re-layouts  33.8 us
    all_to_all x1, blocking collectives, local_body(): lax.all_to_all(attended_heads, 'ctx', split_axis=0, concat_axis=1, tiled=...  32.1 us
    all_to_all x1, blocking collectives, local_body(): lax.all_to_all(grad_head.astype(jnp.bfloat16), 'ctx', split_axis=0, conca...  31.4 us
    all_to_all x1, waiting for transfers between devices, local_body(): lax.all_to_all(copies, 'ctx', split_axis=1, concat_axis=0, tiled=True)  23.7 us
    ppermute x7, starting transfers between devices, weight_gradient(): received.append(lax.ppermute(outgoing, 'dp', pairs))  23.7 us
  transfers between devices with their start and end apart: 14, of which 8 were waited for; matrix products, arithmetic and copies ran while one was open for 11% of the time, Pallas kernels for 0%

profile of v2, /device:TPU:0, one launch (start us, length us, event | category | flops | bytes accessed | tf_op | source)
XLA Modules:
  0.0 457.7 jit_solution(16705087558369228663)
XLA Ops:
  7.2 1.8 copy.59
  9.0 1.5 copy.46
  10.5 7.1 %all-to-all-start = ((bf16[128,16,384]{2,0,1:T(8,128)(2,1)}), bf16[128,16,384]{2,0,1:T(8,128)(2,1)S(1)}, u32[]{:S(2)}, u32[]{:S(2)}) async-start(bf16[128,16,384]{2,0,1:T(8,128)(2,1)} %copy.46), calls=%async_computation | async-start | bytes 3145728 | tf_op jit(solution)/shard_map/all_to_all | solution.py:142
  18.0 1.5 copy.47
  19.5 22.7 %all-to-all-done = bf16[128,16,384]{2,0,1:T(8,128)(2,1)S(1)} async-done(((bf16[128,16,384]{2,0,1:T(8,128)(2,1)}), bf16[128,16,384]{2,0,1:T(8,128)(2,1)S(1)}, u32[]{:S(2)}, u32[]{:S(2)}) %all-to-all-start) | async-done | bytes 1572896 | tf_op jit(solution)/shard_map/all_to_all | solution.py:142
  42.2 4.4 all-to-all-start.1
  47.1 21.7 %all-to-all-done.1 = bf16[128,16,384]{2,0,1:T(8,128)(2,1)} async-done(((bf16[128,16,384]{2,0,1:T(8,128)(2,1)}), bf16[128,16,384]{2,0,1:T(8,128)(2,1)}, u32[]{:S(2)}, u32[]{:S(2)}) %all-to-all-start.1) | async-done | bytes 1572896 | tf_op jit(solution)/shard_map/all_to_all | solution.py:143
  68.8 1.5 broadcast_in_dim.24
  70.3 3.7 all-to-all-start.2
  76.0 1.4 copy.49.qdoc_ref
  77.5 1.3 convert_reduce_fusion
  79.4 23.7 %all-to-all-done.2 = bf16[256,16,256]{2,0,1:T(8,128)(2,1)S(1)} async-done(((bf16[256,16,256]{2,0,1:T(8,128)(2,1)}), bf16[256,16,256]{2,0,1:T(8,128)(2,1)S(1)}, u32[]{:S(2)}, u32[]{:S(2)}) %all-to-all-start.2) | async-done | bytes 2097184 | tf_op jit(solution)/shard_map/all_to_all | solution.py:144
  103.1 1.3 copy-done.1
  104.4 73.4 %band_attention.1 = (bf16[2048,384]{1,0:T(8,128)(2,1)}, bf16[2048,384]{1,0:T(8,128)(2,1)}, f32[4096,256]{1,0:T(8,128)}) custom-call(s32[2048,1]{1,0:T(8,128)} %copy.49.qdoc_ref, s32[1,4096]{1,0:T(1,128)} %compare_select_fusion.kdoc_ref, bf16[2048,384]{1,0:T(8,128)(2,1)} %bitcast.94, bf16[2048,384]{1,0:T(8,128)(2,1)} %bitcast.8.go_ref, bf16[4096,256]{1,0:T(8,128)(2,1)} %bitcast.88), custom_call_target="tpu_custom_call" | custom-call | flops 21743271936 | bytes 12582912 | tf_op jit(solution)/shard_map/band_attention/pallas_call | solution.py:73
  177.9 2.4 convert_element_type.33
  180.3 31.4 %all_to_all.121 = bf16[16,256,256]{2,1,0:T(8,128)(2,1)S(1)} all-to-all(bf16[16,256,256]{2,1,0:T(8,128)(2,1)S(1)} %bitcast.83), channel_id=1, replica_groups=mesh['dp'=8,'ctx'=16] {'ctx'}, dimensions={0} | all-to-all | bytes 4194304 | tf_op jit(solution)/shard_map/all_to_all | solution.py:157
  213.3 8.7 %copy.53 = bf16[1,256,12288]{1,2,0:T(8,128)(2,1)} copy(bf16[1,256,12288]{2,1,0:T(8,128)(2,1)} %param.8) | data formatting | bytes 12582912 | tf_op args[2]
  222.0 6.3 %copy.54 = bf16[8,256,16,96]{1,3,2,0:T(8,128)(2,1)} copy(bf16[8,256,16,96]{1,3,0,2:T(8,128)(2,1)} %bitcast.82) | data formatting | bytes 12582912 | tf_op jit(solution)/shard_map/transpose | solution.py:110
  228.3 4.2 dynamic-slice_bitcast_fusion
  232.5 1.8 collective-permute-start.1
  234.3 2.9 collective-permute-start.2
  237.2 1.2 collective-permute-start.3
  238.4 2.3 collective-permute-start.4
  240.7 2.1 bitcast_dynamic-update-slice_fusion
  242.9 16.2 %collective-permute-done = bf16[256,1536]{0,1:T(8,128)(2,1)} collective-permute-done((bf16[256,1536]{0,1:T(8,128)(2,1)}, bf16[256,1536]{0,1:T(8,128)(2,1)}, u32[]{:S(2)}, u32[]{:S(2)}) %collective-permute-start) | collective-permute-done | bytes 786464 | tf_op jit(solution)/shard_map/ppermute | solution.py:115
  260.0 2.1 constant_dynamic-update-slice_fusion.6
  262.2 14.4 %collective-permute-start.6 = (bf16[256,1536]{0,1:T(8,128)(2,1)S(1)}, bf16[256,1536]{0,1:T(8,128)(2,1)S(1)}, u32[]{:S(2)}, u32[]{:S(2)}) collective-permute-start(bf16[256,1536]{0,1:T(8,128)(2,1)S(1)} %get-tuple-element.18), channel_id=1, source_target_pairs={{0,112},{16,0},{32,16},{48,32},{64,48},{80,64},{96,80},{112,96},{1... | collective-permute-start | bytes 2359304 | tf_op jit(solution)/shard_map/ppermute | solution.py:115
  276.6 2.1 constant_dynamic-update-slice_fusion.5
  278.7 14.5 %collective-permute-done.2 = bf16[256,1536]{0,1:T(8,128)(2,1)} collective-permute-done((bf16[256,1536]{0,1:T(8,128)(2,1)}, bf16[256,1536]{0,1:T(8,128)(2,1)}, u32[]{:S(2)}, u32[]{:S(2)}) %collective-permute-start.2) | collective-permute-done | bytes 786464 | tf_op jit(solution)/shard_map/ppermute | solution.py:115
  293.2 2.1 constant_dynamic-update-slice_fusion.4
  295.3 2.1 constant_dynamic-update-slice_fusion.3
  297.4 9.2 %collective-permute-done.4 = bf16[256,1536]{0,1:T(8,128)(2,1)} collective-permute-done((bf16[256,1536]{0,1:T(8,128)(2,1)S(1)}, bf16[256,1536]{0,1:T(8,128)(2,1)}, u32[]{:S(2)}, u32[]{:S(2)}) %collective-permute-start.4) | collective-permute-done | bytes 786464 | tf_op jit(solution)/shard_map/ppermute | solution.py:115
  306.7 2.1 constant_dynamic-update-slice_fusion.2
  308.8 1.0 constant_dynamic-update-slice_fusion.1
  310.8 1.2 bitcast_dynamic-update-slice_fusion.8
  312.0 1.3 bitcast_dynamic-update-slice_fusion.7
  313.3 1.1 bitcast_dynamic-update-slice_fusion.6
  314.3 1.1 bitcast_dynamic-update-slice_fusion.5
  315.6 10.4 %fusion = f32[1536,1024]{1,0:T(8,128)} fusion(bf16[2048,1536]{0,1:T(8,128)(2,1)} %constant_dynamic-update-slice_fusion, bf16[2048,1024]{1,0:T(8,128)(2,1)S(1)} %bitcast_dynamic-update-slice_fusion.1), kind=kOutput, calls=%fused_computation.32 | convolution fusion | flops 6442450944 | bytes 16777216 | tf_op jit(solution)/shard_map/kd,kc->dc/dot_general | solution.py:122
  326.1 1.4 copy-done.3
  327.5 32.1 %all_to_all.122 = bf16[16,128,384]{2,1,0:T(8,128)(2,1)S(1)} all-to-all(bf16[16,128,384]{2,1,0:T(8,128)(2,1)S(1)} %bitcast.93), channel_id=1, replica_groups=mesh['dp'=8,'ctx'=16] {'ctx'}, dimensions={0} | all-to-all | bytes 3145728 | tf_op jit(solution)/shard_map/all_to_all | solution.py:154
  359.5 3.7 all-to-all-start.4
  363.3 71.8 %reduce-scatter.2.cloned.1.call-done = f32[96,1024]{1,0:T(8,128)} async-done(((f32[1536,1024]{1,0:T(8,128)}), f32[96,1024]{1,0:T(8,128)}) %reduce-scatter.2.cloned.1.call-update) | async-done | bytes 393232 | tf_op jit(solution)/shard_map/reduce_scatter | solution.py:123
  435.0 1.8 copy_bitcast_fusion
  436.8 4.4 all-to-all-start.6
  441.2 2.1 copy.50
  443.3 3.6 broadcast_in_dim.25
  447.8 1.6 broadcast_in_dim.26
  (47 shorter events, 8.8 us)
Async XLA Ops:
  7.2 10.5 %copy-start.2 = (bf16[1,128,6144]{2,1,0:T(8,128)(2,1)S(1)}, bf16[1,128,6144]{2,1,0:T(8,128)(2,1)}, u32[]{:S(2)}) copy-start(bf16[1,128,6144]{2,1,0:T(8,128)(2,1)} %param.9) | copy-start | bytes 4718596
  10.5 31.7 %all-to-all-start = ((bf16[128,16,384]{2,0,1:T(8,128)(2,1)}), bf16[128,16,384]{2,0,1:T(8,128)(2,1)S(1)}, u32[]{:S(2)}, u32[]{:S(2)}) async-start(bf16[128,16,384]{2,0,1:T(8,128)(2,1)} %copy.46), calls=%async_computation | async-start | bytes 3145728 | tf_op jit(solution)/shard_map/all_to_all | solution.py:142
  18.0 28.6 %copy-start.5 = (bf16[1,256,1024]{2,1,0:T(8,128)(2,1)S(1)}, bf16[1,256,1024]{2,1,0:T(8,128)(2,1)}, u32[]{:S(2)}) copy-start(bf16[1,256,1024]{2,1,0:T(8,128)(2,1)} %param.7) | copy-start | bytes 1572868
  42.2 28.1 %copy-start.4 = (bf16[128,16,384]{2,0,1:T(8,128)(2,1)}, bf16[128,16,384]{2,0,1:T(8,128)(2,1)S(1)}, u32[]{:S(2)}) copy-start(bf16[128,16,384]{2,0,1:T(8,128)(2,1)S(1)} %all-to-all-done) | copy-start | bytes 4718596
  42.2 26.6 %all-to-all-start.1 = ((bf16[128,16,384]{2,0,1:T(8,128)(2,1)}), bf16[128,16,384]{2,0,1:T(8,128)(2,1)}, u32[]{:S(2)}, u32[]{:S(2)}) async-start(bf16[128,16,384]{2,0,1:T(8,128)(2,1)} %copy.47), calls=%async_computation.1 | async-start | bytes 3145728 | tf_op jit(solution)/shard_map/all_to_all | solution.py:143
  47.0 27.1 %copy-start.6 = (s32[1,256]{1,0:T(1,128)S(1)}, s32[1,256]{1,0:T(1,128)}, u32[]{:S(2)}) copy-start(s32[1,256]{1,0:T(1,128)} %param.10) | copy-start | bytes 3076
  70.3 32.8 %all-to-all-start.2 = ((bf16[256,16,256]{2,0,1:T(8,128)(2,1)}), bf16[256,16,256]{2,0,1:T(8,128)(2,1)S(1)}, u32[]{:S(2)}, u32[]{:S(2)}) async-start(bf16[256,16,256]{2,0,1:T(8,128)(2,1)} %bitcast.9), calls=%async_computation.2 | async-start | bytes 4194304 | tf_op jit(solution)/shard_map/all_to_all | solution.py:144
  74.1 236.7 %all-gather.2.cloned.1.call-start = ((), (), s32[]{:S(2)}) async-start(), calls=%async_computation.8 | async-start | bytes 4718592 | tf_op jit(solution)/shard_map/all_gather | solution.py:117
  103.1 1.3 copy-start.1
  213.2 221.8 %reduce-scatter.2.cloned.1.call-start = ((), (), s32[]{:S(2)}) async-start(), calls=%async_computation.9 | async-start | bytes 6684672 | tf_op jit(solution)/shard_map/reduce_scatter | solution.py:123
  232.5 26.6 %collective-permute-start = (bf16[256,1536]{0,1:T(8,128)(2,1)}, bf16[256,1536]{0,1:T(8,128)(2,1)}, u32[]{:S(2)}, u32[]{:S(2)}) collective-permute-start(bf16[256,1536]{0,1:T(8,128)(2,1)} %get-tuple-element.24), channel_id=1, source_target_pairs={{0,16},{16,32},{32,48},{48,64},{64,80},{80,96},{96,112},{112,0},{1... | collective-permute-start | bytes 2359304 | tf_op jit(solution)/shard_map/ppermute | solution.py:115
  232.5 29.7 %collective-permute-start.1 = (bf16[256,1536]{0,1:T(8,128)(2,1)}, bf16[256,1536]{0,1:T(8,128)(2,1)}, u32[]{:S(2)}, u32[]{:S(2)}) collective-permute-start(bf16[256,1536]{0,1:T(8,128)(2,1)} %get-tuple-element.23), channel_id=1, source_target_pairs={{0,32},{16,48},{32,64},{48,80},{64,96},{80,112},{96,0},{112,16},{1... | collective-permute-start | bytes 2359304 | tf_op jit(solution)/shard_map/ppermute | solution.py:115
  234.3 58.9 %collective-permute-start.2 = (bf16[256,1536]{0,1:T(8,128)(2,1)}, bf16[256,1536]{0,1:T(8,128)(2,1)}, u32[]{:S(2)}, u32[]{:S(2)}) collective-permute-start(bf16[256,1536]{0,1:T(8,128)(2,1)} %get-tuple-element.22), channel_id=1, source_target_pairs={{0,48},{16,64},{32,80},{48,96},{64,112},{80,0},{96,16},{112,32},{1... | collective-permute-start | bytes 2359304 | tf_op jit(solution)/shard_map/ppermute | solution.py:115
  237.2 58.1 %collective-permute-start.3 = (bf16[256,1536]{0,1:T(8,128)(2,1)S(1)}, bf16[256,1536]{0,1:T(8,128)(2,1)}, u32[]{:S(2)}, u32[]{:S(2)}) collective-permute-start(bf16[256,1536]{0,1:T(8,128)(2,1)S(1)} %get-tuple-element.21), channel_id=1, source_target_pairs={{0,64},{16,80},{32,96},{48,112},{64,0},{80,16},{96,32},{112,48},{1... | collective-permute-start | bytes 2359304 | tf_op jit(solution)/shard_map/ppermute | solution.py:115
  238.4 68.3 %collective-permute-start.4 = (bf16[256,1536]{0,1:T(8,128)(2,1)S(1)}, bf16[256,1536]{0,1:T(8,128)(2,1)}, u32[]{:S(2)}, u32[]{:S(2)}) collective-permute-start(bf16[256,1536]{0,1:T(8,128)(2,1)S(1)} %get-tuple-element.20), channel_id=1, source_target_pairs={{0,80},{16,96},{32,112},{48,0},{64,16},{80,32},{96,48},{112,64},{1... | collective-permute-start | bytes 2359304 | tf_op jit(solution)/shard_map/ppermute | solution.py:115
  259.1 49.7 %collective-permute-start.5 = (bf16[256,1536]{0,1:T(8,128)(2,1)S(1)}, bf16[256,1536]{0,1:T(8,128)(2,1)S(1)}, u32[]{:S(2)}, u32[]{:S(2)}) collective-permute-start(bf16[256,1536]{0,1:T(8,128)(2,1)S(1)} %get-tuple-element.19), channel_id=1, source_target_pairs={{0,96},{16,112},{32,0},{48,16},{64,32},{80,48},{96,64},{112,80},{1... | collective-permute-start | bytes 2359304 | tf_op jit(solution)/shard_map/ppermute | solution.py:115
  262.2 47.6 %collective-permute-start.6 = (bf16[256,1536]{0,1:T(8,128)(2,1)S(1)}, bf16[256,1536]{0,1:T(8,128)(2,1)S(1)}, u32[]{:S(2)}, u32[]{:S(2)}) collective-permute-start(bf16[256,1536]{0,1:T(8,128)(2,1)S(1)} %get-tuple-element.18), channel_id=1, source_target_pairs={{0,112},{16,0},{32,16},{48,32},{64,48},{80,64},{96,80},{112,96},{1... | collective-permute-start | bytes 2359304 | tf_op jit(solution)/shard_map/ppermute | solution.py:115
  310.8 4.7 %copy-start = (bf16[8,256,1024]{2,1,0:T(8,128)(2,1)S(1)}, bf16[8,256,1024]{2,1,0:T(8,128)(2,1)}, u32[]{:S(2)}) copy-start(bf16[8,256,1024]{2,1,0:T(8,128)(2,1)} %all-gather.2.cloned.1.call-done) | copy-start | bytes 12582916
  326.0 1.4 copy-start.3
  359.5 77.3 %all-to-all-start.4 = ((bf16[16,128,384]{2,1,0:T(8,128)(2,1)}), bf16[16,128,384]{2,1,0:T(8,128)(2,1)S(1)}, u32[]{:S(2)}, u32[]{:S(2)}) async-start(bf16[16,128,384]{2,1,0:T(8,128)(2,1)} %bitcast.92), calls=%async_computation.4 | async-start | bytes 3145728 | tf_op jit(solution)/shard_map/all_to_all | solution.py:155
  436.8 13.3 %all-to-all-start.6 = ((f32[96,8,128]{2,0,1:T(8,128)}), f32[96,8,128]{2,0,1:T(8,128)S(1)}, u32[]{:S(2)}, u32[]{:S(2)}) async-start(f32[96,8,128]{2,0,1:T(8,128)} %copy_bitcast_fusion), calls=%async_computation.7 | async-start | bytes 786432 | tf_op jit(solution)/shard_map/all_to_all | solution.py:124
Sparse Core Ops, SparseCore 0:
  213.3 36.1 all-gather.1
  326.2 108.7 reduce-scatter.1

commit v3 on v2

--- a/solution.py
+++ b/solution.py
@@ -100,6 +100,48 @@
     )(q_doc.reshape(rows, 1), k_doc.reshape(1, keys), head_queries, head_upstream, head_keys)
 
 
+def weight_kernel(me_ref, *refs, parts):
+    pieces, grad_ref, out_ref = refs[:parts], refs[parts], refs[parts + 1]
+    me = me_ref[0]
+    total = None
+    for shift in range(parts):
+        source = lax.rem(me - shift + parts, parts)
+        term = lax.dot_general(
+            pieces[shift][...], grad_ref[source], (((0,), (0,)), ((), ())),
+            preferred_element_type=jnp.float32,
+        )
+        total = term if total is None else total + term
+    out_ref[...] = total.astype(out_ref.dtype)
+
+
+def stacked_weight_product(me, pieces, grad_all):
+    parts = len(pieces)
+    rows, width = pieces[0].shape
+    columns = grad_all.shape[2]
+    tile = 512 if width % 512 == 0 else width
+    grid_spec = pltpu.PrefetchScalarGridSpec(
+        num_scalar_prefetch=1,
+        grid=(width // tile,),
+        in_specs=[pl.BlockSpec((rows, tile), lambda i, me: (0, i)) for _ in range(parts)]
+        + [pl.BlockSpec((parts, rows, columns), lambda i, me: (0, 0, 0))],
+        out_specs=pl.BlockSpec((tile, columns), lambda i, me: (i, 0)),
+    )
+    return pl.pallas_call(
+        functools.partial(weight_kernel, parts=parts),
+        grid_spec=grid_spec,
+        out_shape=jax.ShapeDtypeStruct((width, columns), jnp.bfloat16),
+        compiler_params=pltpu.CompilerParams(
+            dimension_semantics=("arbitrary",), vmem_limit_bytes=48 * 1024 * 1024
+        ),
+        cost_estimate=pl.CostEstimate(
+            flops=2 * parts * rows * width * columns,
+            transcendentals=0,
+            bytes_accessed=2 * parts * rows * (width + columns) + 2 * width * columns,
+        ),
+        name="weight_product",
+    )(jnp.reshape(me, (1,)).astype(jnp.int32), *pieces, grad_all)
+
+
 def weight_gradient(hidden_rows, grad_low):
     dp = lax.axis_size("dp")
     ctx = lax.axis_size("ctx")
@@ -113,15 +155,10 @@
         outgoing = lax.dynamic_index_in_dim(interleaved, (me + shift) % dp, 0, keepdims=False)
         pairs = [(i, (i + shift) % dp) for i in range(dp)]
         received.append(lax.ppermute(outgoing, "dp", pairs))
-    hidden_dp = jnp.concatenate(received, axis=0)
     grad_all = lax.all_gather(grad_low, "dp", axis=0, tiled=False)
-    grad_dp = jnp.concatenate(
-        [lax.dynamic_index_in_dim(grad_all, (me - shift) % dp, 0, keepdims=False) for shift in range(dp)],
-        axis=0,
-    )
-    partial = jnp.einsum("kd,kc->dc", hidden_dp, grad_dp, preferred_element_type=jnp.float32)
+    partial = stacked_weight_product(me, received, grad_all)
     reduced = lax.psum_scatter(partial, "ctx", scatter_dimension=0, tiled=True)
-    return lax.all_to_all(reduced, "dp", split_axis=1, concat_axis=0, tiled=True)
+    return lax.all_to_all(reduced.astype(jnp.float32), "dp", split_axis=1, concat_axis=0, tiled=True)
 
 
 def local_body(queries, kv_proj, hidden, grad_out, doc_lengths, slab_offsets):
@@ -149,7 +186,9 @@
     key_pos = offset - WINDOW + jnp.arange(keys, dtype=jnp.int32)
     q_doc = doc_index(query_pos, bounds)
     k_doc = jnp.where(key_pos >= 0, doc_index(key_pos, bounds), -1)
-    attended_heads, grad_query_heads, grad_head = head_attention(head_queries, head_upstream, head_keys, q_doc, k_doc)
+    attended_heads, grad_query_heads, grad_head = head_attention(
+        head_queries, head_upstream, head_keys, q_doc, k_doc
+    )
     attended, grad_query = (
         lax.all_to_all(attended_heads, "ctx", split_axis=0, concat_axis=1, tiled=True),
         lax.all_to_all(grad_query_heads, "ctx", split_axis=0, concat_axis=1, tiled=True),

time: 460 us -> 446 us (0.970)
  Pallas kernels: 73.4 us -> 84.2 us
  matrix products: 10.4 us -> 0 us
  waiting for transfers between devices: 181 us -> 171 us
  local copies, waits for them, and re-layouts: 62.1 us -> 54.2 us
    unnamed x33 -> x17, local copies, waits for them, and re-layouts: 33.8 us -> 15.2 us
    dynamic_slice x0 -> x9, local copies, waits for them, and re-layouts: none -> 17.7 us  [the longest x8 16.3 us: weight_gradient(): lax.dynamic_index_in_dim(interleaved, (me + shift) % dp, 0, keepdims=False)]
    pallas_call x0 -> x1, Pallas kernels: none -> 10.8 us  [stacked_weight_product(): pl.pallas_call(functools.partial(weight_kernel, parts=parts), grid_spec=g...]
    dot_general x1 -> x0, matrix products: 10.4 us -> none  [weight_gradient(): jnp.einsum('kd,kc->dc', hidden_dp, grad_dp, preferred_element_type=jnp.fl...]
    reduce_scatter x1, waiting for transfers between devices: 71.8 us -> 64 us  [weight_gradient(): reduced = lax.psum_scatter(partial, 'ctx', scatter_dimension=0, tiled=True)]
  transfers between devices with their start and end apart: 14 -> 14, of which waited for: 8 -> 11; matrix products, arithmetic and copies ran while one was open for 11% -> 11% of each run, Pallas kernels for 0% -> 0%
where the time goes in v3:
time: 446 us; the launch traced here: 444 us
  waiting for transfers between devices  171 us (38%)
  Pallas kernels  84.2 us (19%)
  blocking collectives  63.5 us (14%)
  local copies, waits for them, and re-layouts  54.2 us (12%)
  starting transfers between devices  49.4 us (11%)
  between operations  14.9 us (3%)
  other arithmetic  7.36 us (2%)
    pallas_call x1, Pallas kernels, head_attention(): pl.pallas_call(kernel, grid=grid, in_specs=[pl.BlockSpec((bq, 1), lambda...  73.4 us
    reduce_scatter x1, waiting for transfers between devices, weight_gradient(): reduced = lax.psum_scatter(partial, 'ctx', scatter_dimension=0, tiled=True)  64 us
    ppermute x7, waiting for transfers between devices, weight_gradient(): received.append(lax.ppermute(outgoing, 'dp', pairs))  37.8 us
    all_to_all x1, blocking collectives, local_body(): lax.all_to_all(attended_heads, 'ctx', split_axis=0, concat_axis=1, tiled=...  32.1 us
    all_to_all x1, blocking collectives, local_body(): lax.all_to_all(grad_head.astype(jnp.bfloat16), 'ctx', split_axis=0, conca...  31.4 us
    ppermute x7, starting transfers between devices, weight_gradient(): received.append(lax.ppermute(outgoing, 'dp', pairs))  25.4 us
    all_to_all x1, waiting for transfers between devices, local_body(): lax.all_to_all(copies, 'ctx', split_axis=1, concat_axis=0, tiled=True)  23.7 us
    all_to_all x1, waiting for transfers between devices, local_body(): lax.all_to_all(query_matrix_rows, 'ctx', split_axis=1, concat_axis=0, til...  22.7 us
  transfers between devices with their start and end apart: 14, of which 11 were waited for; matrix products, arithmetic and copies ran while one was open for 11% of the time, Pallas kernels for 0%

profile of v3, /device:TPU:0, one launch (start us, length us, event | category | flops | bytes accessed | tf_op | source)
XLA Modules:
  0.0 444.1 jit_solution(5353048112040161417)
XLA Ops:
  7.2 1.7 copy.92
  8.9 1.5 copy.71
  10.4 7.3 %all-to-all-start = ((bf16[128,16,384]{2,0,1:T(8,128)(2,1)}), bf16[128,16,384]{2,0,1:T(8,128)(2,1)S(1)}, u32[]{:S(2)}, u32[]{:S(2)}) async-start(bf16[128,16,384]{2,0,1:T(8,128)(2,1)} %copy.71), calls=%async_computation | async-start | bytes 3145728 | tf_op jit(solution)/shard_map/all_to_all | solution.py:179
  18.0 1.5 copy.72
  19.5 22.7 %all-to-all-done = bf16[128,16,384]{2,0,1:T(8,128)(2,1)S(1)} async-done(((bf16[128,16,384]{2,0,1:T(8,128)(2,1)}), bf16[128,16,384]{2,0,1:T(8,128)(2,1)S(1)}, u32[]{:S(2)}, u32[]{:S(2)}) %all-to-all-start) | async-done | bytes 1572896 | tf_op jit(solution)/shard_map/all_to_all | solution.py:179
  42.2 4.4 all-to-all-start.1
  47.1 21.7 %all-to-all-done.1 = bf16[128,16,384]{2,0,1:T(8,128)(2,1)} async-done(((bf16[128,16,384]{2,0,1:T(8,128)(2,1)}), bf16[128,16,384]{2,0,1:T(8,128)(2,1)}, u32[]{:S(2)}, u32[]{:S(2)}) %all-to-all-start.1) | async-done | bytes 1572896 | tf_op jit(solution)/shard_map/all_to_all | solution.py:180
  68.8 1.5 broadcast_in_dim.24
  70.3 3.8 all-to-all-start.2
  76.2 1.5 copy.74.qdoc_ref
  77.6 1.3 convert_reduce_fusion
  79.5 23.7 %all-to-all-done.2 = bf16[256,16,256]{2,0,1:T(8,128)(2,1)S(1)} async-done(((bf16[256,16,256]{2,0,1:T(8,128)(2,1)}), bf16[256,16,256]{2,0,1:T(8,128)(2,1)S(1)}, u32[]{:S(2)}, u32[]{:S(2)}) %all-to-all-start.2) | async-done | bytes 2097184 | tf_op jit(solution)/shard_map/all_to_all | solution.py:181
  103.2 1.3 copy-done
  104.5 73.4 %band_attention.1 = (bf16[2048,384]{1,0:T(8,128)(2,1)}, bf16[2048,384]{1,0:T(8,128)(2,1)}, f32[4096,256]{1,0:T(8,128)}) custom-call(s32[2048,1]{1,0:T(8,128)} %copy.74.qdoc_ref, s32[1,4096]{1,0:T(1,128)} %compare_select_fusion.kdoc_ref, bf16[2048,384]{1,0:T(8,128)(2,1)} %bitcast.69, bf16[2048,384]{1,0:T(8,128)(2,1)} %bitcast.8.go_ref, bf16[4096,256]{1,0:T(8,128)(2,1)} %bitcast.63), custom_call_target="tpu_custom_call" | custom-call | flops 21743271936 | bytes 12582912 | tf_op jit(solution)/shard_map/band_attention/pallas_call | solution.py:73
  178.0 2.4 convert_element_type.34
  180.4 31.4 %all_to_all.127 = bf16[16,256,256]{2,1,0:T(8,128)(2,1)S(1)} all-to-all(bf16[16,256,256]{2,1,0:T(8,128)(2,1)S(1)} %bitcast.58), channel_id=1, replica_groups=mesh['dp'=8,'ctx'=16] {'ctx'}, dimensions={0} | all-to-all | bytes 4194304 | tf_op jit(solution)/shard_map/all_to_all | solution.py:196
  212.3 1.0 copy.90
  213.4 8.7 %copy.78 = bf16[1,256,12288]{1,2,0:T(8,128)(2,1)} copy(bf16[1,256,12288]{2,1,0:T(8,128)(2,1)} %param.8) | data formatting | bytes 12582912 | tf_op args[2]
  222.1 6.3 %copy.79 = bf16[8,256,16,96]{1,3,2,0:T(8,128)(2,1)} copy(bf16[8,256,16,96]{1,3,0,2:T(8,128)(2,1)} %bitcast.57) | data formatting | bytes 12582912 | tf_op jit(solution)/shard_map/transpose | solution.py:152
  228.4 4.7 %constant_dynamic-slice_fusion = (bf16[1,256,1536]{1,2,0:T(8,128)(2,1)S(1)}, bf16[1,256,1536]{1,2,0:T(8,128)(2,1)}, bf16[1,256,1536]{1,2,0:T(8,128)(2,1)}, bf16[...) fusion(bf16[8,256,1536]{1,2,0:T(8,128)(2,1)} %bitcast.56, ...), kind=kLoop, calls=%fused_computation.8 | loop fusion | bytes 12582944 | tf_op jit(solution)/shard_map/jit(dynamic_index_in_dim)/dynamic_slice | solution.py:155
  233.1 1.1 copy.81
  234.3 1.2 copy.82
  235.4 1.8 collective-permute-start.1
  237.2 1.2 copy.83
  238.4 2.9 collective-permute-start.2
  241.3 2.3 copy.84
  243.6 1.2 collective-permute-start.3
  244.9 2.3 copy.85
  247.2 2.3 collective-permute-start.4
  249.5 2.3 copy.86
  251.8 1.2 copy.87
  253.0 5.7 %collective-permute-done.refs_1_ = bf16[256,1536]{1,0:T(8,128)(2,1)S(1)} collective-permute-done((bf16[256,1536]{1,0:T(8,128)(2,1)}, bf16[256,1536]{1,0:T(8,128)(2,1)S(1)}, u32[]{:S(2)}, u32[]{:S(2)}) %collective-permute-start) | collective-permute-done | bytes 786464 | tf_op jit(solution)/shard_map/ppermute | solution.py:157
  260.2 16.2 %collective-permute-start.6 = (bf16[256,1536]{1,0:T(8,128)(2,1)}, bf16[256,1536]{1,0:T(8,128)(2,1)}, u32[]{:S(2)}, u32[]{:S(2)}) collective-permute-start(bf16[256,1536]{1,0:T(8,128)(2,1)} %bitcast.74), channel_id=1, source_target_pairs={{0,112},{16,0},{32,16},{48,32},{64,48},{80,64},{96,80},{112,96},{1... | collective-permute-start | bytes 2359304 | tf_op jit(solution)/shard_map/ppermute | solution.py:157
  276.3 1.4 copy.80
  277.7 15.1 %collective-permute-done.2.refs_3_ = bf16[256,1536]{1,0:T(8,128)(2,1)S(1)} collective-permute-done((bf16[256,1536]{1,0:T(8,128)(2,1)}, bf16[256,1536]{1,0:T(8,128)(2,1)S(1)}, u32[]{:S(2)}, u32[]{:S(2)}) %collective-permute-start.2) | collective-permute-done | bytes 786464 | tf_op jit(solution)/shard_map/ppermute | solution.py:157
  292.8 1.2 collective-permute-done.3.refs_4_
  294.0 12.9 %collective-permute-done.4.refs_5_ = bf16[256,1536]{1,0:T(8,128)(2,1)} collective-permute-done((bf16[256,1536]{1,0:T(8,128)(2,1)}, bf16[256,1536]{1,0:T(8,128)(2,1)}, u32[]{:S(2)}, u32[]{:S(2)}) %collective-permute-start.4) | collective-permute-done | bytes 786464 | tf_op jit(solution)/shard_map/ppermute | solution.py:157
  306.9 2.4 collective-permute-done.6.refs_7_
  309.3 10.8 %weight_product.1 = bf16[1536,1024]{1,0:T(8,128)(2,1)} custom-call(s32[1]{0:T(128)} %bitcast.20.me_ref, bf16[256,1536]{1,0:T(8,128)(2,1)S(1)} %bitcast.55, bf16[256,1536]{1,0:T(8,128)(2,1)S(1)} %collective-permute-done.refs_1_, bf16[256,1536]{1,0:T(8,128)(2,1)S(1)} %collective-permute-done.1.refs_2_, bf16[256,1536]{1,0:T(8,128)(2,1)S(1)} %collective-permute-done.2.refs_3_, ...), custom_call_target="tpu_custom_call" | custom-call | flops 6442450944 | bytes 13631488 | tf_op jit(solution)/shard_map/weight_product/pallas_call | solution.py:129
  320.1 1.4 copy-done.2
  321.5 32.1 %all_to_all.128 = bf16[16,128,384]{2,1,0:T(8,128)(2,1)S(1)} all-to-all(bf16[16,128,384]{2,1,0:T(8,128)(2,1)S(1)} %bitcast.68), channel_id=1, replica_groups=mesh['dp'=8,'ctx'=16] {'ctx'}, dimensions={0} | all-to-all | bytes 3145728 | tf_op jit(solution)/shard_map/all_to_all | solution.py:193
  353.6 3.9 all-to-all-start.4
  357.5 64.0 %reduce-scatter.2.cloned.1.call-done = bf16[96,1024]{1,0:T(8,128)(2,1)} async-done(((bf16[1536,1024]{1,0:T(8,128)(2,1)}), bf16[96,1024]{1,0:T(8,128)(2,1)}) %reduce-scatter.2.cloned.1.call-update) | async-done | bytes 196624 | tf_op jit(solution)/shard_map/reduce_scatter | solution.py:160
  421.5 1.7 copy_bitcast_fusion
  423.2 4.4 all-to-all-start.6
  427.6 2.1 copy.75
  429.7 3.6 broadcast_in_dim.25
  434.2 1.6 broadcast_in_dim.26
  (37 shorter events, 7.2 us)
Async XLA Ops:
  10.4 7.3 %copy-start.1 = (bf16[1,128,6144]{2,1,0:T(8,128)(2,1)S(1)}, bf16[1,128,6144]{2,1,0:T(8,128)(2,1)}, u32[]{:S(2)}) copy-start(bf16[1,128,6144]{2,1,0:T(8,128)(2,1)} %param.9) | copy-start | bytes 4718596
  10.4 31.8 %all-to-all-start = ((bf16[128,16,384]{2,0,1:T(8,128)(2,1)}), bf16[128,16,384]{2,0,1:T(8,128)(2,1)S(1)}, u32[]{:S(2)}, u32[]{:S(2)}) async-start(bf16[128,16,384]{2,0,1:T(8,128)(2,1)} %copy.71), calls=%async_computation | async-start | bytes 3145728 | tf_op jit(solution)/shard_map/all_to_all | solution.py:179
  19.5 27.1 %copy-start.4 = (bf16[1,256,1024]{2,1,0:T(8,128)(2,1)S(1)}, bf16[1,256,1024]{2,1,0:T(8,128)(2,1)}, u32[]{:S(2)}) copy-start(bf16[1,256,1024]{2,1,0:T(8,128)(2,1)} %param.7) | copy-start | bytes 1572868
  42.2 4.8 %copy-start.3 = (bf16[128,16,384]{2,0,1:T(8,128)(2,1)}, bf16[128,16,384]{2,0,1:T(8,128)(2,1)S(1)}, u32[]{:S(2)}) copy-start(bf16[128,16,384]{2,0,1:T(8,128)(2,1)S(1)} %all-to-all-done) | copy-start | bytes 4718596
  42.2 26.6 %all-to-all-start.1 = ((bf16[128,16,384]{2,0,1:T(8,128)(2,1)}), bf16[128,16,384]{2,0,1:T(8,128)(2,1)}, u32[]{:S(2)}, u32[]{:S(2)}) async-start(bf16[128,16,384]{2,0,1:T(8,128)(2,1)} %copy.72), calls=%async_computation.1 | async-start | bytes 3145728 | tf_op jit(solution)/shard_map/all_to_all | solution.py:180
  70.3 3.9 copy-start.5
  70.3 32.9 %all-to-all-start.2 = ((bf16[256,16,256]{2,0,1:T(8,128)(2,1)}), bf16[256,16,256]{2,0,1:T(8,128)(2,1)S(1)}, u32[]{:S(2)}, u32[]{:S(2)}) async-start(bf16[256,16,256]{2,0,1:T(8,128)(2,1)} %bitcast.9), calls=%async_computation.2 | async-start | bytes 4194304 | tf_op jit(solution)/shard_map/all_to_all | solution.py:181
  74.2 235.1 %all-gather.2.cloned.1.call-start = ((), (), s32[]{:S(2)}) async-start(), calls=%async_computation.8 | async-start | bytes 4718592 | tf_op jit(solution)/shard_map/all_gather | solution.py:158
  103.2 1.3 copy-start
  213.3 208.2 %reduce-scatter.2.cloned.1.call-start = ((), (), s32[]{:S(2)}) async-start(), calls=%async_computation.9 | async-start | bytes 3342336 | tf_op jit(solution)/shard_map/reduce_scatter | solution.py:160
  234.3 24.4 %collective-permute-start = (bf16[256,1536]{1,0:T(8,128)(2,1)}, bf16[256,1536]{1,0:T(8,128)(2,1)S(1)}, u32[]{:S(2)}, u32[]{:S(2)}) collective-permute-start(bf16[256,1536]{1,0:T(8,128)(2,1)} %bitcast.77), channel_id=1, source_target_pairs={{0,16},{16,32},{32,48},{48,64},{64,80},{80,96},{96,112},{112,0},{1... | collective-permute-start | bytes 2359304 | tf_op jit(solution)/shard_map/ppermute | solution.py:157
  235.4 24.7 %collective-permute-start.1 = (bf16[256,1536]{1,0:T(8,128)(2,1)}, bf16[256,1536]{1,0:T(8,128)(2,1)S(1)}, u32[]{:S(2)}, u32[]{:S(2)}) collective-permute-start(bf16[256,1536]{1,0:T(8,128)(2,1)} %bitcast.75), channel_id=1, source_target_pairs={{0,32},{16,48},{32,64},{48,80},{64,96},{80,112},{96,0},{112,16},{1... | collective-permute-start | bytes 2359304 | tf_op jit(solution)/shard_map/ppermute | solution.py:157
  238.4 54.4 %collective-permute-start.2 = (bf16[256,1536]{1,0:T(8,128)(2,1)}, bf16[256,1536]{1,0:T(8,128)(2,1)S(1)}, u32[]{:S(2)}, u32[]{:S(2)}) collective-permute-start(bf16[256,1536]{1,0:T(8,128)(2,1)} %bitcast.71), channel_id=1, source_target_pairs={{0,48},{16,64},{32,80},{48,96},{64,112},{80,0},{96,16},{112,32},{1... | collective-permute-start | bytes 2359304 | tf_op jit(solution)/shard_map/ppermute | solution.py:157
  243.6 50.3 %collective-permute-start.3 = (bf16[256,1536]{1,0:T(8,128)(2,1)}, bf16[256,1536]{1,0:T(8,128)(2,1)}, u32[]{:S(2)}, u32[]{:S(2)}) collective-permute-start(bf16[256,1536]{1,0:T(8,128)(2,1)} %bitcast.72), channel_id=1, source_target_pairs={{0,64},{16,80},{32,96},{48,112},{64,0},{80,16},{96,32},{112,48},{1... | collective-permute-start | bytes 2359304 | tf_op jit(solution)/shard_map/ppermute | solution.py:157
  247.2 59.7 %collective-permute-start.4 = (bf16[256,1536]{1,0:T(8,128)(2,1)}, bf16[256,1536]{1,0:T(8,128)(2,1)}, u32[]{:S(2)}, u32[]{:S(2)}) collective-permute-start(bf16[256,1536]{1,0:T(8,128)(2,1)} %bitcast.73), channel_id=1, source_target_pairs={{0,80},{16,96},{32,112},{48,0},{64,16},{80,32},{96,48},{112,64},{1... | collective-permute-start | bytes 2359304 | tf_op jit(solution)/shard_map/ppermute | solution.py:157
  258.7 48.2 %collective-permute-start.5 = (bf16[256,1536]{1,0:T(8,128)(2,1)}, bf16[256,1536]{1,0:T(8,128)(2,1)}, u32[]{:S(2)}, u32[]{:S(2)}) collective-permute-start(bf16[256,1536]{1,0:T(8,128)(2,1)} %bitcast.76), channel_id=1, source_target_pairs={{0,96},{16,112},{32,0},{48,16},{64,32},{80,48},{96,64},{112,80},{1... | collective-permute-start | bytes 2359304 | tf_op jit(solution)/shard_map/ppermute | solution.py:157
  260.2 49.1 %collective-permute-start.6 = (bf16[256,1536]{1,0:T(8,128)(2,1)}, bf16[256,1536]{1,0:T(8,128)(2,1)}, u32[]{:S(2)}, u32[]{:S(2)}) collective-permute-start(bf16[256,1536]{1,0:T(8,128)(2,1)} %bitcast.74), channel_id=1, source_target_pairs={{0,112},{16,0},{32,16},{48,32},{64,48},{80,64},{96,80},{112,96},{1... | collective-permute-start | bytes 2359304 | tf_op jit(solution)/shard_map/ppermute | solution.py:157
  320.1 1.4 copy-start.2
  353.6 69.6 %all-to-all-start.4 = ((bf16[16,128,384]{2,1,0:T(8,128)(2,1)}), bf16[16,128,384]{2,1,0:T(8,128)(2,1)S(1)}, u32[]{:S(2)}, u32[]{:S(2)}) async-start(bf16[16,128,384]{2,1,0:T(8,128)(2,1)} %bitcast.67), calls=%async_computation.4 | async-start | bytes 3145728 | tf_op jit(solution)/shard_map/all_to_all | solution.py:194
  423.2 13.3 %all-to-all-start.6 = ((f32[96,8,128]{2,0,1:T(8,128)}), f32[96,8,128]{2,0,1:T(8,128)S(1)}, u32[]{:S(2)}, u32[]{:S(2)}) async-start(f32[96,8,128]{2,0,1:T(8,128)} %copy_bitcast_fusion), calls=%async_computation.7 | async-start | bytes 786432 | tf_op jit(solution)/shard_map/all_to_all | solution.py:161
Sparse Core Ops, SparseCore 0:
  213.4 34.0 all-gather.1
  320.3 101.1 reduce-scatter.1

commit v4 on v3

--- a/solution.py
+++ b/solution.py
@@ -46,7 +46,7 @@
     scores = jnp.where(allowed, scores, -1e30)
     maxima = jnp.max(scores, axis=1, keepdims=True)
     raised = jnp.exp(scores - maxima)
-    weights = raised / jnp.sum(raised, axis=1, keepdims=True)
+    weights = raised * (1.0 / jnp.sum(raised, axis=1, keepdims=True))
     weights_low = weights.astype(bf16)
     att = jnp.dot(weights_low, v, preferred_element_type=f32).astype(bf16)
     att_ref[...] = att
@@ -142,7 +142,7 @@
     )(jnp.reshape(me, (1,)).astype(jnp.int32), *pieces, grad_all)
 
 
-def weight_gradient(hidden_rows, grad_low):
+def send_hidden(hidden_rows):
     dp = lax.axis_size("dp")
     ctx = lax.axis_size("ctx")
     rows, features = hidden_rows.shape
@@ -155,7 +155,10 @@
         outgoing = lax.dynamic_index_in_dim(interleaved, (me + shift) % dp, 0, keepdims=False)
         pairs = [(i, (i + shift) % dp) for i in range(dp)]
         received.append(lax.ppermute(outgoing, "dp", pairs))
-    grad_all = lax.all_gather(grad_low, "dp", axis=0, tiled=False)
+    return me, received
+
+
+def weight_gradient(me, received, grad_all):
     partial = stacked_weight_product(me, received, grad_all)
     reduced = lax.psum_scatter(partial, "ctx", scatter_dimension=0, tiled=True)
     return lax.all_to_all(reduced.astype(jnp.float32), "dp", split_axis=1, concat_axis=0, tiled=True)
@@ -180,6 +183,7 @@
         lax.all_to_all(upstream_gradient, "ctx", split_axis=1, concat_axis=0, tiled=True),
         lax.all_to_all(copies, "ctx", split_axis=1, concat_axis=0, tiled=True),
     )
+    me, received = send_hidden(hidden_rows)
     rows = head_queries.shape[0]
     keys = head_keys.shape[0]
     query_pos = offset + jnp.arange(rows, dtype=jnp.int32)
@@ -203,7 +207,9 @@
         axis=2,
     ).reshape(partial_sums.shape[0], key_value_width)
     grad_low = grad_keys.astype(jnp.bfloat16)
-    grad_weight = weight_gradient(hidden_rows, grad_low)
+    grad_all = lax.all_gather(grad_low, "dp", axis=0, tiled=False)
+    attended, grad_query, grad_all = lax.optimization_barrier((attended, grad_query, grad_all))
+    grad_weight = weight_gradient(me, received, grad_all)
     return (attended[None], grad_query[None], grad_low[None], grad_weight)
 
 

time: 446 us -> 435 us (0.975)
  blocking collectives: 63.5 us -> 44.5 us
  waiting for transfers between devices: 171 us -> 184 us
    all_to_all x1, blocking collectives: 32.1 us -> 13.1 us  [weight_gradient(): lax.all_to_all(reduced.astype(jnp.float32), 'dp', split_axis=1, concat_ax...]
    reduce_scatter x1, waiting for transfers between devices: 64 us -> 78.9 us  [weight_gradient(): reduced = lax.psum_scatter(partial, 'ctx', scatter_dimension=0, tiled=True)]
    ppermute x7, starting transfers between devices: 25.4 us -> 20.1 us  [send_hidden(): received.append(lax.ppermute(outgoing, 'dp', pairs))]
    broadcast_in_dim x2 -> x0, local copies, waits for them, and re-layouts: 5.2 us -> none  [local_body(): return (attended[None], grad_query[None], grad_low[None], grad_weight)]
    unnamed x17 -> x18, local copies, waits for them, and re-layouts: 15.2 us -> 12.8 us
  transfers between devices with their start and end apart: 14 -> 14, of which waited for: 11 -> 9; matrix products, arithmetic and copies ran while one was open for 11% -> 11% of each run, Pallas kernels for 0% -> 0%
where the time goes in v4:
time: 435 us; the launch traced here: 433 us
  waiting for transfers between devices  184 us (42%)
  Pallas kernels  84.2 us (19%)
  local copies, waits for them, and re-layouts  51.8 us (12%)
  starting transfers between devices  46.7 us (11%)
  blocking collectives  44.5 us (10%)
  between operations  14.9 us (3%)
  other arithmetic  6.61 us (2%)
    reduce_scatter x1, waiting for transfers between devices, weight_gradient(): reduced = lax.psum_scatter(partial, 'ctx', scatter_dimension=0, tiled=True)  78.9 us
    pallas_call x1, Pallas kernels, head_attention(): pl.pallas_call(kernel, grid=grid, in_specs=[pl.BlockSpec((bq, 1), lambda...  73.4 us
    ppermute x7, waiting for transfers between devices, send_hidden(): received.append(lax.ppermute(outgoing, 'dp', pairs))  37.2 us
    all_to_all x1, blocking collectives, local_body(): lax.all_to_all(grad_head.astype(jnp.bfloat16), 'ctx', split_axis=0, conca...  31.4 us
    all_to_all x1, waiting for transfers between devices, local_body(): lax.all_to_all(copies, 'ctx', split_axis=1, concat_axis=0, tiled=True)  23.7 us
    all_to_all x1, waiting for transfers between devices, local_body(): lax.all_to_all(query_matrix_rows, 'ctx', split_axis=1, concat_axis=0, til...  22.7 us
    all_to_all x1, waiting for transfers between devices, local_body(): lax.all_to_all(upstream_gradient, 'ctx', split_axis=1, concat_axis=0, til...  21.7 us
    ppermute x7, starting transfers between devices, send_hidden(): received.append(lax.ppermute(outgoing, 'dp', pairs))  20.1 us
  transfers between devices with their start and end apart: 14, of which 9 were waited for; matrix products, arithmetic and copies ran while one was open for 11% of the time, Pallas kernels for 0%

profile of v4, /device:TPU:0, one launch (start us, length us, event | category | flops | bytes accessed | tf_op | source)
XLA Modules:
  0.0 433.1 jit_solution(228861053643206491)
XLA Ops:
  7.2 1.7 copy.94
  8.9 1.5 copy.71
  10.4 7.3 %all-to-all-start = ((bf16[128,16,384]{2,0,1:T(8,128)(2,1)}), bf16[128,16,384]{2,0,1:T(8,128)(2,1)S(1)}, u32[]{:S(2)}, u32[]{:S(2)}) async-start(bf16[128,16,384]{2,0,1:T(8,128)(2,1)} %copy.71), calls=%async_computation | async-start | bytes 3145728 | tf_op jit(solution)/shard_map/all_to_all | solution.py:182
  18.0 1.5 copy.72
  19.5 22.7 %all-to-all-done = bf16[128,16,384]{2,0,1:T(8,128)(2,1)S(1)} async-done(((bf16[128,16,384]{2,0,1:T(8,128)(2,1)}), bf16[128,16,384]{2,0,1:T(8,128)(2,1)S(1)}, u32[]{:S(2)}, u32[]{:S(2)}) %all-to-all-start) | async-done | bytes 1572896 | tf_op jit(solution)/shard_map/all_to_all | solution.py:182
  42.2 4.4 %all-to-all-start.1 = ((bf16[128,16,384]{2,0,1:T(8,128)(2,1)}), bf16[128,16,384]{2,0,1:T(8,128)(2,1)}, u32[]{:S(2)}, u32[]{:S(2)}) async-start(bf16[128,16,384]{2,0,1:T(8,128)(2,1)} %copy.72), calls=%async_computation.1 | async-start | bytes 3145728 | tf_op jit(solution)/shard_map/all_to_all | solution.py:183
  47.1 21.7 %all-to-all-done.1 = bf16[128,16,384]{2,0,1:T(8,128)(2,1)} async-done(((bf16[128,16,384]{2,0,1:T(8,128)(2,1)}), bf16[128,16,384]{2,0,1:T(8,128)(2,1)}, u32[]{:S(2)}, u32[]{:S(2)}) %all-to-all-start.1) | async-done | bytes 1572896 | tf_op jit(solution)/shard_map/all_to_all | solution.py:183
  68.8 1.5 broadcast_in_dim.24
  70.3 3.8 all-to-all-start.2
  76.2 1.4 copy.74.qdoc_ref
  77.6 1.3 convert_reduce_fusion
  79.5 23.7 %all-to-all-done.2 = bf16[256,16,256]{2,0,1:T(8,128)(2,1)S(1)} async-done(((bf16[256,16,256]{2,0,1:T(8,128)(2,1)}), bf16[256,16,256]{2,0,1:T(8,128)(2,1)S(1)}, u32[]{:S(2)}, u32[]{:S(2)}) %all-to-all-start.2) | async-done | bytes 2097184 | tf_op jit(solution)/shard_map/all_to_all | solution.py:184
  103.3 1.3 copy-done.2
  104.6 73.4 %band_attention.1 = (bf16[2048,384]{1,0:T(8,128)(2,1)}, bf16[2048,384]{1,0:T(8,128)(2,1)}, f32[4096,256]{1,0:T(8,128)}) custom-call(s32[2048,1]{1,0:T(8,128)} %copy.74.qdoc_ref, s32[1,4096]{1,0:T(1,128)} %compare_select_fusion.kdoc_ref, bf16[2048,384]{1,0:T(8,128)(2,1)} %bitcast.74, bf16[2048,384]{1,0:T(8,128)(2,1)} %bitcast.8.go_ref, bf16[4096,256]{1,0:T(8,128)(2,1)} %bitcast.68), custom_call_target="tpu_custom_call" | custom-call | flops 21743271936 | bytes 12582912 | tf_op jit(solution)/shard_map/band_attention/pallas_call | solution.py:73
  178.0 2.4 convert_element_type.34
  180.4 31.4 %all_to_all.133 = bf16[16,256,256]{2,1,0:T(8,128)(2,1)S(1)} all-to-all(bf16[16,256,256]{2,1,0:T(8,128)(2,1)S(1)} %bitcast.64), channel_id=1, replica_groups=mesh['dp'=8,'ctx'=16] {'ctx'}, dimensions={0} | all-to-all | bytes 4194304 | tf_op jit(solution)/shard_map/all_to_all | solution.py:200
  212.3 1.0 copy.78
  213.3 3.7 all-to-all-start.3
  217.1 8.7 %copy.79 = bf16[1,256,12288]{1,2,0:T(8,128)(2,1)} copy(bf16[1,256,12288]{2,1,0:T(8,128)(2,1)} %param.8) | data formatting | bytes 12582912 | tf_op args[2]
  225.8 6.1 %copy.80 = bf16[8,256,16,96]{1,3,2,0:T(8,128)(2,1)} copy(bf16[8,256,16,96]{1,3,0,2:T(8,128)(2,1)} %bitcast.63) | data formatting | bytes 12582912 | tf_op jit(solution)/shard_map/transpose | solution.py:152
  231.9 5.2 %constant_dynamic-slice_fusion = (bf16[1,256,1536]{1,2,0:T(8,128)(2,1)}, bf16[1,256,1536]{1,2,0:T(8,128)(2,1)}, bf16[1,256,1536]{1,2,0:T(8,128)(2,1)}, bf16[1,25...) fusion(bf16[8,256,1536]{1,2,0:T(8,128)(2,1)} %bitcast.62, ...), kind=kLoop, calls=%fused_computation.8 | loop fusion | bytes 12582944 | tf_op jit(solution)/shard_map/jit(dynamic_index_in_dim)/dynamic_slice | solution.py:155
  237.1 1.3 copy.82
  238.4 1.2 copy.83
  239.6 1.9 collective-permute-start.1
  241.5 7.3 %all-to-all-start.4 = ((bf16[16,128,384]{2,1,0:T(8,128)(2,1)}), bf16[16,128,384]{2,1,0:T(8,128)(2,1)}, u32[]{:S(2)}, u32[]{:S(2)}) async-start(bf16[16,128,384]{2,1,0:T(8,128)(2,1)} %bitcast.72), calls=%async_computation.4 | async-start | bytes 3145728 | tf_op jit(solution)/shard_map/all_to_all | solution.py:198
  248.8 2.3 copy.84
  251.1 2.6 collective-permute-start.2
  253.7 2.4 copy.85
  256.1 1.2 collective-permute-start.3
  257.3 2.3 copy.86
  259.6 2.6 collective-permute-start.4
  262.2 2.3 copy.87
  264.5 1.3 copy.88
  265.8 1.0 collective-permute-start.5
  266.8 10.7 %collective-permute-start.6 = (bf16[256,1536]{1,0:T(8,128)(2,1)}, bf16[256,1536]{1,0:T(8,128)(2,1)}, u32[]{:S(2)}, u32[]{:S(2)}) collective-permute-start(bf16[256,1536]{1,0:T(8,128)(2,1)} %bitcast.82), channel_id=1, source_target_pairs={{0,112},{16,0},{32,16},{48,32},{64,48},{80,64},{96,80},{112,96},{1... | collective-permute-start | bytes 2359304 | tf_op jit(solution)/shard_map/ppermute | solution.py:157
  277.5 1.4 copy.81
  278.9 2.8 copy.92
  281.7 2.8 copy.93
  284.5 9.5 %collective-permute-done.2.refs_3_ = bf16[256,1536]{1,0:T(8,128)(2,1)S(1)} collective-permute-done((bf16[256,1536]{1,0:T(8,128)(2,1)}, bf16[256,1536]{1,0:T(8,128)(2,1)S(1)}, u32[]{:S(2)}, u32[]{:S(2)}) %collective-permute-start.2) | collective-permute-done | bytes 786464 | tf_op jit(solution)/shard_map/ppermute | solution.py:157
  293.9 3.6 collective-permute-done.3.refs_4_
  297.6 11.0 %collective-permute-done.4.refs_5_ = bf16[256,1536]{1,0:T(8,128)(2,1)} collective-permute-done((bf16[256,1536]{1,0:T(8,128)(2,1)}, bf16[256,1536]{1,0:T(8,128)(2,1)}, u32[]{:S(2)}, u32[]{:S(2)}) %collective-permute-start.4) | collective-permute-done | bytes 786464 | tf_op jit(solution)/shard_map/ppermute | solution.py:157
  308.6 2.4 collective-permute-done.5.refs_6_
  311.0 10.7 %collective-permute-done.6.refs_7_ = bf16[256,1536]{1,0:T(8,128)(2,1)} collective-permute-done((bf16[256,1536]{1,0:T(8,128)(2,1)}, bf16[256,1536]{1,0:T(8,128)(2,1)}, u32[]{:S(2)}, u32[]{:S(2)}) %collective-permute-start.6) | collective-permute-done | bytes 786464 | tf_op jit(solution)/shard_map/ppermute | solution.py:157
  321.7 10.8 %weight_product.1 = bf16[1536,1024]{1,0:T(8,128)(2,1)} custom-call(s32[1]{0:T(128)} %bitcast.22.me_ref, bf16[256,1536]{1,0:T(8,128)(2,1)S(1)} %bitcast.61, bf16[256,1536]{1,0:T(8,128)(2,1)S(1)} %collective-permute-done.refs_1_, bf16[256,1536]{1,0:T(8,128)(2,1)S(1)} %collective-permute-done.1.refs_2_, bf16[256,1536]{1,0:T(8,128)(2,1)S(1)} %collective-permute-done.2.refs_3_, ...), custom_call_target="tpu_custom_call" | custom-call | flops 6442450944 | bytes 13631488 | tf_op jit(solution)/shard_map/weight_product/pallas_call | solution.py:129
  332.5 78.9 %reduce-scatter.2.cloned.1.call-done = bf16[96,1024]{1,0:T(8,128)(2,1)} async-done(((bf16[1536,1024]{1,0:T(8,128)(2,1)}), bf16[96,1024]{1,0:T(8,128)(2,1)}) %reduce-scatter.2.cloned.1.call-update) | async-done | bytes 196624 | tf_op jit(solution)/shard_map/reduce_scatter | solution.py:163
  411.4 1.0 copy_bitcast_fusion
  412.3 13.1 %all_to_all.134 = f32[96,8,128]{2,0,1:T(8,128)S(1)} all-to-all(f32[96,8,128]{2,0,1:T(8,128)S(1)} %copy_bitcast_fusion), channel_id=1, replica_groups=mesh['dp'=8,'ctx'=16] {'dp'}, dimensions={1} | all-to-all | bytes 786432 | tf_op jit(solution)/shard_map/all_to_all | solution.py:164
  425.5 0.7 copy.99
  (37 shorter events, 3.3 us)
Async XLA Ops:
  10.4 7.3 %copy-start.3 = (bf16[1,128,6144]{2,1,0:T(8,128)(2,1)S(1)}, bf16[1,128,6144]{2,1,0:T(8,128)(2,1)}, u32[]{:S(2)}) copy-start(bf16[1,128,6144]{2,1,0:T(8,128)(2,1)} %param.9) | copy-start | bytes 4718596
  10.4 31.8 %all-to-all-start = ((bf16[128,16,384]{2,0,1:T(8,128)(2,1)}), bf16[128,16,384]{2,0,1:T(8,128)(2,1)S(1)}, u32[]{:S(2)}, u32[]{:S(2)}) async-start(bf16[128,16,384]{2,0,1:T(8,128)(2,1)} %copy.71), calls=%async_computation | async-start | bytes 3145728 | tf_op jit(solution)/shard_map/all_to_all | solution.py:182
  19.5 27.1 %copy-start.5 = (bf16[1,256,1024]{2,1,0:T(8,128)(2,1)S(1)}, bf16[1,256,1024]{2,1,0:T(8,128)(2,1)}, u32[]{:S(2)}) copy-start(bf16[1,256,1024]{2,1,0:T(8,128)(2,1)} %param.7) | copy-start | bytes 1572868
  42.2 4.8 %copy-start.4 = (bf16[128,16,384]{2,0,1:T(8,128)(2,1)}, bf16[128,16,384]{2,0,1:T(8,128)(2,1)S(1)}, u32[]{:S(2)}) copy-start(bf16[128,16,384]{2,0,1:T(8,128)(2,1)S(1)} %all-to-all-done) | copy-start | bytes 4718596
  42.2 26.6 %all-to-all-start.1 = ((bf16[128,16,384]{2,0,1:T(8,128)(2,1)}), bf16[128,16,384]{2,0,1:T(8,128)(2,1)}, u32[]{:S(2)}, u32[]{:S(2)}) async-start(bf16[128,16,384]{2,0,1:T(8,128)(2,1)} %copy.72), calls=%async_computation.1 | async-start | bytes 3145728 | tf_op jit(solution)/shard_map/all_to_all | solution.py:183
  70.3 3.9 copy-start.6
  70.3 32.9 %all-to-all-start.2 = ((bf16[256,16,256]{2,0,1:T(8,128)(2,1)}), bf16[256,16,256]{2,0,1:T(8,128)(2,1)S(1)}, u32[]{:S(2)}, u32[]{:S(2)}) async-start(bf16[256,16,256]{2,0,1:T(8,128)(2,1)} %bitcast.9), calls=%async_computation.2 | async-start | bytes 4194304 | tf_op jit(solution)/shard_map/all_to_all | solution.py:184
  74.2 210.3 %all-gather.2.cloned.1.call-start = ((), (), s32[]{:S(2)}) async-start(), calls=%async_computation.8 | async-start | bytes 4718592 | tf_op jit(solution)/shard_map/all_gather | solution.py:210
  103.3 1.3 copy-start.2
  213.3 28.2 %all-to-all-start.3 = ((bf16[16,128,384]{2,1,0:T(8,128)(2,1)}), bf16[16,128,384]{2,1,0:T(8,128)(2,1)S(1)}, u32[]{:S(2)}, u32[]{:S(2)}) async-start(bf16[16,128,384]{2,1,0:T(8,128)(2,1)} %bitcast.73), calls=%async_computation.3 | async-start | bytes 3145728 | tf_op jit(solution)/shard_map/all_to_all | solution.py:197
  238.4 27.4 %collective-permute-start = (bf16[256,1536]{1,0:T(8,128)(2,1)}, bf16[256,1536]{1,0:T(8,128)(2,1)S(1)}, u32[]{:S(2)}, u32[]{:S(2)}) collective-permute-start(bf16[256,1536]{1,0:T(8,128)(2,1)} %bitcast.83), channel_id=1, source_target_pairs={{0,16},{16,32},{32,48},{48,64},{64,80},{80,96},{96,112},{112,0},{1... | collective-permute-start | bytes 2359304 | tf_op jit(solution)/shard_map/ppermute | solution.py:157
  239.6 27.2 %collective-permute-start.1 = (bf16[256,1536]{1,0:T(8,128)(2,1)}, bf16[256,1536]{1,0:T(8,128)(2,1)S(1)}, u32[]{:S(2)}, u32[]{:S(2)}) collective-permute-start(bf16[256,1536]{1,0:T(8,128)(2,1)} %bitcast.80), channel_id=1, source_target_pairs={{0,32},{16,48},{32,64},{48,80},{64,96},{80,112},{96,0},{112,16},{1... | collective-permute-start | bytes 2359304 | tf_op jit(solution)/shard_map/ppermute | solution.py:157
  241.5 9.6 %copy-start = (bf16[16,128,384]{2,1,0:T(8,128)(2,1)}, bf16[16,128,384]{2,1,0:T(8,128)(2,1)S(1)}, u32[]{:S(2)}) copy-start(bf16[16,128,384]{2,1,0:T(8,128)(2,1)S(1)} %all-to-all-done.3) | copy-start | bytes 4718596
  241.5 40.2 %all-to-all-start.4 = ((bf16[16,128,384]{2,1,0:T(8,128)(2,1)}), bf16[16,128,384]{2,1,0:T(8,128)(2,1)}, u32[]{:S(2)}, u32[]{:S(2)}) async-start(bf16[16,128,384]{2,1,0:T(8,128)(2,1)} %bitcast.72), calls=%async_computation.4 | async-start | bytes 3145728 | tf_op jit(solution)/shard_map/all_to_all | solution.py:198
  248.7 162.6 %reduce-scatter.2.cloned.1.call-start = ((), (), s32[]{:S(2)}) async-start(), calls=%async_computation.9 | async-start | bytes 3342336 | tf_op jit(solution)/shard_map/reduce_scatter | solution.py:163
  251.1 42.9 %collective-permute-start.2 = (bf16[256,1536]{1,0:T(8,128)(2,1)}, bf16[256,1536]{1,0:T(8,128)(2,1)S(1)}, u32[]{:S(2)}, u32[]{:S(2)}) collective-permute-start(bf16[256,1536]{1,0:T(8,128)(2,1)} %bitcast.78), channel_id=1, source_target_pairs={{0,48},{16,64},{32,80},{48,96},{64,112},{80,0},{96,16},{112,32},{1... | collective-permute-start | bytes 2359304 | tf_op jit(solution)/shard_map/ppermute | solution.py:157
  253.7 10.8 %copy-start.1 = (bf16[1,256,1536]{1,2,0:T(8,128)(2,1)S(1)}, bf16[1,256,1536]{1,2,0:T(8,128)(2,1)}, u32[]{:S(2)}) copy-start(bf16[1,256,1536]{1,2,0:T(8,128)(2,1)} %get-tuple-element.24) | copy-start | bytes 2359300
  256.1 41.5 %collective-permute-start.3 = (bf16[256,1536]{1,0:T(8,128)(2,1)}, bf16[256,1536]{1,0:T(8,128)(2,1)}, u32[]{:S(2)}, u32[]{:S(2)}) collective-permute-start(bf16[256,1536]{1,0:T(8,128)(2,1)} %bitcast.79), channel_id=1, source_target_pairs={{0,64},{16,80},{32,96},{48,112},{64,0},{80,16},{96,32},{112,48},{1... | collective-permute-start | bytes 2359304 | tf_op jit(solution)/shard_map/ppermute | solution.py:157
  259.6 49.0 %collective-permute-start.4 = (bf16[256,1536]{1,0:T(8,128)(2,1)}, bf16[256,1536]{1,0:T(8,128)(2,1)}, u32[]{:S(2)}, u32[]{:S(2)}) collective-permute-start(bf16[256,1536]{1,0:T(8,128)(2,1)} %bitcast.81), channel_id=1, source_target_pairs={{0,80},{16,96},{32,112},{48,0},{64,16},{80,32},{96,48},{112,64},{1... | collective-permute-start | bytes 2359304 | tf_op jit(solution)/shard_map/ppermute | solution.py:157
  265.8 45.2 %collective-permute-start.5 = (bf16[256,1536]{1,0:T(8,128)(2,1)}, bf16[256,1536]{1,0:T(8,128)(2,1)}, u32[]{:S(2)}, u32[]{:S(2)}) collective-permute-start(bf16[256,1536]{1,0:T(8,128)(2,1)} %bitcast.84), channel_id=1, source_target_pairs={{0,96},{16,112},{32,0},{48,16},{64,32},{80,48},{96,64},{112,80},{1... | collective-permute-start | bytes 2359304 | tf_op jit(solution)/shard_map/ppermute | solution.py:157
  266.8 54.9 %collective-permute-start.6 = (bf16[256,1536]{1,0:T(8,128)(2,1)}, bf16[256,1536]{1,0:T(8,128)(2,1)}, u32[]{:S(2)}, u32[]{:S(2)}) collective-permute-start(bf16[256,1536]{1,0:T(8,128)(2,1)} %bitcast.82), channel_id=1, source_target_pairs={{0,112},{16,0},{32,16},{48,32},{64,48},{80,64},{96,80},{112,96},{1... | collective-permute-start | bytes 2359304 | tf_op jit(solution)/shard_map/ppermute | solution.py:157
Sparse Core Ops, SparseCore 0:
  213.4 30.7 all-gather.1
  332.6 78.6 reduce-scatter.1

commit v5 on v4

--- a/solution.py
+++ b/solution.py
@@ -12,6 +12,7 @@
 KEY_VALUE_HEADS = 4
 WINDOW = 2048
 BLOCK_QUERIES = 256
+CTX_ROWS = 4
 
 
 def doc_index(positions, bounds):
@@ -149,7 +150,12 @@
     piece = features // (ctx * dp)
     width = features // dp
     me = lax.axis_index("dp")
-    interleaved = hidden_rows.reshape(rows, ctx, dp, piece).transpose(2, 0, 1, 3).reshape(dp, rows, width)
+    across = ctx // CTX_ROWS
+    interleaved = (
+        hidden_rows.reshape(rows, CTX_ROWS, across, dp, piece)
+        .transpose(3, 0, 2, 1, 4)
+        .reshape(dp, rows, width)
+    )
     received = [lax.dynamic_index_in_dim(interleaved, me, 0, keepdims=False)]
     for shift in range(1, dp):
         outgoing = lax.dynamic_index_in_dim(interleaved, (me + shift) % dp, 0, keepdims=False)
@@ -160,7 +166,12 @@
 
 def weight_gradient(me, received, grad_all):
     partial = stacked_weight_product(me, received, grad_all)
-    reduced = lax.psum_scatter(partial, "ctx", scatter_dimension=0, tiled=True)
+    ctx = lax.axis_size("ctx")
+    across = ctx // CTX_ROWS
+    along_x = [[y * across + x for x in range(across)] for y in range(CTX_ROWS)]
+    along_y = [[y * across + x for y in range(CTX_ROWS)] for x in range(across)]
+    reduced = lax.psum_scatter(partial, "ctx", scatter_dimension=0, axis_index_groups=along_x, tiled=True)
+    reduced = lax.psum_scatter(reduced, "ctx", scatter_dimension=0, axis_index_groups=along_y, tiled=True)
     return lax.all_to_all(reduced.astype(jnp.float32), "dp", split_axis=1, concat_axis=0, tiled=True)
 
 
@@ -190,9 +201,7 @@
     key_pos = offset - WINDOW + jnp.arange(keys, dtype=jnp.int32)
     q_doc = doc_index(query_pos, bounds)
     k_doc = jnp.where(key_pos >= 0, doc_index(key_pos, bounds), -1)
-    attended_heads, grad_query_heads, grad_head = head_attention(
-        head_queries, head_upstream, head_keys, q_doc, k_doc
-    )
+    attended_heads, grad_query_heads, grad_head = head_attention(head_queries, head_upstream, head_keys, q_doc, k_doc)
     attended, grad_query = (
         lax.all_to_all(attended_heads, "ctx", split_axis=0, concat_axis=1, tiled=True),
         lax.all_to_all(grad_query_heads, "ctx", split_axis=0, concat_axis=1, tiled=True),

time: 435 us -> 421 us (0.968)
  waiting for transfers between devices: 184 us -> 171 us
    reduce_scatter x1 -> x2, waiting for transfers between devices: 78.9 us -> 65.2 us  [the longest x1 40.4 us: weight_gradient(): lax.psum_scatter(partial, 'ctx', scatter_dimension=0, axis_index_groups=a...]
  transfers between devices with their start and end apart: 14 -> 15, of which waited for: 9 -> 10; matrix products, arithmetic and copies ran while one was open for 11% -> 11% of each run, Pallas kernels for 0% -> 0%
where the time goes in v5:
time: 421 us; the launch traced here: 419 us
  waiting for transfers between devices  171 us (41%)
  Pallas kernels  84.2 us (20%)
  local copies, waits for them, and re-layouts  51.9 us (12%)
  starting transfers between devices  46.7 us (11%)
  blocking collectives  44.5 us (11%)
  between operations  14.7 us (3%)
  other arithmetic  6.61 us (2%)
    pallas_call x1, Pallas kernels, head_attention(): pl.pallas_call(kernel, grid=grid, in_specs=[pl.BlockSpec((bq, 1), lambda...  73.4 us
    reduce_scatter x1, waiting for transfers between devices, weight_gradient(): lax.psum_scatter(partial, 'ctx', scatter_dimension=0, axis_index_groups=a...  40.4 us
    ppermute x7, waiting for transfers between devices, send_hidden(): received.append(lax.ppermute(outgoing, 'dp', pairs))  37.2 us
    all_to_all x1, blocking collectives, local_body(): lax.all_to_all(grad_head.astype(jnp.bfloat16), 'ctx', split_axis=0, conca...  31.4 us
    reduce_scatter x1, waiting for transfers between devices, weight_gradient(): lax.psum_scatter(reduced, 'ctx', scatter_dimension=0, axis_index_groups=a...  24.8 us
    all_to_all x1, waiting for transfers between devices, local_body(): lax.all_to_all(copies, 'ctx', split_axis=1, concat_axis=0, tiled=True)  23.7 us
    all_to_all x1, waiting for transfers between devices, local_body(): lax.all_to_all(query_matrix_rows, 'ctx', split_axis=1, concat_axis=0, til...  22.7 us
    all_to_all x1, waiting for transfers between devices, local_body(): lax.all_to_all(upstream_gradient, 'ctx', split_axis=1, concat_axis=0, til...  21.7 us
  transfers between devices with their start and end apart: 15, of which 10 were waited for; matrix products, arithmetic and copies ran while one was open for 11% of the time, Pallas kernels for 0%

profile of v5, /device:TPU:0, one launch (start us, length us, event | category | flops | bytes accessed | tf_op | source)
XLA Modules:
  0.0 419.2 jit_solution(2751282956959547092)
XLA Ops:
  7.2 1.7 copy.94
  8.9 1.5 copy.71
  10.4 7.3 %all-to-all-start = ((bf16[128,16,384]{2,0,1:T(8,128)(2,1)}), bf16[128,16,384]{2,0,1:T(8,128)(2,1)S(1)}, u32[]{:S(2)}, u32[]{:S(2)}) async-start(bf16[128,16,384]{2,0,1:T(8,128)(2,1)} %copy.71), calls=%async_computation | async-start | bytes 3145728 | tf_op jit(solution)/shard_map/all_to_all | solution.py:193
  18.0 1.5 copy.72
  19.5 22.7 %all-to-all-done = bf16[128,16,384]{2,0,1:T(8,128)(2,1)S(1)} async-done(((bf16[128,16,384]{2,0,1:T(8,128)(2,1)}), bf16[128,16,384]{2,0,1:T(8,128)(2,1)S(1)}, u32[]{:S(2)}, u32[]{:S(2)}) %all-to-all-start) | async-done | bytes 1572896 | tf_op jit(solution)/shard_map/all_to_all | solution.py:193
  42.2 4.4 %all-to-all-start.1 = ((bf16[128,16,384]{2,0,1:T(8,128)(2,1)}), bf16[128,16,384]{2,0,1:T(8,128)(2,1)}, u32[]{:S(2)}, u32[]{:S(2)}) async-start(bf16[128,16,384]{2,0,1:T(8,128)(2,1)} %copy.72), calls=%async_computation.1 | async-start | bytes 3145728 | tf_op jit(solution)/shard_map/all_to_all | solution.py:194
  47.1 21.7 %all-to-all-done.1 = bf16[128,16,384]{2,0,1:T(8,128)(2,1)} async-done(((bf16[128,16,384]{2,0,1:T(8,128)(2,1)}), bf16[128,16,384]{2,0,1:T(8,128)(2,1)}, u32[]{:S(2)}, u32[]{:S(2)}) %all-to-all-start.1) | async-done | bytes 1572896 | tf_op jit(solution)/shard_map/all_to_all | solution.py:194
  68.8 1.5 broadcast_in_dim.24
  70.3 3.8 all-to-all-start.2
  76.2 1.4 copy.74.qdoc_ref
  77.6 1.3 convert_reduce_fusion
  79.5 23.7 %all-to-all-done.2 = bf16[256,16,256]{2,0,1:T(8,128)(2,1)S(1)} async-done(((bf16[256,16,256]{2,0,1:T(8,128)(2,1)}), bf16[256,16,256]{2,0,1:T(8,128)(2,1)S(1)}, u32[]{:S(2)}, u32[]{:S(2)}) %all-to-all-start.2) | async-done | bytes 2097184 | tf_op jit(solution)/shard_map/all_to_all | solution.py:195
  103.3 1.3 copy-done.2
  104.6 73.4 %band_attention.1 = (bf16[2048,384]{1,0:T(8,128)(2,1)}, bf16[2048,384]{1,0:T(8,128)(2,1)}, f32[4096,256]{1,0:T(8,128)}) custom-call(s32[2048,1]{1,0:T(8,128)} %copy.74.qdoc_ref, s32[1,4096]{1,0:T(1,128)} %compare_select_fusion.kdoc_ref, bf16[2048,384]{1,0:T(8,128)(2,1)} %bitcast.76, bf16[2048,384]{1,0:T(8,128)(2,1)} %bitcast.8.go_ref, bf16[4096,256]{1,0:T(8,128)(2,1)} %bitcast.68), custom_call_target="tpu_custom_call" | custom-call | flops 21743271936 | bytes 12582912 | tf_op jit(solution)/shard_map/band_attention/pallas_call | solution.py:74
  178.0 2.4 convert_element_type.34
  180.4 31.4 %all_to_all.133 = bf16[16,256,256]{2,1,0:T(8,128)(2,1)S(1)} all-to-all(bf16[16,256,256]{2,1,0:T(8,128)(2,1)S(1)} %bitcast.64), channel_id=1, replica_groups=mesh['dp'=8,'ctx'=16] {'ctx'}, dimensions={0} | all-to-all | bytes 4194304 | tf_op jit(solution)/shard_map/all_to_all | solution.py:209
  212.3 1.0 copy.78
  213.3 3.7 all-to-all-start.3
  217.1 8.7 %copy.79 = bf16[1,256,12288]{1,2,0:T(8,128)(2,1)} copy(bf16[1,256,12288]{2,1,0:T(8,128)(2,1)} %param.8) | data formatting | bytes 12582912 | tf_op args[2]
  225.8 6.1 %copy.80 = bf16[8,256,4,4,96]{1,4,3,2,0:T(8,128)(2,1)} copy(bf16[8,256,4,4,96]{1,4,0,2,3:T(8,128)(2,1)} %bitcast.63) | data formatting | bytes 12582912 | tf_op jit(solution)/shard_map/transpose | solution.py:156
  231.9 5.2 %constant_dynamic-slice_fusion = (bf16[1,256,1536]{1,2,0:T(8,128)(2,1)}, bf16[1,256,1536]{1,2,0:T(8,128)(2,1)}, bf16[1,256,1536]{1,2,0:T(8,128)(2,1)}, bf16[1,25...) fusion(bf16[8,256,1536]{1,2,0:T(8,128)(2,1)} %bitcast.62, ...), kind=kLoop, calls=%fused_computation.8 | loop fusion | bytes 12582944 | tf_op jit(solution)/shard_map/jit(dynamic_index_in_dim)/dynamic_slice | solution.py:161
  237.1 1.3 copy.82
  238.4 1.2 copy.83
  239.6 1.9 collective-permute-start.1
  241.5 7.3 %all-to-all-start.4 = ((bf16[16,128,384]{2,1,0:T(8,128)(2,1)}), bf16[16,128,384]{2,1,0:T(8,128)(2,1)}, u32[]{:S(2)}, u32[]{:S(2)}) async-start(bf16[16,128,384]{2,1,0:T(8,128)(2,1)} %bitcast.72), calls=%async_computation.4 | async-start | bytes 3145728 | tf_op jit(solution)/shard_map/all_to_all | solution.py:207
  248.8 2.3 copy.84
  251.1 2.6 collective-permute-start.2
  253.7 2.4 copy.85
  256.1 1.2 collective-permute-start.3
  257.3 2.3 copy.86
  259.6 2.6 collective-permute-start.4
  262.2 2.3 copy.87
  264.5 1.3 copy.88
  265.8 1.0 collective-permute-start.5
  266.8 10.7 %collective-permute-start.6 = (bf16[256,1536]{1,0:T(8,128)(2,1)}, bf16[256,1536]{1,0:T(8,128)(2,1)}, u32[]{:S(2)}, u32[]{:S(2)}) collective-permute-start(bf16[256,1536]{1,0:T(8,128)(2,1)} %bitcast.82), channel_id=1, source_target_pairs={{0,112},{16,0},{32,16},{48,32},{64,48},{80,64},{96,80},{112,96},{1... | collective-permute-start | bytes 2359304 | tf_op jit(solution)/shard_map/ppermute | solution.py:163
  277.5 1.4 copy.81
  278.9 2.8 copy.92
  281.7 2.8 copy.93
  284.5 9.5 %collective-permute-done.2.refs_3_ = bf16[256,1536]{1,0:T(8,128)(2,1)S(1)} collective-permute-done((bf16[256,1536]{1,0:T(8,128)(2,1)}, bf16[256,1536]{1,0:T(8,128)(2,1)S(1)}, u32[]{:S(2)}, u32[]{:S(2)}) %collective-permute-start.2) | collective-permute-done | bytes 786464 | tf_op jit(solution)/shard_map/ppermute | solution.py:163
  293.9 3.6 collective-permute-done.3.refs_4_
  297.6 11.0 %collective-permute-done.4.refs_5_ = bf16[256,1536]{1,0:T(8,128)(2,1)} collective-permute-done((bf16[256,1536]{1,0:T(8,128)(2,1)}, bf16[256,1536]{1,0:T(8,128)(2,1)}, u32[]{:S(2)}, u32[]{:S(2)}) %collective-permute-start.4) | collective-permute-done | bytes 786464 | tf_op jit(solution)/shard_map/ppermute | solution.py:163
  308.6 2.4 collective-permute-done.5.refs_6_
  311.0 10.7 %collective-permute-done.6.refs_7_ = bf16[256,1536]{1,0:T(8,128)(2,1)} collective-permute-done((bf16[256,1536]{1,0:T(8,128)(2,1)}, bf16[256,1536]{1,0:T(8,128)(2,1)}, u32[]{:S(2)}, u32[]{:S(2)}) %collective-permute-start.6) | collective-permute-done | bytes 786464 | tf_op jit(solution)/shard_map/ppermute | solution.py:163
  321.7 10.8 %weight_product.1 = bf16[1536,1024]{1,0:T(8,128)(2,1)} custom-call(s32[1]{0:T(128)} %bitcast.22.me_ref, bf16[256,1536]{1,0:T(8,128)(2,1)S(1)} %bitcast.61, bf16[256,1536]{1,0:T(8,128)(2,1)S(1)} %collective-permute-done.refs_1_, bf16[256,1536]{1,0:T(8,128)(2,1)S(1)} %collective-permute-done.1.refs_2_, bf16[256,1536]{1,0:T(8,128)(2,1)S(1)} %collective-permute-done.2.refs_3_, ...), custom_call_target="tpu_custom_call" | custom-call | flops 6442450944 | bytes 13631488 | tf_op jit(solution)/shard_map/weight_product/pallas_call | solution.py:130
  332.6 40.4 %reduce-scatter.3.cloned.1.call-done = bf16[384,1024]{1,0:T(8,128)(2,1)} async-done(((bf16[1536,1024]{1,0:T(8,128)(2,1)}), bf16[384,1024]{1,0:T(8,128)(2,1)}) %reduce-scatter.3.cloned.1.call-update) | async-done | bytes 786448 | tf_op jit(solution)/shard_map/reduce_scatter | solution.py:173
  373.0 24.8 %reduce-scatter.5.cloned.1.call-done = bf16[96,1024]{1,0:T(8,128)(2,1)} async-done(((bf16[384,1024]{1,0:T(8,128)(2,1)}), bf16[96,1024]{1,0:T(8,128)(2,1)}) %reduce-scatter.5.cloned.1.call-update) | async-done | bytes 196624 | tf_op jit(solution)/shard_map/reduce_scatter | solution.py:174
  397.8 1.0 copy_bitcast_fusion
  398.7 13.2 %all_to_all.134 = f32[96,8,128]{2,0,1:T(8,128)S(1)} all-to-all(f32[96,8,128]{2,0,1:T(8,128)S(1)} %copy_bitcast_fusion), channel_id=1, replica_groups=mesh['dp'=8,'ctx'=16] {'dp'}, dimensions={1} | all-to-all | bytes 786432 | tf_op jit(solution)/shard_map/all_to_all | solution.py:175
  (40 shorter events, 4.1 us)
Async XLA Ops:
  10.4 7.3 %copy-start.3 = (bf16[1,128,6144]{2,1,0:T(8,128)(2,1)S(1)}, bf16[1,128,6144]{2,1,0:T(8,128)(2,1)}, u32[]{:S(2)}) copy-start(bf16[1,128,6144]{2,1,0:T(8,128)(2,1)} %param.9) | copy-start | bytes 4718596
  10.4 31.8 %all-to-all-start = ((bf16[128,16,384]{2,0,1:T(8,128)(2,1)}), bf16[128,16,384]{2,0,1:T(8,128)(2,1)S(1)}, u32[]{:S(2)}, u32[]{:S(2)}) async-start(bf16[128,16,384]{2,0,1:T(8,128)(2,1)} %copy.71), calls=%async_computation | async-start | bytes 3145728 | tf_op jit(solution)/shard_map/all_to_all | solution.py:193
  19.5 27.1 %copy-start.5 = (bf16[1,256,1024]{2,1,0:T(8,128)(2,1)S(1)}, bf16[1,256,1024]{2,1,0:T(8,128)(2,1)}, u32[]{:S(2)}) copy-start(bf16[1,256,1024]{2,1,0:T(8,128)(2,1)} %param.7) | copy-start | bytes 1572868
  42.2 4.8 %copy-start.4 = (bf16[128,16,384]{2,0,1:T(8,128)(2,1)}, bf16[128,16,384]{2,0,1:T(8,128)(2,1)S(1)}, u32[]{:S(2)}) copy-start(bf16[128,16,384]{2,0,1:T(8,128)(2,1)S(1)} %all-to-all-done) | copy-start | bytes 4718596
  42.2 26.6 %all-to-all-start.1 = ((bf16[128,16,384]{2,0,1:T(8,128)(2,1)}), bf16[128,16,384]{2,0,1:T(8,128)(2,1)}, u32[]{:S(2)}, u32[]{:S(2)}) async-start(bf16[128,16,384]{2,0,1:T(8,128)(2,1)} %copy.72), calls=%async_computation.1 | async-start | bytes 3145728 | tf_op jit(solution)/shard_map/all_to_all | solution.py:194
  70.3 3.9 copy-start.6
  70.3 32.9 %all-to-all-start.2 = ((bf16[256,16,256]{2,0,1:T(8,128)(2,1)}), bf16[256,16,256]{2,0,1:T(8,128)(2,1)S(1)}, u32[]{:S(2)}, u32[]{:S(2)}) async-start(bf16[256,16,256]{2,0,1:T(8,128)(2,1)} %bitcast.9), calls=%async_computation.2 | async-start | bytes 4194304 | tf_op jit(solution)/shard_map/all_to_all | solution.py:195
  74.2 210.3 %all-gather.2.cloned.1.call-start = ((), (), s32[]{:S(2)}) async-start(), calls=%async_computation.9 | async-start | bytes 4718592 | tf_op jit(solution)/shard_map/all_gather | solution.py:219
  103.3 1.3 copy-start.2
  213.3 28.2 %all-to-all-start.3 = ((bf16[16,128,384]{2,1,0:T(8,128)(2,1)}), bf16[16,128,384]{2,1,0:T(8,128)(2,1)S(1)}, u32[]{:S(2)}, u32[]{:S(2)}) async-start(bf16[16,128,384]{2,1,0:T(8,128)(2,1)} %bitcast.73), calls=%async_computation.3 | async-start | bytes 3145728 | tf_op jit(solution)/shard_map/all_to_all | solution.py:206
  238.4 27.4 %collective-permute-start = (bf16[256,1536]{1,0:T(8,128)(2,1)}, bf16[256,1536]{1,0:T(8,128)(2,1)S(1)}, u32[]{:S(2)}, u32[]{:S(2)}) collective-permute-start(bf16[256,1536]{1,0:T(8,128)(2,1)} %bitcast.83), channel_id=1, source_target_pairs={{0,16},{16,32},{32,48},{48,64},{64,80},{80,96},{96,112},{112,0},{1... | collective-permute-start | bytes 2359304 | tf_op jit(solution)/shard_map/ppermute | solution.py:163
  239.6 27.2 %collective-permute-start.1 = (bf16[256,1536]{1,0:T(8,128)(2,1)}, bf16[256,1536]{1,0:T(8,128)(2,1)S(1)}, u32[]{:S(2)}, u32[]{:S(2)}) collective-permute-start(bf16[256,1536]{1,0:T(8,128)(2,1)} %bitcast.80), channel_id=1, source_target_pairs={{0,32},{16,48},{32,64},{48,80},{64,96},{80,112},{96,0},{112,16},{1... | collective-permute-start | bytes 2359304 | tf_op jit(solution)/shard_map/ppermute | solution.py:163
  241.5 9.6 %copy-start = (bf16[16,128,384]{2,1,0:T(8,128)(2,1)}, bf16[16,128,384]{2,1,0:T(8,128)(2,1)S(1)}, u32[]{:S(2)}) copy-start(bf16[16,128,384]{2,1,0:T(8,128)(2,1)S(1)} %all-to-all-done.3) | copy-start | bytes 4718596
  241.5 40.2 %all-to-all-start.4 = ((bf16[16,128,384]{2,1,0:T(8,128)(2,1)}), bf16[16,128,384]{2,1,0:T(8,128)(2,1)}, u32[]{:S(2)}, u32[]{:S(2)}) async-start(bf16[16,128,384]{2,1,0:T(8,128)(2,1)} %bitcast.72), calls=%async_computation.4 | async-start | bytes 3145728 | tf_op jit(solution)/shard_map/all_to_all | solution.py:207
  248.8 124.2 %reduce-scatter.3.cloned.1.call-start = ((), (), s32[]{:S(2)}) async-start(), calls=%async_computation.10 | async-start | bytes 3932160 | tf_op jit(solution)/shard_map/reduce_scatter | solution.py:173
  251.1 42.9 %collective-permute-start.2 = (bf16[256,1536]{1,0:T(8,128)(2,1)}, bf16[256,1536]{1,0:T(8,128)(2,1)S(1)}, u32[]{:S(2)}, u32[]{:S(2)}) collective-permute-start(bf16[256,1536]{1,0:T(8,128)(2,1)} %bitcast.78), channel_id=1, source_target_pairs={{0,48},{16,64},{32,80},{48,96},{64,112},{80,0},{96,16},{112,32},{1... | collective-permute-start | bytes 2359304 | tf_op jit(solution)/shard_map/ppermute | solution.py:163
  253.7 10.8 %copy-start.1 = (bf16[1,256,1536]{1,2,0:T(8,128)(2,1)S(1)}, bf16[1,256,1536]{1,2,0:T(8,128)(2,1)}, u32[]{:S(2)}) copy-start(bf16[1,256,1536]{1,2,0:T(8,128)(2,1)} %get-tuple-element.24) | copy-start | bytes 2359300
  256.1 41.5 %collective-permute-start.3 = (bf16[256,1536]{1,0:T(8,128)(2,1)}, bf16[256,1536]{1,0:T(8,128)(2,1)}, u32[]{:S(2)}, u32[]{:S(2)}) collective-permute-start(bf16[256,1536]{1,0:T(8,128)(2,1)} %bitcast.79), channel_id=1, source_target_pairs={{0,64},{16,80},{32,96},{48,112},{64,0},{80,16},{96,32},{112,48},{1... | collective-permute-start | bytes 2359304 | tf_op jit(solution)/shard_map/ppermute | solution.py:163
  259.6 49.0 %collective-permute-start.4 = (bf16[256,1536]{1,0:T(8,128)(2,1)}, bf16[256,1536]{1,0:T(8,128)(2,1)}, u32[]{:S(2)}, u32[]{:S(2)}) collective-permute-start(bf16[256,1536]{1,0:T(8,128)(2,1)} %bitcast.81), channel_id=1, source_target_pairs={{0,80},{16,96},{32,112},{48,0},{64,16},{80,32},{96,48},{112,64},{1... | collective-permute-start | bytes 2359304 | tf_op jit(solution)/shard_map/ppermute | solution.py:163
  265.8 45.2 %collective-permute-start.5 = (bf16[256,1536]{1,0:T(8,128)(2,1)}, bf16[256,1536]{1,0:T(8,128)(2,1)}, u32[]{:S(2)}, u32[]{:S(2)}) collective-permute-start(bf16[256,1536]{1,0:T(8,128)(2,1)} %bitcast.84), channel_id=1, source_target_pairs={{0,96},{16,112},{32,0},{48,16},{64,32},{80,48},{96,64},{112,80},{1... | collective-permute-start | bytes 2359304 | tf_op jit(solution)/shard_map/ppermute | solution.py:163
  266.8 54.9 %collective-permute-start.6 = (bf16[256,1536]{1,0:T(8,128)(2,1)}, bf16[256,1536]{1,0:T(8,128)(2,1)}, u32[]{:S(2)}, u32[]{:S(2)}) collective-permute-start(bf16[256,1536]{1,0:T(8,128)(2,1)} %bitcast.82), channel_id=1, source_target_pairs={{0,112},{16,0},{32,16},{48,32},{64,48},{80,64},{96,80},{112,96},{1... | collective-permute-start | bytes 2359304 | tf_op jit(solution)/shard_map/ppermute | solution.py:163
  332.5 65.2 %reduce-scatter.5.cloned.1.call-start = ((), (), s32[]{:S(2)}) async-start(), calls=%async_computation.11 | async-start | bytes 983040 | tf_op jit(solution)/shard_map/reduce_scatter | solution.py:174
Sparse Core Ops, SparseCore 0:
  213.4 30.7 all-gather.1
  332.6 40.2 reduce-scatter.2
  375.4 22.3 reduce-scatter.4

commit v6 on v5

--- a/solution.py
+++ b/solution.py
@@ -143,6 +143,31 @@
     )(jnp.reshape(me, (1,)).astype(jnp.int32), *pieces, grad_all)
 
 
+def ctx_groups():
+    ctx = lax.axis_size("ctx")
+    across = ctx // CTX_ROWS
+    along_x = [[y * across + x for x in range(across)] for y in range(CTX_ROWS)]
+    along_y = [[y * across + x for y in range(CTX_ROWS)] for x in range(across)]
+    return across, along_x, along_y
+
+
+def gather_key_gradient(grad_head):
+    keys, width = grad_head.shape
+    across, along_x, along_y = ctx_groups()
+    block = keys // (CTX_ROWS * across)
+    ordered = (
+        grad_head.astype(jnp.bfloat16)
+        .reshape(CTX_ROWS, across, block, width)
+        .transpose(1, 0, 2, 3)
+        .reshape(keys, width)
+    )
+    summed = lax.psum_scatter(ordered, "ctx", scatter_dimension=0, axis_index_groups=along_x, tiled=True)
+    owners = lax.all_to_all(
+        summed.reshape(CTX_ROWS, block, width), "ctx", 0, 0, axis_index_groups=along_y, tiled=True
+    )
+    return owners.transpose(1, 0, 2).reshape(block, CTX_ROWS * width)
+
+
 def send_hidden(hidden_rows):
     dp = lax.axis_size("dp")
     ctx = lax.axis_size("ctx")
@@ -166,10 +191,7 @@
 
 def weight_gradient(me, received, grad_all):
     partial = stacked_weight_product(me, received, grad_all)
-    ctx = lax.axis_size("ctx")
-    across = ctx // CTX_ROWS
-    along_x = [[y * across + x for x in range(across)] for y in range(CTX_ROWS)]
-    along_y = [[y * across + x for y in range(CTX_ROWS)] for x in range(across)]
+    _, along_x, along_y = ctx_groups()
     reduced = lax.psum_scatter(partial, "ctx", scatter_dimension=0, axis_index_groups=along_x, tiled=True)
     reduced = lax.psum_scatter(reduced, "ctx", scatter_dimension=0, axis_index_groups=along_y, tiled=True)
     return lax.all_to_all(reduced.astype(jnp.float32), "dp", split_axis=1, concat_axis=0, tiled=True)
@@ -182,7 +204,6 @@
     hidden_rows = hidden[0]
     bounds = jnp.cumsum(doc_lengths[0], dtype=jnp.int32)
     offset = slab_offsets[0]
-    key_value_width = 2 * KEY_VALUE_HEADS * HEAD_FEATURES
     repeat_heads = lax.axis_size("ctx") // KEY_VALUE_HEADS
     key_total_count = key_matrix_rows.shape[0]
     copies = jnp.broadcast_to(
@@ -206,16 +227,7 @@
         lax.all_to_all(attended_heads, "ctx", split_axis=0, concat_axis=1, tiled=True),
         lax.all_to_all(grad_query_heads, "ctx", split_axis=0, concat_axis=1, tiled=True),
     )
-    partial_sums = lax.all_to_all(
-        grad_head.astype(jnp.bfloat16), "ctx", split_axis=0, concat_axis=1, tiled=True
-    )
-    grad_keys = jnp.sum(
-        partial_sums.reshape(
-            partial_sums.shape[0], KEY_VALUE_HEADS, repeat_heads, 2 * HEAD_FEATURES
-        ).astype(jnp.float32),
-        axis=2,
-    ).reshape(partial_sums.shape[0], key_value_width)
-    grad_low = grad_keys.astype(jnp.bfloat16)
+    grad_low = gather_key_gradient(grad_head)
     grad_all = lax.all_gather(grad_low, "dp", axis=0, tiled=False)
     attended, grad_query, grad_all = lax.optimization_barrier((attended, grad_query, grad_all))
     grad_weight = weight_gradient(me, received, grad_all)

time: 421 us -> 432 us (1.026)
  waiting for transfers between devices: 171 us -> 199 us
  blocking collectives: 44.5 us -> 26.9 us
    reduce_scatter x0 -> x1, waiting for transfers between devices: none -> 28.1 us  [gather_key_gradient(): lax.psum_scatter(ordered, 'ctx', scatter_dimension=0, axis_index_groups=a...]
    all_to_all x1, blocking collectives: 31.4 us -> 13.7 us  [gather_key_gradient(): lax.all_to_all(summed.reshape(CTX_ROWS, block, width), 'ctx', 0, 0, axis_...]
  transfers between devices with their start and end apart: 15 -> 16, of which waited for: 10 -> 11; matrix products, arithmetic and copies ran while one was open for 11% -> 11% of each run, Pallas kernels for 0% -> 0%
where the time goes in v6:
time: 432 us; the launch traced here: 430 us
  waiting for transfers between devices  199 us (46%)
  Pallas kernels  84.2 us (19%)
  local copies, waits for them, and re-layouts  53.3 us (12%)
  starting transfers between devices  45.7 us (11%)
  blocking collectives  26.9 us (6%)
  between operations  14.7 us (3%)
  other arithmetic  6.3 us (1%)
    pallas_call x1, Pallas kernels, head_attention(): pl.pallas_call(kernel, grid=grid, in_specs=[pl.BlockSpec((bq, 1), lambda...  73.4 us
    reduce_scatter x1, waiting for transfers between devices, weight_gradient(): lax.psum_scatter(partial, 'ctx', scatter_dimension=0, axis_index_groups=a...  40.5 us
    ppermute x7, waiting for transfers between devices, send_hidden(): received.append(lax.ppermute(outgoing, 'dp', pairs))  37.4 us
    reduce_scatter x1, waiting for transfers between devices, gather_key_gradient(): lax.psum_scatter(ordered, 'ctx', scatter_dimension=0, axis_index_groups=a...  28.1 us
    reduce_scatter x1, waiting for transfers between devices, weight_gradient(): lax.psum_scatter(reduced, 'ctx', scatter_dimension=0, axis_index_groups=a...  24.7 us
    all_to_all x1, waiting for transfers between devices, local_body(): lax.all_to_all(copies, 'ctx', split_axis=1, concat_axis=0, tiled=True)  23.8 us
    all_to_all x1, waiting for transfers between devices, local_body(): lax.all_to_all(query_matrix_rows, 'ctx', split_axis=1, concat_axis=0, til...  22.7 us
    all_to_all x1, waiting for transfers between devices, local_body(): lax.all_to_all(upstream_gradient, 'ctx', split_axis=1, concat_axis=0, til...  21.7 us
  transfers between devices with their start and end apart: 16, of which 11 were waited for; matrix products, arithmetic and copies ran while one was open for 11% of the time, Pallas kernels for 0%

profile of v6, /device:TPU:0, one launch (start us, length us, event | category | flops | bytes accessed | tf_op | source)
XLA Modules:
  0.0 430.0 jit_solution(10420950099629301102)
XLA Ops:
  7.2 1.7 copy.99
  8.9 1.5 copy.75
  10.4 7.3 %all-to-all-start = ((bf16[128,16,384]{2,0,1:T(8,128)(2,1)}), bf16[128,16,384]{2,0,1:T(8,128)(2,1)S(1)}, u32[]{:S(2)}, u32[]{:S(2)}) async-start(bf16[128,16,384]{2,0,1:T(8,128)(2,1)} %copy.75), calls=%async_computation | async-start | bytes 3145728 | tf_op jit(solution)/shard_map/all_to_all | solution.py:214
  18.0 1.5 copy.76
  19.5 22.7 %all-to-all-done = bf16[128,16,384]{2,0,1:T(8,128)(2,1)S(1)} async-done(((bf16[128,16,384]{2,0,1:T(8,128)(2,1)}), bf16[128,16,384]{2,0,1:T(8,128)(2,1)S(1)}, u32[]{:S(2)}, u32[]{:S(2)}) %all-to-all-start) | async-done | bytes 1572896 | tf_op jit(solution)/shard_map/all_to_all | solution.py:214
  42.2 4.4 %all-to-all-start.1 = ((bf16[128,16,384]{2,0,1:T(8,128)(2,1)}), bf16[128,16,384]{2,0,1:T(8,128)(2,1)}, u32[]{:S(2)}, u32[]{:S(2)}) async-start(bf16[128,16,384]{2,0,1:T(8,128)(2,1)} %copy.76), calls=%async_computation.1 | async-start | bytes 3145728 | tf_op jit(solution)/shard_map/all_to_all | solution.py:215
  47.1 21.7 %all-to-all-done.1 = bf16[128,16,384]{2,0,1:T(8,128)(2,1)} async-done(((bf16[128,16,384]{2,0,1:T(8,128)(2,1)}), bf16[128,16,384]{2,0,1:T(8,128)(2,1)}, u32[]{:S(2)}, u32[]{:S(2)}) %all-to-all-start.1) | async-done | bytes 1572896 | tf_op jit(solution)/shard_map/all_to_all | solution.py:215
  68.8 1.5 broadcast_in_dim.23
  70.4 3.8 all-to-all-start.2
  76.2 1.4 copy.78.qdoc_ref
  77.6 1.3 convert_reduce_fusion
  79.5 23.8 %all-to-all-done.2 = bf16[256,16,256]{2,0,1:T(8,128)(2,1)S(1)} async-done(((bf16[256,16,256]{2,0,1:T(8,128)(2,1)}), bf16[256,16,256]{2,0,1:T(8,128)(2,1)S(1)}, u32[]{:S(2)}, u32[]{:S(2)}) %all-to-all-start.2) | async-done | bytes 2097184 | tf_op jit(solution)/shard_map/all_to_all | solution.py:216
  103.3 1.3 copy-done.2
  104.6 73.4 %band_attention.1 = (bf16[2048,384]{1,0:T(8,128)(2,1)}, bf16[2048,384]{1,0:T(8,128)(2,1)}, f32[4096,256]{1,0:T(8,128)}) custom-call(s32[2048,1]{1,0:T(8,128)} %copy.78.qdoc_ref, s32[1,4096]{1,0:T(1,128)} %compare_select_fusion.kdoc_ref, bf16[2048,384]{1,0:T(8,128)(2,1)} %bitcast.79, bf16[2048,384]{1,0:T(8,128)(2,1)} %bitcast.8.go_ref, bf16[4096,256]{1,0:T(8,128)(2,1)} %bitcast.70), custom_call_target="tpu_custom_call" | custom-call | flops 21743271936 | bytes 12582912 | tf_op jit(solution)/shard_map/band_attention/pallas_call | solution.py:74
  178.0 2.4 convert_element_type.12
  180.4 1.5 copy.81
  182.0 28.1 %reduce-scatter.4.cloned.1.call-done = bf16[1024,256]{1,0:T(8,128)(2,1)} async-done(((bf16[4096,256]{1,0:T(8,128)(2,1)}), bf16[1024,256]{1,0:T(8,128)(2,1)}) %reduce-scatter.4.cloned.1.call-update) | async-done | bytes 524304 | tf_op jit(solution)/shard_map/reduce_scatter | solution.py:164
  210.1 13.7 %all_to_all.125 = bf16[4,256,256]{2,1,0:T(8,128)(2,1)S(1)} all-to-all(bf16[4,256,256]{2,1,0:T(8,128)(2,1)} %bitcast.88), channel_id=1, replica_groups={{0,4,8,12},{1,5,9,13},{2,6,10,14},{3,7,11,15},{16,20,24,28},{17,21,25,2..., dimensions={0} | all-to-all | bytes 1048576 | tf_op jit(solution)/shard_map/all_to_all | solution.py:165
  225.1 3.7 all-to-all-start.3
  228.9 8.7 %copy.84 = bf16[1,256,12288]{1,2,0:T(8,128)(2,1)} copy(bf16[1,256,12288]{2,1,0:T(8,128)(2,1)} %param.8) | data formatting | bytes 12582912 | tf_op args[2]
  237.6 6.1 %copy.85 = bf16[8,256,4,4,96]{1,4,3,2,0:T(8,128)(2,1)} copy(bf16[8,256,4,4,96]{1,4,0,2,3:T(8,128)(2,1)} %bitcast.64) | data formatting | bytes 12582912 | tf_op jit(solution)/shard_map/transpose | solution.py:181
  243.7 5.2 %constant_dynamic-slice_fusion = (bf16[1,256,1536]{1,2,0:T(8,128)(2,1)}, bf16[1,256,1536]{1,2,0:T(8,128)(2,1)}, bf16[1,256,1536]{1,2,0:T(8,128)(2,1)}, bf16[1,25...) fusion(bf16[8,256,1536]{1,2,0:T(8,128)(2,1)} %bitcast.63, ...), kind=kLoop, calls=%fused_computation.7 | loop fusion | bytes 12582944 | tf_op jit(solution)/shard_map/jit(dynamic_index_in_dim)/dynamic_slice | solution.py:186
  248.9 1.2 copy.87
  250.1 1.2 copy.88
  251.3 1.7 collective-permute-start.1
  253.0 7.1 %all-to-all-start.4 = ((bf16[16,128,384]{2,1,0:T(8,128)(2,1)}), bf16[16,128,384]{2,1,0:T(8,128)(2,1)}, u32[]{:S(2)}, u32[]{:S(2)}) async-start(bf16[16,128,384]{2,1,0:T(8,128)(2,1)} %bitcast.75), calls=%async_computation.4 | async-start | bytes 3145728 | tf_op jit(solution)/shard_map/all_to_all | solution.py:228
  260.1 2.3 copy.89
  262.4 1.9 collective-permute-start.2
  264.4 2.4 copy.90
  266.7 1.9 collective-permute-start.3
  268.7 2.3 copy.91
  271.0 1.9 collective-permute-start.4
  272.9 2.3 copy.92
  275.2 1.2 copy.93
  276.5 1.3 collective-permute-start.5
  277.8 10.3 %collective-permute-start.6 = (bf16[256,1536]{1,0:T(8,128)(2,1)}, bf16[256,1536]{1,0:T(8,128)(2,1)}, u32[]{:S(2)}, u32[]{:S(2)}) collective-permute-start(bf16[256,1536]{1,0:T(8,128)(2,1)} %bitcast.85), channel_id=1, source_target_pairs={{0,112},{16,0},{32,16},{48,32},{64,48},{80,64},{96,80},{112,96},{1... | collective-permute-start | bytes 2359304 | tf_op jit(solution)/shard_map/ppermute | solution.py:188
  288.1 1.4 copy.86
  289.5 2.8 copy.97
  292.3 2.8 copy.98
  295.1 9.5 %collective-permute-done.2.refs_3_ = bf16[256,1536]{1,0:T(8,128)(2,1)S(1)} collective-permute-done((bf16[256,1536]{1,0:T(8,128)(2,1)}, bf16[256,1536]{1,0:T(8,128)(2,1)S(1)}, u32[]{:S(2)}, u32[]{:S(2)}) %collective-permute-start.2) | collective-permute-done | bytes 786464 | tf_op jit(solution)/shard_map/ppermute | solution.py:188
  304.6 3.6 collective-permute-done.3.refs_4_
  308.2 11.8 %collective-permute-done.4.refs_5_ = bf16[256,1536]{1,0:T(8,128)(2,1)} collective-permute-done((bf16[256,1536]{1,0:T(8,128)(2,1)}, bf16[256,1536]{1,0:T(8,128)(2,1)}, u32[]{:S(2)}, u32[]{:S(2)}) %collective-permute-start.4) | collective-permute-done | bytes 786464 | tf_op jit(solution)/shard_map/ppermute | solution.py:188
  320.0 2.0 collective-permute-done.5.refs_6_
  322.0 10.5 %collective-permute-done.6.refs_7_ = bf16[256,1536]{1,0:T(8,128)(2,1)} collective-permute-done((bf16[256,1536]{1,0:T(8,128)(2,1)}, bf16[256,1536]{1,0:T(8,128)(2,1)}, u32[]{:S(2)}, u32[]{:S(2)}) %collective-permute-start.6) | collective-permute-done | bytes 786464 | tf_op jit(solution)/shard_map/ppermute | solution.py:188
  332.5 10.8 %weight_product.1 = bf16[1536,1024]{1,0:T(8,128)(2,1)} custom-call(s32[1]{0:T(128)} %bitcast.24.me_ref, bf16[256,1536]{1,0:T(8,128)(2,1)S(1)} %bitcast.62, bf16[256,1536]{1,0:T(8,128)(2,1)S(1)} %collective-permute-done.refs_1_, bf16[256,1536]{1,0:T(8,128)(2,1)S(1)} %collective-permute-done.1.refs_2_, bf16[256,1536]{1,0:T(8,128)(2,1)S(1)} %collective-permute-done.2.refs_3_, ...), custom_call_target="tpu_custom_call" | custom-call | flops 6442450944 | bytes 13631488 | tf_op jit(solution)/shard_map/weight_product/pallas_call | solution.py:130
  343.4 40.5 %reduce-scatter.6.cloned.1.call-done = bf16[384,1024]{1,0:T(8,128)(2,1)} async-done(((bf16[1536,1024]{1,0:T(8,128)(2,1)}), bf16[384,1024]{1,0:T(8,128)(2,1)}) %reduce-scatter.6.cloned.1.call-update) | async-done | bytes 786448 | tf_op jit(solution)/shard_map/reduce_scatter | solution.py:195
  384.0 24.7 %reduce-scatter.8.cloned.1.call-done = bf16[96,1024]{1,0:T(8,128)(2,1)} async-done(((bf16[384,1024]{1,0:T(8,128)(2,1)}), bf16[96,1024]{1,0:T(8,128)(2,1)}) %reduce-scatter.8.cloned.1.call-update) | async-done | bytes 196624 | tf_op jit(solution)/shard_map/reduce_scatter | solution.py:196
  409.6 13.2 %all_to_all.126 = f32[96,8,128]{2,0,1:T(8,128)S(1)} all-to-all(f32[96,8,128]{2,0,1:T(8,128)S(1)} %copy_bitcast_fusion), channel_id=1, replica_groups=mesh['dp'=8,'ctx'=16] {'dp'}, dimensions={1} | all-to-all | bytes 786432 | tf_op jit(solution)/shard_map/all_to_all | solution.py:197
  (43 shorter events, 5.8 us)
Async XLA Ops:
  10.4 7.3 %copy-start.3 = (bf16[1,128,6144]{2,1,0:T(8,128)(2,1)S(1)}, bf16[1,128,6144]{2,1,0:T(8,128)(2,1)}, u32[]{:S(2)}) copy-start(bf16[1,128,6144]{2,1,0:T(8,128)(2,1)} %param.9) | copy-start | bytes 4718596
  10.4 31.8 %all-to-all-start = ((bf16[128,16,384]{2,0,1:T(8,128)(2,1)}), bf16[128,16,384]{2,0,1:T(8,128)(2,1)S(1)}, u32[]{:S(2)}, u32[]{:S(2)}) async-start(bf16[128,16,384]{2,0,1:T(8,128)(2,1)} %copy.75), calls=%async_computation | async-start | bytes 3145728 | tf_op jit(solution)/shard_map/all_to_all | solution.py:214
  19.5 27.1 %copy-start.5 = (bf16[1,256,1024]{2,1,0:T(8,128)(2,1)S(1)}, bf16[1,256,1024]{2,1,0:T(8,128)(2,1)}, u32[]{:S(2)}) copy-start(bf16[1,256,1024]{2,1,0:T(8,128)(2,1)} %param.7) | copy-start | bytes 1572868
  42.2 4.8 %copy-start.4 = (bf16[128,16,384]{2,0,1:T(8,128)(2,1)}, bf16[128,16,384]{2,0,1:T(8,128)(2,1)S(1)}, u32[]{:S(2)}) copy-start(bf16[128,16,384]{2,0,1:T(8,128)(2,1)S(1)} %all-to-all-done) | copy-start | bytes 4718596
  42.2 26.6 %all-to-all-start.1 = ((bf16[128,16,384]{2,0,1:T(8,128)(2,1)}), bf16[128,16,384]{2,0,1:T(8,128)(2,1)}, u32[]{:S(2)}, u32[]{:S(2)}) async-start(bf16[128,16,384]{2,0,1:T(8,128)(2,1)} %copy.76), calls=%async_computation.1 | async-start | bytes 3145728 | tf_op jit(solution)/shard_map/all_to_all | solution.py:215
  70.3 3.9 copy-start.6
  70.4 32.9 %all-to-all-start.2 = ((bf16[256,16,256]{2,0,1:T(8,128)(2,1)}), bf16[256,16,256]{2,0,1:T(8,128)(2,1)S(1)}, u32[]{:S(2)}, u32[]{:S(2)}) async-start(bf16[256,16,256]{2,0,1:T(8,128)(2,1)} %bitcast.9), calls=%async_computation.2 | async-start | bytes 4194304 | tf_op jit(solution)/shard_map/all_to_all | solution.py:216
  74.2 135.9 %reduce-scatter.4.cloned.1.call-start = ((), (), s32[]{:S(2)}) async-start(), calls=%async_computation.10 | async-start | bytes 2621440 | tf_op jit(solution)/shard_map/reduce_scatter | solution.py:164
  103.3 1.3 copy-start.2
  181.9 113.2 %all-gather.2.cloned.1.call-start = ((), (), s32[]{:S(2)}) async-start(), calls=%async_computation.11 | async-start | bytes 4718592 | tf_op jit(solution)/shard_map/all_gather | solution.py:231
  225.1 27.9 %all-to-all-start.3 = ((bf16[16,128,384]{2,1,0:T(8,128)(2,1)}), bf16[16,128,384]{2,1,0:T(8,128)(2,1)S(1)}, u32[]{:S(2)}, u32[]{:S(2)}) async-start(bf16[16,128,384]{2,1,0:T(8,128)(2,1)} %bitcast.76), calls=%async_computation.3 | async-start | bytes 3145728 | tf_op jit(solution)/shard_map/all_to_all | solution.py:227
  250.1 26.4 %collective-permute-start = (bf16[256,1536]{1,0:T(8,128)(2,1)}, bf16[256,1536]{1,0:T(8,128)(2,1)S(1)}, u32[]{:S(2)}, u32[]{:S(2)}) collective-permute-start(bf16[256,1536]{1,0:T(8,128)(2,1)} %bitcast.86), channel_id=1, source_target_pairs={{0,16},{16,32},{32,48},{48,64},{64,80},{80,96},{96,112},{112,0},{1... | collective-permute-start | bytes 2359304 | tf_op jit(solution)/shard_map/ppermute | solution.py:188
  251.3 26.5 %collective-permute-start.1 = (bf16[256,1536]{1,0:T(8,128)(2,1)}, bf16[256,1536]{1,0:T(8,128)(2,1)S(1)}, u32[]{:S(2)}, u32[]{:S(2)}) collective-permute-start(bf16[256,1536]{1,0:T(8,128)(2,1)} %bitcast.83), channel_id=1, source_target_pairs={{0,32},{16,48},{32,64},{48,80},{64,96},{80,112},{96,0},{112,16},{1... | collective-permute-start | bytes 2359304 | tf_op jit(solution)/shard_map/ppermute | solution.py:188
  253.0 9.5 %copy-start = (bf16[16,128,384]{2,1,0:T(8,128)(2,1)}, bf16[16,128,384]{2,1,0:T(8,128)(2,1)S(1)}, u32[]{:S(2)}) copy-start(bf16[16,128,384]{2,1,0:T(8,128)(2,1)S(1)} %all-to-all-done.3) | copy-start | bytes 4718596
  253.0 39.4 %all-to-all-start.4 = ((bf16[16,128,384]{2,1,0:T(8,128)(2,1)}), bf16[16,128,384]{2,1,0:T(8,128)(2,1)}, u32[]{:S(2)}, u32[]{:S(2)}) async-start(bf16[16,128,384]{2,1,0:T(8,128)(2,1)} %bitcast.75), calls=%async_computation.4 | async-start | bytes 3145728 | tf_op jit(solution)/shard_map/all_to_all | solution.py:228
  260.1 123.8 %reduce-scatter.6.cloned.1.call-start = ((), (), s32[]{:S(2)}) async-start(), calls=%async_computation.12 | async-start | bytes 3932160 | tf_op jit(solution)/shard_map/reduce_scatter | solution.py:195
  262.4 42.2 %collective-permute-start.2 = (bf16[256,1536]{1,0:T(8,128)(2,1)}, bf16[256,1536]{1,0:T(8,128)(2,1)S(1)}, u32[]{:S(2)}, u32[]{:S(2)}) collective-permute-start(bf16[256,1536]{1,0:T(8,128)(2,1)} %bitcast.81), channel_id=1, source_target_pairs={{0,48},{16,64},{32,80},{48,96},{64,112},{80,0},{96,16},{112,32},{1... | collective-permute-start | bytes 2359304 | tf_op jit(solution)/shard_map/ppermute | solution.py:188
  264.4 10.8 %copy-start.1 = (bf16[1,256,1536]{1,2,0:T(8,128)(2,1)S(1)}, bf16[1,256,1536]{1,2,0:T(8,128)(2,1)}, u32[]{:S(2)}) copy-start(bf16[1,256,1536]{1,2,0:T(8,128)(2,1)} %get-tuple-element.24) | copy-start | bytes 2359300
  266.7 41.5 %collective-permute-start.3 = (bf16[256,1536]{1,0:T(8,128)(2,1)}, bf16[256,1536]{1,0:T(8,128)(2,1)}, u32[]{:S(2)}, u32[]{:S(2)}) collective-permute-start(bf16[256,1536]{1,0:T(8,128)(2,1)} %bitcast.82), channel_id=1, source_target_pairs={{0,64},{16,80},{32,96},{48,112},{64,0},{80,16},{96,32},{112,48},{1... | collective-permute-start | bytes 2359304 | tf_op jit(solution)/shard_map/ppermute | solution.py:188
  271.0 49.1 %collective-permute-start.4 = (bf16[256,1536]{1,0:T(8,128)(2,1)}, bf16[256,1536]{1,0:T(8,128)(2,1)}, u32[]{:S(2)}, u32[]{:S(2)}) collective-permute-start(bf16[256,1536]{1,0:T(8,128)(2,1)} %bitcast.84), channel_id=1, source_target_pairs={{0,80},{16,96},{32,112},{48,0},{64,16},{80,32},{96,48},{112,64},{1... | collective-permute-start | bytes 2359304 | tf_op jit(solution)/shard_map/ppermute | solution.py:188
  276.5 45.6 %collective-permute-start.5 = (bf16[256,1536]{1,0:T(8,128)(2,1)}, bf16[256,1536]{1,0:T(8,128)(2,1)}, u32[]{:S(2)}, u32[]{:S(2)}) collective-permute-start(bf16[256,1536]{1,0:T(8,128)(2,1)} %bitcast.87), channel_id=1, source_target_pairs={{0,96},{16,112},{32,0},{48,16},{64,32},{80,48},{96,64},{112,80},{1... | collective-permute-start | bytes 2359304 | tf_op jit(solution)/shard_map/ppermute | solution.py:188
  277.8 54.7 %collective-permute-start.6 = (bf16[256,1536]{1,0:T(8,128)(2,1)}, bf16[256,1536]{1,0:T(8,128)(2,1)}, u32[]{:S(2)}, u32[]{:S(2)}) collective-permute-start(bf16[256,1536]{1,0:T(8,128)(2,1)} %bitcast.85), channel_id=1, source_target_pairs={{0,112},{16,0},{32,16},{48,32},{64,48},{80,64},{96,80},{112,96},{1... | collective-permute-start | bytes 2359304 | tf_op jit(solution)/shard_map/ppermute | solution.py:188
  343.4 65.3 %reduce-scatter.8.cloned.1.call-start = ((), (), s32[]{:S(2)}) async-start(), calls=%async_computation.13 | async-start | bytes 983040 | tf_op jit(solution)/shard_map/reduce_scatter | solution.py:196
Sparse Core Ops, SparseCore 0:
  182.0 28.0 reduce-scatter.3
  225.2 30.1 all-gather.1
  343.5 40.4 reduce-scatter.5
  386.2 22.3 reduce-scatter.7

commit v7 on v5

--- a/solution.py
+++ b/solution.py
@@ -55,10 +55,10 @@
     deltas = jnp.sum(go.astype(f32) * att.astype(f32), axis=1, keepdims=True)
     grad_scores = (weights * (grad_probs - deltas) * factor).astype(bf16)
     dq_ref[...] = jnp.dot(grad_scores, k, preferred_element_type=f32).astype(bf16)
-    dk = lax.dot_general(grad_scores, q, tn, preferred_element_type=f32)
-    dv = lax.dot_general(weights_low, go, tn, preferred_element_type=f32)
-    dkv_ref[pl.ds(start, span), 0:HEAD_FEATURES] += dk
-    dkv_ref[pl.ds(start, span), HEAD_FEATURES : 2 * HEAD_FEATURES] += dv
+    dk = lax.dot_general(q, grad_scores, tn, preferred_element_type=f32)
+    dv = lax.dot_general(go, weights_low, tn, preferred_element_type=f32)
+    dkv_ref[0:HEAD_FEATURES, pl.ds(start, span)] += dk
+    dkv_ref[HEAD_FEATURES : 2 * HEAD_FEATURES, pl.ds(start, span)] += dv
 
 
 def head_attention(head_queries, head_upstream, head_keys, q_doc, k_doc):
@@ -84,12 +84,12 @@
         out_specs=[
             pl.BlockSpec((bq, HEAD_FEATURES), lambda i, h: (i, h)),
             pl.BlockSpec((bq, HEAD_FEATURES), lambda i, h: (i, h)),
-            pl.BlockSpec((keys, 2 * HEAD_FEATURES), lambda i, h: (0, 0)),
+            pl.BlockSpec((2 * HEAD_FEATURES, keys), lambda i, h: (0, 0)),
         ],
         out_shape=[
             jax.ShapeDtypeStruct(head_queries.shape, jnp.bfloat16),
             jax.ShapeDtypeStruct(head_queries.shape, jnp.bfloat16),
-            jax.ShapeDtypeStruct((keys, 2 * HEAD_FEATURES), jnp.float32),
+            jax.ShapeDtypeStruct((2 * HEAD_FEATURES, keys), jnp.float32),
         ],
         compiler_params=pltpu.CompilerParams(
             dimension_semantics=("arbitrary", "arbitrary"), vmem_limit_bytes=60 * 1024 * 1024
@@ -207,7 +207,7 @@
         lax.all_to_all(grad_query_heads, "ctx", split_axis=0, concat_axis=1, tiled=True),
     )
     partial_sums = lax.all_to_all(
-        grad_head.astype(jnp.bfloat16), "ctx", split_axis=0, concat_axis=1, tiled=True
+        grad_head.T.astype(jnp.bfloat16), "ctx", split_axis=0, concat_axis=1, tiled=True
     )
     grad_keys = jnp.sum(
         partial_sums.reshape(

time: 421 us -> 413 us (0.981)
  Pallas kernels: 84.2 us -> 76.5 us
    pallas_call x1, Pallas kernels: 73.4 us -> 65.7 us  [head_attention(): pl.pallas_call(kernel, grid=grid, in_specs=[pl.BlockSpec((bq, 1), lambda...]
where the time goes in v7:
time: 413 us; the launch traced here: 412 us
  waiting for transfers between devices  171 us (41%)
  Pallas kernels  76.5 us (19%)
  local copies, waits for them, and re-layouts  51.9 us (13%)
  starting transfers between devices  46.8 us (11%)
  blocking collectives  44.5 us (11%)
  between operations  14.7 us (4%)
  other arithmetic  6.68 us (2%)
    pallas_call x1, Pallas kernels, head_attention(): pl.pallas_call(kernel, grid=grid, in_specs=[pl.BlockSpec((bq, 1), lambda...  65.7 us
    reduce_scatter x1, waiting for transfers between devices, weight_gradient(): lax.psum_scatter(partial, 'ctx', scatter_dimension=0, axis_index_groups=a...  40.4 us
    ppermute x7, waiting for transfers between devices, send_hidden(): received.append(lax.ppermute(outgoing, 'dp', pairs))  37.2 us
    all_to_all x1, blocking collectives, local_body(): lax.all_to_all(grad_head.T.astype(jnp.bfloat16), 'ctx', split_axis=0, con...  31.3 us
    reduce_scatter x1, waiting for transfers between devices, weight_gradient(): lax.psum_scatter(reduced, 'ctx', scatter_dimension=0, axis_index_groups=a...  24.8 us
    all_to_all x1, waiting for transfers between devices, local_body(): lax.all_to_all(copies, 'ctx', split_axis=1, concat_axis=0, tiled=True)  23.7 us
    all_to_all x1, waiting for transfers between devices, local_body(): lax.all_to_all(query_matrix_rows, 'ctx', split_axis=1, concat_axis=0, til...  22.7 us
    all_to_all x1, waiting for transfers between devices, local_body(): lax.all_to_all(upstream_gradient, 'ctx', split_axis=1, concat_axis=0, til...  21.7 us
  transfers between devices with their start and end apart: 15, of which 10 were waited for; matrix products, arithmetic and copies ran while one was open for 11% of the time, Pallas kernels for 0%

profile of v7, /device:TPU:0, one launch (start us, length us, event | category | flops | bytes accessed | tf_op | source)
XLA Modules:
  0.0 411.6 jit_solution(16105920268681720922)
XLA Ops:
  7.2 1.7 copy.102
  8.9 1.5 copy.75
  10.4 7.3 %all-to-all-start = ((bf16[128,16,384]{2,0,1:T(8,128)(2,1)}), bf16[128,16,384]{2,0,1:T(8,128)(2,1)S(1)}, u32[]{:S(2)}, u32[]{:S(2)}) async-start(bf16[128,16,384]{2,0,1:T(8,128)(2,1)} %copy.75), calls=%async_computation | async-start | bytes 3145728 | tf_op jit(solution)/shard_map/all_to_all | solution.py:193
  18.0 1.5 copy.76
  19.5 22.7 %all-to-all-done = bf16[128,16,384]{2,0,1:T(8,128)(2,1)S(1)} async-done(((bf16[128,16,384]{2,0,1:T(8,128)(2,1)}), bf16[128,16,384]{2,0,1:T(8,128)(2,1)S(1)}, u32[]{:S(2)}, u32[]{:S(2)}) %all-to-all-start) | async-done | bytes 1572896 | tf_op jit(solution)/shard_map/all_to_all | solution.py:193
  42.2 4.4 %all-to-all-start.1 = ((bf16[128,16,384]{2,0,1:T(8,128)(2,1)}), bf16[128,16,384]{2,0,1:T(8,128)(2,1)}, u32[]{:S(2)}, u32[]{:S(2)}) async-start(bf16[128,16,384]{2,0,1:T(8,128)(2,1)} %copy.76), calls=%async_computation.1 | async-start | bytes 3145728 | tf_op jit(solution)/shard_map/all_to_all | solution.py:194
  47.1 21.7 %all-to-all-done.1 = bf16[128,16,384]{2,0,1:T(8,128)(2,1)} async-done(((bf16[128,16,384]{2,0,1:T(8,128)(2,1)}), bf16[128,16,384]{2,0,1:T(8,128)(2,1)}, u32[]{:S(2)}, u32[]{:S(2)}) %all-to-all-start.1) | async-done | bytes 1572896 | tf_op jit(solution)/shard_map/all_to_all | solution.py:194
  68.8 1.5 broadcast_in_dim.24
  70.3 3.8 all-to-all-start.2
  76.2 1.4 copy.78.qdoc_ref
  77.6 1.3 convert_reduce_fusion
  79.5 23.7 %all-to-all-done.2 = bf16[256,16,256]{2,0,1:T(8,128)(2,1)S(1)} async-done(((bf16[256,16,256]{2,0,1:T(8,128)(2,1)}), bf16[256,16,256]{2,0,1:T(8,128)(2,1)S(1)}, u32[]{:S(2)}, u32[]{:S(2)}) %all-to-all-start.2) | async-done | bytes 2097184 | tf_op jit(solution)/shard_map/all_to_all | solution.py:195
  103.3 1.3 copy-done.2
  104.6 65.7 %band_attention.1 = (bf16[2048,384]{1,0:T(8,128)(2,1)}, bf16[2048,384]{1,0:T(8,128)(2,1)}, f32[256,4096]{1,0:T(8,128)}) custom-call(s32[2048,1]{1,0:T(8,128)} %copy.78.qdoc_ref, s32[1,4096]{1,0:T(1,128)} %compare_select_fusion.kdoc_ref, bf16[2048,384]{1,0:T(8,128)(2,1)} %bitcast.81, bf16[2048,384]{1,0:T(8,128)(2,1)} %bitcast.8.go_ref, bf16[4096,256]{1,0:T(8,128)(2,1)} %bitcast.74), custom_call_target="tpu_custom_call" | custom-call | flops 21743271936 | bytes 12582912 | tf_op jit(solution)/shard_map/band_attention/pallas_call | solution.py:74
  170.3 2.5 convert_element_type.37
  173.0 31.3 %all_to_all.133 = bf16[16,256,256]{1,2,0:T(8,128)(2,1)S(1)} all-to-all(bf16[16,256,256]{1,2,0:T(8,128)(2,1)S(1)} %bitcast.69), channel_id=1, replica_groups=mesh['dp'=8,'ctx'=16] {'ctx'}, dimensions={0} | all-to-all | bytes 4194304 | tf_op jit(solution)/shard_map/all_to_all | solution.py:209
  204.6 1.0 copy.84
  205.7 3.7 all-to-all-start.3
  209.5 8.7 %copy.85 = bf16[1,256,12288]{1,2,0:T(8,128)(2,1)} copy(bf16[1,256,12288]{2,1,0:T(8,128)(2,1)} %param.8) | data formatting | bytes 12582912 | tf_op args[2]
  218.2 6.1 %copy.86 = bf16[8,256,4,4,96]{1,4,3,2,0:T(8,128)(2,1)} copy(bf16[8,256,4,4,96]{1,4,0,2,3:T(8,128)(2,1)} %bitcast.67) | data formatting | bytes 12582912 | tf_op jit(solution)/shard_map/transpose | solution.py:156
  224.3 5.2 %constant_dynamic-slice_fusion = (bf16[1,256,1536]{1,2,0:T(8,128)(2,1)}, bf16[1,256,1536]{1,2,0:T(8,128)(2,1)}, bf16[1,256,1536]{1,2,0:T(8,128)(2,1)}, bf16[1,25...) fusion(bf16[8,256,1536]{1,2,0:T(8,128)(2,1)} %bitcast.66, ...), kind=kLoop, calls=%fused_computation.9 | loop fusion | bytes 12582944 | tf_op jit(solution)/shard_map/jit(dynamic_index_in_dim)/dynamic_slice | solution.py:161
  229.5 1.3 copy.88
  230.7 1.2 copy.89
  231.9 1.9 collective-permute-start.1
  233.9 7.3 %all-to-all-start.4 = ((bf16[16,128,384]{2,1,0:T(8,128)(2,1)}), bf16[16,128,384]{2,1,0:T(8,128)(2,1)}, u32[]{:S(2)}, u32[]{:S(2)}) async-start(bf16[16,128,384]{2,1,0:T(8,128)(2,1)} %bitcast.77), calls=%async_computation.4 | async-start | bytes 3145728 | tf_op jit(solution)/shard_map/all_to_all | solution.py:207
  241.2 2.3 copy.90
  243.5 2.6 collective-permute-start.2
  246.1 2.4 copy.91
  248.5 1.2 collective-permute-start.3
  249.7 2.3 copy.92
  252.0 2.6 collective-permute-start.4
  254.6 2.3 copy.93
  256.9 1.3 copy.94
  258.2 1.0 collective-permute-start.5
  259.2 10.7 %collective-permute-start.6 = (bf16[256,1536]{1,0:T(8,128)(2,1)}, bf16[256,1536]{1,0:T(8,128)(2,1)}, u32[]{:S(2)}, u32[]{:S(2)}) collective-permute-start(bf16[256,1536]{1,0:T(8,128)(2,1)} %bitcast.87), channel_id=1, source_target_pairs={{0,112},{16,0},{32,16},{48,32},{64,48},{80,64},{96,80},{112,96},{1... | collective-permute-start | bytes 2359304 | tf_op jit(solution)/shard_map/ppermute | solution.py:163
  269.9 1.4 copy.87
  271.3 2.8 copy.100
  274.1 2.8 copy.101
  276.9 9.5 %collective-permute-done.2.refs_3_ = bf16[256,1536]{1,0:T(8,128)(2,1)S(1)} collective-permute-done((bf16[256,1536]{1,0:T(8,128)(2,1)}, bf16[256,1536]{1,0:T(8,128)(2,1)S(1)}, u32[]{:S(2)}, u32[]{:S(2)}) %collective-permute-start.2) | collective-permute-done | bytes 786464 | tf_op jit(solution)/shard_map/ppermute | solution.py:163
  286.3 3.6 collective-permute-done.3.refs_4_
  289.9 11.0 %collective-permute-done.4.refs_5_ = bf16[256,1536]{1,0:T(8,128)(2,1)} collective-permute-done((bf16[256,1536]{1,0:T(8,128)(2,1)}, bf16[256,1536]{1,0:T(8,128)(2,1)}, u32[]{:S(2)}, u32[]{:S(2)}) %collective-permute-start.4) | collective-permute-done | bytes 786464 | tf_op jit(solution)/shard_map/ppermute | solution.py:163
  301.0 2.4 collective-permute-done.5.refs_6_
  303.4 10.7 %collective-permute-done.6.refs_7_ = bf16[256,1536]{1,0:T(8,128)(2,1)} collective-permute-done((bf16[256,1536]{1,0:T(8,128)(2,1)}, bf16[256,1536]{1,0:T(8,128)(2,1)}, u32[]{:S(2)}, u32[]{:S(2)}) %collective-permute-start.6) | collective-permute-done | bytes 786464 | tf_op jit(solution)/shard_map/ppermute | solution.py:163
  314.1 10.8 %weight_product.1 = bf16[1536,1024]{1,0:T(8,128)(2,1)} custom-call(s32[1]{0:T(128)} %bitcast.22.me_ref, bf16[256,1536]{1,0:T(8,128)(2,1)S(1)} %bitcast.65, bf16[256,1536]{1,0:T(8,128)(2,1)S(1)} %collective-permute-done.refs_1_, bf16[256,1536]{1,0:T(8,128)(2,1)S(1)} %collective-permute-done.1.refs_2_, bf16[256,1536]{1,0:T(8,128)(2,1)S(1)} %collective-permute-done.2.refs_3_, ...), custom_call_target="tpu_custom_call" | custom-call | flops 6442450944 | bytes 13631488 | tf_op jit(solution)/shard_map/weight_product/pallas_call | solution.py:130
  325.0 40.4 %reduce-scatter.3.cloned.1.call-done = bf16[384,1024]{1,0:T(8,128)(2,1)} async-done(((bf16[1536,1024]{1,0:T(8,128)(2,1)}), bf16[384,1024]{1,0:T(8,128)(2,1)}) %reduce-scatter.3.cloned.1.call-update) | async-done | bytes 786448 | tf_op jit(solution)/shard_map/reduce_scatter | solution.py:173
  365.4 24.8 %reduce-scatter.5.cloned.1.call-done = bf16[96,1024]{1,0:T(8,128)(2,1)} async-done(((bf16[384,1024]{1,0:T(8,128)(2,1)}), bf16[96,1024]{1,0:T(8,128)(2,1)}) %reduce-scatter.5.cloned.1.call-update) | async-done | bytes 196624 | tf_op jit(solution)/shard_map/reduce_scatter | solution.py:174
  390.2 1.0 copy_bitcast_fusion.1
  391.2 13.1 %all_to_all.134 = f32[96,8,128]{2,0,1:T(8,128)S(1)} all-to-all(f32[96,8,128]{2,0,1:T(8,128)S(1)} %copy_bitcast_fusion.1), channel_id=1, replica_groups=mesh['dp'=8,'ctx'=16] {'dp'}, dimensions={1} | all-to-all | bytes 786432 | tf_op jit(solution)/shard_map/all_to_all | solution.py:175
  (40 shorter events, 4.1 us)
Async XLA Ops:
  10.4 7.3 %copy-start.3 = (bf16[1,128,6144]{2,1,0:T(8,128)(2,1)S(1)}, bf16[1,128,6144]{2,1,0:T(8,128)(2,1)}, u32[]{:S(2)}) copy-start(bf16[1,128,6144]{2,1,0:T(8,128)(2,1)} %param.9) | copy-start | bytes 4718596
  10.4 31.8 %all-to-all-start = ((bf16[128,16,384]{2,0,1:T(8,128)(2,1)}), bf16[128,16,384]{2,0,1:T(8,128)(2,1)S(1)}, u32[]{:S(2)}, u32[]{:S(2)}) async-start(bf16[128,16,384]{2,0,1:T(8,128)(2,1)} %copy.75), calls=%async_computation | async-start | bytes 3145728 | tf_op jit(solution)/shard_map/all_to_all | solution.py:193
  19.5 27.1 %copy-start.5 = (bf16[1,256,1024]{2,1,0:T(8,128)(2,1)S(1)}, bf16[1,256,1024]{2,1,0:T(8,128)(2,1)}, u32[]{:S(2)}) copy-start(bf16[1,256,1024]{2,1,0:T(8,128)(2,1)} %param.7) | copy-start | bytes 1572868
  42.2 4.8 %copy-start.4 = (bf16[128,16,384]{2,0,1:T(8,128)(2,1)}, bf16[128,16,384]{2,0,1:T(8,128)(2,1)S(1)}, u32[]{:S(2)}) copy-start(bf16[128,16,384]{2,0,1:T(8,128)(2,1)S(1)} %all-to-all-done) | copy-start | bytes 4718596
  42.2 26.6 %all-to-all-start.1 = ((bf16[128,16,384]{2,0,1:T(8,128)(2,1)}), bf16[128,16,384]{2,0,1:T(8,128)(2,1)}, u32[]{:S(2)}, u32[]{:S(2)}) async-start(bf16[128,16,384]{2,0,1:T(8,128)(2,1)} %copy.76), calls=%async_computation.1 | async-start | bytes 3145728 | tf_op jit(solution)/shard_map/all_to_all | solution.py:194
  70.3 3.9 copy-start.6
  70.3 32.9 %all-to-all-start.2 = ((bf16[256,16,256]{2,0,1:T(8,128)(2,1)}), bf16[256,16,256]{2,0,1:T(8,128)(2,1)S(1)}, u32[]{:S(2)}, u32[]{:S(2)}) async-start(bf16[256,16,256]{2,0,1:T(8,128)(2,1)} %bitcast.9), calls=%async_computation.2 | async-start | bytes 4194304 | tf_op jit(solution)/shard_map/all_to_all | solution.py:195
  74.2 202.7 %all-gather.2.cloned.1.call-start = ((), (), s32[]{:S(2)}) async-start(), calls=%async_computation.9 | async-start | bytes 4718592 | tf_op jit(solution)/shard_map/all_gather | solution.py:219
  103.3 1.3 copy-start.2
  205.7 28.2 %all-to-all-start.3 = ((bf16[16,128,384]{2,1,0:T(8,128)(2,1)}), bf16[16,128,384]{2,1,0:T(8,128)(2,1)S(1)}, u32[]{:S(2)}, u32[]{:S(2)}) async-start(bf16[16,128,384]{2,1,0:T(8,128)(2,1)} %bitcast.78), calls=%async_computation.3 | async-start | bytes 3145728 | tf_op jit(solution)/shard_map/all_to_all | solution.py:206
  230.7 27.4 %collective-permute-start = (bf16[256,1536]{1,0:T(8,128)(2,1)}, bf16[256,1536]{1,0:T(8,128)(2,1)S(1)}, u32[]{:S(2)}, u32[]{:S(2)}) collective-permute-start(bf16[256,1536]{1,0:T(8,128)(2,1)} %bitcast.88), channel_id=1, source_target_pairs={{0,16},{16,32},{32,48},{48,64},{64,80},{80,96},{96,112},{112,0},{1... | collective-permute-start | bytes 2359304 | tf_op jit(solution)/shard_map/ppermute | solution.py:163
  231.9 27.3 %collective-permute-start.1 = (bf16[256,1536]{1,0:T(8,128)(2,1)}, bf16[256,1536]{1,0:T(8,128)(2,1)S(1)}, u32[]{:S(2)}, u32[]{:S(2)}) collective-permute-start(bf16[256,1536]{1,0:T(8,128)(2,1)} %bitcast.85), channel_id=1, source_target_pairs={{0,32},{16,48},{32,64},{48,80},{64,96},{80,112},{96,0},{112,16},{1... | collective-permute-start | bytes 2359304 | tf_op jit(solution)/shard_map/ppermute | solution.py:163
  233.9 9.6 %copy-start = (bf16[16,128,384]{2,1,0:T(8,128)(2,1)}, bf16[16,128,384]{2,1,0:T(8,128)(2,1)S(1)}, u32[]{:S(2)}) copy-start(bf16[16,128,384]{2,1,0:T(8,128)(2,1)S(1)} %all-to-all-done.3) | copy-start | bytes 4718596
  233.9 40.2 %all-to-all-start.4 = ((bf16[16,128,384]{2,1,0:T(8,128)(2,1)}), bf16[16,128,384]{2,1,0:T(8,128)(2,1)}, u32[]{:S(2)}, u32[]{:S(2)}) async-start(bf16[16,128,384]{2,1,0:T(8,128)(2,1)} %bitcast.77), calls=%async_computation.4 | async-start | bytes 3145728 | tf_op jit(solution)/shard_map/all_to_all | solution.py:207
  241.1 124.2 %reduce-scatter.3.cloned.1.call-start = ((), (), s32[]{:S(2)}) async-start(), calls=%async_computation.10 | async-start | bytes 3932160 | tf_op jit(solution)/shard_map/reduce_scatter | solution.py:173
  243.5 42.9 %collective-permute-start.2 = (bf16[256,1536]{1,0:T(8,128)(2,1)}, bf16[256,1536]{1,0:T(8,128)(2,1)S(1)}, u32[]{:S(2)}, u32[]{:S(2)}) collective-permute-start(bf16[256,1536]{1,0:T(8,128)(2,1)} %bitcast.83), channel_id=1, source_target_pairs={{0,48},{16,64},{32,80},{48,96},{64,112},{80,0},{96,16},{112,32},{1... | collective-permute-start | bytes 2359304 | tf_op jit(solution)/shard_map/ppermute | solution.py:163
  246.1 10.8 %copy-start.1 = (bf16[1,256,1536]{1,2,0:T(8,128)(2,1)S(1)}, bf16[1,256,1536]{1,2,0:T(8,128)(2,1)}, u32[]{:S(2)}) copy-start(bf16[1,256,1536]{1,2,0:T(8,128)(2,1)} %get-tuple-element.24) | copy-start | bytes 2359300
  248.5 41.5 %collective-permute-start.3 = (bf16[256,1536]{1,0:T(8,128)(2,1)}, bf16[256,1536]{1,0:T(8,128)(2,1)}, u32[]{:S(2)}, u32[]{:S(2)}) collective-permute-start(bf16[256,1536]{1,0:T(8,128)(2,1)} %bitcast.84), channel_id=1, source_target_pairs={{0,64},{16,80},{32,96},{48,112},{64,0},{80,16},{96,32},{112,48},{1... | collective-permute-start | bytes 2359304 | tf_op jit(solution)/shard_map/ppermute | solution.py:163
  252.0 49.0 %collective-permute-start.4 = (bf16[256,1536]{1,0:T(8,128)(2,1)}, bf16[256,1536]{1,0:T(8,128)(2,1)}, u32[]{:S(2)}, u32[]{:S(2)}) collective-permute-start(bf16[256,1536]{1,0:T(8,128)(2,1)} %bitcast.86), channel_id=1, source_target_pairs={{0,80},{16,96},{32,112},{48,0},{64,16},{80,32},{96,48},{112,64},{1... | collective-permute-start | bytes 2359304 | tf_op jit(solution)/shard_map/ppermute | solution.py:163
  258.2 45.2 %collective-permute-start.5 = (bf16[256,1536]{1,0:T(8,128)(2,1)}, bf16[256,1536]{1,0:T(8,128)(2,1)}, u32[]{:S(2)}, u32[]{:S(2)}) collective-permute-start(bf16[256,1536]{1,0:T(8,128)(2,1)} %bitcast.89), channel_id=1, source_target_pairs={{0,96},{16,112},{32,0},{48,16},{64,32},{80,48},{96,64},{112,80},{1... | collective-permute-start | bytes 2359304 | tf_op jit(solution)/shard_map/ppermute | solution.py:163
  259.2 54.9 %collective-permute-start.6 = (bf16[256,1536]{1,0:T(8,128)(2,1)}, bf16[256,1536]{1,0:T(8,128)(2,1)}, u32[]{:S(2)}, u32[]{:S(2)}) collective-permute-start(bf16[256,1536]{1,0:T(8,128)(2,1)} %bitcast.87), channel_id=1, source_target_pairs={{0,112},{16,0},{32,16},{48,32},{64,48},{80,64},{96,80},{112,96},{1... | collective-permute-start | bytes 2359304 | tf_op jit(solution)/shard_map/ppermute | solution.py:163
  324.9 65.3 %reduce-scatter.5.cloned.1.call-start = ((), (), s32[]{:S(2)}) async-start(), calls=%async_computation.11 | async-start | bytes 983040 | tf_op jit(solution)/shard_map/reduce_scatter | solution.py:174
Sparse Core Ops, SparseCore 0:
  205.8 30.7 all-gather.1
  325.0 40.2 reduce-scatter.2
  367.8 22.3 reduce-scatter.4

commit v8 on v7

--- a/solution.py
+++ b/solution.py
@@ -164,15 +164,18 @@
     return me, received
 
 
-def weight_gradient(me, received, grad_all):
+def weight_gradient(me, received, grad_all, grad_query_heads):
     partial = stacked_weight_product(me, received, grad_all)
     ctx = lax.axis_size("ctx")
     across = ctx // CTX_ROWS
     along_x = [[y * across + x for x in range(across)] for y in range(CTX_ROWS)]
     along_y = [[y * across + x for y in range(CTX_ROWS)] for x in range(across)]
     reduced = lax.psum_scatter(partial, "ctx", scatter_dimension=0, axis_index_groups=along_x, tiled=True)
+    reduced, grad_query_heads = lax.optimization_barrier((reduced, grad_query_heads))
+    grad_query = lax.all_to_all(grad_query_heads, "ctx", split_axis=0, concat_axis=1, tiled=True)
     reduced = lax.psum_scatter(reduced, "ctx", scatter_dimension=0, axis_index_groups=along_y, tiled=True)
-    return lax.all_to_all(reduced.astype(jnp.float32), "dp", split_axis=1, concat_axis=0, tiled=True)
+    weight = lax.all_to_all(reduced.astype(jnp.float32), "dp", split_axis=1, concat_axis=0, tiled=True)
+    return weight, grad_query
 
 
 def local_body(queries, kv_proj, hidden, grad_out, doc_lengths, slab_offsets):
@@ -202,10 +205,7 @@
     q_doc = doc_index(query_pos, bounds)
     k_doc = jnp.where(key_pos >= 0, doc_index(key_pos, bounds), -1)
     attended_heads, grad_query_heads, grad_head = head_attention(head_queries, head_upstream, head_keys, q_doc, k_doc)
-    attended, grad_query = (
-        lax.all_to_all(attended_heads, "ctx", split_axis=0, concat_axis=1, tiled=True),
-        lax.all_to_all(grad_query_heads, "ctx", split_axis=0, concat_axis=1, tiled=True),
-    )
+    attended = lax.all_to_all(attended_heads, "ctx", split_axis=0, concat_axis=1, tiled=True)
     partial_sums = lax.all_to_all(
         grad_head.T.astype(jnp.bfloat16), "ctx", split_axis=0, concat_axis=1, tiled=True
     )
@@ -217,8 +217,8 @@
     ).reshape(partial_sums.shape[0], key_value_width)
     grad_low = grad_keys.astype(jnp.bfloat16)
     grad_all = lax.all_gather(grad_low, "dp", axis=0, tiled=False)
-    attended, grad_query, grad_all = lax.optimization_barrier((attended, grad_query, grad_all))
-    grad_weight = weight_gradient(me, received, grad_all)
+    attended, grad_all = lax.optimization_barrier((attended, grad_all))
+    grad_weight, grad_query = weight_gradient(me, received, grad_all, grad_query_heads)
     return (attended[None], grad_query[None], grad_low[None], grad_weight)
 
 

time: 413 us -> 416 us (level)
  blocking collectives: 44.5 us -> 31.3 us
  starting transfers between devices: 46.8 us -> 55.2 us
  waiting for transfers between devices: 171 us -> 179 us
    all_to_all x1 -> x0, blocking collectives: 13.1 us -> none  [weight_gradient(): lax.all_to_all(reduced.astype(jnp.float32), 'dp', split_axis=1, concat_ax...]
    all_to_all x1 -> x2, waiting for transfers between devices: 0.01 us -> 6.36 us  [the longest x1 6.36 us: weight_gradient(): lax.all_to_all(reduced.astype(jnp.float32), 'dp', split_axis=1, concat_ax...]
    ppermute x7, starting transfers between devices: 20.1 us -> 25.4 us  [send_hidden(): received.append(lax.ppermute(outgoing, 'dp', pairs))]
    reduce_scatter x1, waiting for transfers between devices: 24.8 us -> 29.6 us  [weight_gradient(): lax.psum_scatter(reduced, 'ctx', scatter_dimension=0, axis_index_groups=a...]
    all_to_all x1 -> x2, starting transfers between devices: 7.25 us -> 9.81 us  [the longest x1 5.32 us: weight_gradient(): lax.all_to_all(grad_query_heads, 'ctx', split_axis=0, concat_axis=1, tile...]
    unnamed x18 -> x14, local copies, waits for them, and re-layouts: 12.8 us -> 12.8 us
  transfers between devices with their start and end apart: 15 -> 16, of which waited for: 10 -> 12; matrix products, arithmetic and copies ran while one was open for 11% -> 11% of each run, Pallas kernels for 0% -> 0%
where the time goes in v8:
time: 416 us; the launch traced here: 414 us
  waiting for transfers between devices  179 us (43%)
  Pallas kernels  76.5 us (18%)
  starting transfers between devices  55.2 us (13%)
  local copies, waits for them, and re-layouts  50.1 us (12%)
  blocking collectives  31.3 us (8%)
  between operations  14.7 us (4%)
  other arithmetic  7.43 us (2%)
    pallas_call x1, Pallas kernels, head_attention(): pl.pallas_call(kernel, grid=grid, in_specs=[pl.BlockSpec((bq, 1), lambda...  65.7 us
    reduce_scatter x1, waiting for transfers between devices, weight_gradient(): lax.psum_scatter(partial, 'ctx', scatter_dimension=0, axis_index_groups=a...  40.1 us
    ppermute x7, waiting for transfers between devices, send_hidden(): received.append(lax.ppermute(outgoing, 'dp', pairs))  34.9 us
    all_to_all x1, blocking collectives, local_body(): lax.all_to_all(grad_head.T.astype(jnp.bfloat16), 'ctx', split_axis=0, con...  31.3 us
    reduce_scatter x1, waiting for transfers between devices, weight_gradient(): lax.psum_scatter(reduced, 'ctx', scatter_dimension=0, axis_index_groups=a...  29.6 us
    ppermute x7, starting transfers between devices, send_hidden(): received.append(lax.ppermute(outgoing, 'dp', pairs))  25.4 us
    all_to_all x1, waiting for transfers between devices, local_body(): lax.all_to_all(copies, 'ctx', split_axis=1, concat_axis=0, tiled=True)  23.7 us
    all_to_all x1, waiting for transfers between devices, local_body(): lax.all_to_all(query_matrix_rows, 'ctx', split_axis=1, concat_axis=0, til...  22.7 us
  transfers between devices with their start and end apart: 16, of which 12 were waited for; matrix products, arithmetic and copies ran while one was open for 11% of the time, Pallas kernels for 0%

profile of v8, /device:TPU:0, one launch (start us, length us, event | category | flops | bytes accessed | tf_op | source)
XLA Modules:
  0.0 414.4 jit_solution(8334287793024395129)
XLA Ops:
  7.2 1.7 copy.101
  8.9 1.5 copy.75
  10.4 7.3 %all-to-all-start = ((bf16[128,16,384]{2,0,1:T(8,128)(2,1)}), bf16[128,16,384]{2,0,1:T(8,128)(2,1)S(1)}, u32[]{:S(2)}, u32[]{:S(2)}) async-start(bf16[128,16,384]{2,0,1:T(8,128)(2,1)} %copy.75), calls=%async_computation | async-start | bytes 3145728 | tf_op jit(solution)/shard_map/all_to_all | solution.py:196
  18.0 1.5 copy.76
  19.5 22.7 %all-to-all-done = bf16[128,16,384]{2,0,1:T(8,128)(2,1)S(1)} async-done(((bf16[128,16,384]{2,0,1:T(8,128)(2,1)}), bf16[128,16,384]{2,0,1:T(8,128)(2,1)S(1)}, u32[]{:S(2)}, u32[]{:S(2)}) %all-to-all-start) | async-done | bytes 1572896 | tf_op jit(solution)/shard_map/all_to_all | solution.py:196
  42.2 4.4 %all-to-all-start.1 = ((bf16[128,16,384]{2,0,1:T(8,128)(2,1)}), bf16[128,16,384]{2,0,1:T(8,128)(2,1)}, u32[]{:S(2)}, u32[]{:S(2)}) async-start(bf16[128,16,384]{2,0,1:T(8,128)(2,1)} %copy.76), calls=%async_computation.1 | async-start | bytes 3145728 | tf_op jit(solution)/shard_map/all_to_all | solution.py:197
  47.1 21.7 %all-to-all-done.1 = bf16[128,16,384]{2,0,1:T(8,128)(2,1)} async-done(((bf16[128,16,384]{2,0,1:T(8,128)(2,1)}), bf16[128,16,384]{2,0,1:T(8,128)(2,1)}, u32[]{:S(2)}, u32[]{:S(2)}) %all-to-all-start.1) | async-done | bytes 1572896 | tf_op jit(solution)/shard_map/all_to_all | solution.py:197
  68.8 1.5 broadcast_in_dim.24
  70.3 3.8 all-to-all-start.2
  76.2 1.4 copy.78.qdoc_ref
  77.6 1.3 convert_reduce_fusion
  79.5 23.7 %all-to-all-done.2 = bf16[256,16,256]{2,0,1:T(8,128)(2,1)S(1)} async-done(((bf16[256,16,256]{2,0,1:T(8,128)(2,1)}), bf16[256,16,256]{2,0,1:T(8,128)(2,1)S(1)}, u32[]{:S(2)}, u32[]{:S(2)}) %all-to-all-start.2) | async-done | bytes 2097184 | tf_op jit(solution)/shard_map/all_to_all | solution.py:198
  103.3 1.3 copy-done
  104.6 65.7 %band_attention.1 = (bf16[2048,384]{1,0:T(8,128)(2,1)}, bf16[2048,384]{1,0:T(8,128)(2,1)}, f32[256,4096]{1,0:T(8,128)}) custom-call(s32[2048,1]{1,0:T(8,128)} %copy.78.qdoc_ref, s32[1,4096]{1,0:T(1,128)} %compare_select_fusion.kdoc_ref, bf16[2048,384]{1,0:T(8,128)(2,1)} %bitcast.76, bf16[2048,384]{1,0:T(8,128)(2,1)} %bitcast.8.go_ref, bf16[4096,256]{1,0:T(8,128)(2,1)} %bitcast.71), custom_call_target="tpu_custom_call" | custom-call | flops 21743271936 | bytes 12582912 | tf_op jit(solution)/shard_map/band_attention/pallas_call | solution.py:74
  170.3 2.5 convert_element_type.37
  173.0 31.3 %all_to_all.130 = bf16[16,256,256]{1,2,0:T(8,128)(2,1)S(1)} all-to-all(bf16[16,256,256]{1,2,0:T(8,128)(2,1)S(1)} %bitcast.66), channel_id=1, replica_groups=mesh['dp'=8,'ctx'=16] {'ctx'}, dimensions={0} | all-to-all | bytes 4194304 | tf_op jit(solution)/shard_map/all_to_all | solution.py:209
  204.6 1.0 copy.83
  205.8 8.7 %copy.84 = bf16[1,256,12288]{1,2,0:T(8,128)(2,1)} copy(bf16[1,256,12288]{2,1,0:T(8,128)(2,1)} %param.8) | data formatting | bytes 12582912 | tf_op args[2]
  214.4 6.4 %copy.85 = bf16[8,256,4,4,96]{1,4,3,2,0:T(8,128)(2,1)} copy(bf16[8,256,4,4,96]{1,4,0,2,3:T(8,128)(2,1)} %bitcast.64) | data formatting | bytes 12582912 | tf_op jit(solution)/shard_map/transpose | solution.py:156
  220.8 4.7 %constant_dynamic-slice_fusion = (bf16[1,256,1536]{1,2,0:T(8,128)(2,1)S(1)}, bf16[1,256,1536]{1,2,0:T(8,128)(2,1)}, bf16[1,256,1536]{1,2,0:T(8,128)(2,1)}, bf16[...) fusion(bf16[8,256,1536]{1,2,0:T(8,128)(2,1)} %bitcast.63, ...), kind=kLoop, calls=%fused_computation.9 | loop fusion | bytes 12582944 | tf_op jit(solution)/shard_map/jit(dynamic_index_in_dim)/dynamic_slice | solution.py:161
  225.5 1.2 copy.87
  226.7 1.2 copy.88
  227.9 1.8 collective-permute-start.1
  229.7 4.4 %all-to-all-start.3 = ((bf16[16,128,384]{2,1,0:T(8,128)(2,1)}), bf16[16,128,384]{2,1,0:T(8,128)(2,1)}, u32[]{:S(2)}, u32[]{:S(2)}) async-start(bf16[16,128,384]{2,1,0:T(8,128)(2,1)} %bitcast.74), calls=%async_computation.3 | async-start | bytes 3145728 | tf_op jit(solution)/shard_map/all_to_all | solution.py:208
  234.1 1.1 copy.89
  235.3 2.9 collective-permute-start.2
  238.2 2.3 copy.90
  240.4 1.2 collective-permute-start.3
  241.7 2.3 copy.91
  244.0 2.3 collective-permute-start.4
  246.3 2.4 copy.92
  248.7 1.2 copy.93
  249.8 1.3 collective-permute-done.refs_1_
  252.6 16.2 %collective-permute-start.6 = (bf16[256,1536]{1,0:T(8,128)(2,1)}, bf16[256,1536]{1,0:T(8,128)(2,1)}, u32[]{:S(2)}, u32[]{:S(2)}) collective-permute-start(bf16[256,1536]{1,0:T(8,128)(2,1)} %bitcast.81), channel_id=1, source_target_pairs={{0,112},{16,0},{32,16},{48,32},{64,48},{80,64},{96,80},{112,96},{1... | collective-permute-start | bytes 2359304 | tf_op jit(solution)/shard_map/ppermute | solution.py:163
  268.7 1.4 copy.86
  270.2 2.8 copy.100
  273.0 12.2 %collective-permute-done.2.refs_3_ = bf16[256,1536]{1,0:T(8,128)(2,1)S(1)} collective-permute-done((bf16[256,1536]{1,0:T(8,128)(2,1)}, bf16[256,1536]{1,0:T(8,128)(2,1)S(1)}, u32[]{:S(2)}, u32[]{:S(2)}) %collective-permute-start.2) | collective-permute-done | bytes 786464 | tf_op jit(solution)/shard_map/ppermute | solution.py:163
  285.2 1.2 collective-permute-done.3.refs_4_
  286.4 12.9 %collective-permute-done.4.refs_5_ = bf16[256,1536]{1,0:T(8,128)(2,1)} collective-permute-done((bf16[256,1536]{1,0:T(8,128)(2,1)}, bf16[256,1536]{1,0:T(8,128)(2,1)}, u32[]{:S(2)}, u32[]{:S(2)}) %collective-permute-start.4) | collective-permute-done | bytes 786464 | tf_op jit(solution)/shard_map/ppermute | solution.py:163
  299.3 6.8 %collective-permute-done.6.refs_7_ = bf16[256,1536]{1,0:T(8,128)(2,1)} collective-permute-done((bf16[256,1536]{1,0:T(8,128)(2,1)}, bf16[256,1536]{1,0:T(8,128)(2,1)}, u32[]{:S(2)}, u32[]{:S(2)}) %collective-permute-start.6) | collective-permute-done | bytes 786464 | tf_op jit(solution)/shard_map/ppermute | solution.py:163
  306.1 10.8 %weight_product.1 = bf16[1536,1024]{1,0:T(8,128)(2,1)} custom-call(s32[1]{0:T(128)} %bitcast.19.me_ref, bf16[256,1536]{1,0:T(8,128)(2,1)S(1)} %bitcast.62, bf16[256,1536]{1,0:T(8,128)(2,1)S(1)} %collective-permute-done.refs_1_, bf16[256,1536]{1,0:T(8,128)(2,1)S(1)} %collective-permute-done.1.refs_2_, bf16[256,1536]{1,0:T(8,128)(2,1)S(1)} %collective-permute-done.2.refs_3_, ...), custom_call_target="tpu_custom_call" | custom-call | flops 6442450944 | bytes 13631488 | tf_op jit(solution)/shard_map/weight_product/pallas_call | solution.py:130
  317.0 40.1 %reduce-scatter.3.cloned.1.call-done = bf16[384,1024]{1,0:T(8,128)(2,1)} async-done(((bf16[1536,1024]{1,0:T(8,128)(2,1)}), bf16[384,1024]{1,0:T(8,128)(2,1)}) %reduce-scatter.3.cloned.1.call-update) | async-done | bytes 786448 | tf_op jit(solution)/shard_map/reduce_scatter | solution.py:173
  357.1 5.3 %all-to-all-start.5 = ((bf16[16,128,384]{2,1,0:T(8,128)(2,1)}), bf16[16,128,384]{2,1,0:T(8,128)(2,1)S(1)}, u32[]{:S(2)}, u32[]{:S(2)}) async-start(bf16[16,128,384]{2,1,0:T(8,128)(2,1)} %bitcast.31), calls=%async_computation.6 | async-start | bytes 3145728 | tf_op jit(solution)/shard_map/all_to_all | solution.py:175
  362.4 29.6 %reduce-scatter.5.cloned.1.call-done = bf16[96,1024]{1,0:T(8,128)(2,1)} async-done(((bf16[384,1024]{1,0:T(8,128)(2,1)}), bf16[96,1024]{1,0:T(8,128)(2,1)}) %reduce-scatter.5.cloned.1.call-update) | async-done | bytes 196624 | tf_op jit(solution)/shard_map/reduce_scatter | solution.py:176
  392.0 1.7 copy_bitcast_fusion.1
  393.8 4.5 %all-to-all-start.6 = ((f32[96,8,128]{2,0,1:T(8,128)}), f32[96,8,128]{2,0,1:T(8,128)S(1)}, u32[]{:S(2)}, u32[]{:S(2)}) async-start(f32[96,8,128]{2,0,1:T(8,128)} %copy_bitcast_fusion.1), calls=%async_computation.8 | async-start | bytes 786432 | tf_op jit(solution)/shard_map/all_to_all | solution.py:177
  399.2 1.6 broadcast_in_dim.26
  400.8 6.4 %all-to-all-done.6 = f32[96,8,128]{2,0,1:T(8,128)S(1)} async-done(((f32[96,8,128]{2,0,1:T(8,128)}), f32[96,8,128]{2,0,1:T(8,128)S(1)}, u32[]{:S(2)}, u32[]{:S(2)}) %all-to-all-start.6) | async-done | bytes 393248 | tf_op jit(solution)/shard_map/all_to_all | solution.py:177
  (38 shorter events, 6.5 us)
Async XLA Ops:
  10.4 7.3 %copy-start.1 = (bf16[1,128,6144]{2,1,0:T(8,128)(2,1)S(1)}, bf16[1,128,6144]{2,1,0:T(8,128)(2,1)}, u32[]{:S(2)}) copy-start(bf16[1,128,6144]{2,1,0:T(8,128)(2,1)} %param.9) | copy-start | bytes 4718596
  10.4 31.8 %all-to-all-start = ((bf16[128,16,384]{2,0,1:T(8,128)(2,1)}), bf16[128,16,384]{2,0,1:T(8,128)(2,1)S(1)}, u32[]{:S(2)}, u32[]{:S(2)}) async-start(bf16[128,16,384]{2,0,1:T(8,128)(2,1)} %copy.75), calls=%async_computation | async-start | bytes 3145728 | tf_op jit(solution)/shard_map/all_to_all | solution.py:196
  19.5 27.1 %copy-start.3 = (bf16[1,256,1024]{2,1,0:T(8,128)(2,1)S(1)}, bf16[1,256,1024]{2,1,0:T(8,128)(2,1)}, u32[]{:S(2)}) copy-start(bf16[1,256,1024]{2,1,0:T(8,128)(2,1)} %param.7) | copy-start | bytes 1572868
  42.2 4.8 %copy-start.2 = (bf16[128,16,384]{2,0,1:T(8,128)(2,1)}, bf16[128,16,384]{2,0,1:T(8,128)(2,1)S(1)}, u32[]{:S(2)}) copy-start(bf16[128,16,384]{2,0,1:T(8,128)(2,1)S(1)} %all-to-all-done) | copy-start | bytes 4718596
  42.2 26.6 %all-to-all-start.1 = ((bf16[128,16,384]{2,0,1:T(8,128)(2,1)}), bf16[128,16,384]{2,0,1:T(8,128)(2,1)}, u32[]{:S(2)}, u32[]{:S(2)}) async-start(bf16[128,16,384]{2,0,1:T(8,128)(2,1)} %copy.76), calls=%async_computation.1 | async-start | bytes 3145728 | tf_op jit(solution)/shard_map/all_to_all | solution.py:197
  70.3 3.9 copy-start.4
  70.3 32.9 %all-to-all-start.2 = ((bf16[256,16,256]{2,0,1:T(8,128)(2,1)}), bf16[256,16,256]{2,0,1:T(8,128)(2,1)S(1)}, u32[]{:S(2)}, u32[]{:S(2)}) async-start(bf16[256,16,256]{2,0,1:T(8,128)(2,1)} %bitcast.9), calls=%async_computation.2 | async-start | bytes 4194304 | tf_op jit(solution)/shard_map/all_to_all | solution.py:198
  74.2 198.8 %all-gather.2.cloned.1.call-start = ((), (), s32[]{:S(2)}) async-start(), calls=%async_computation.9 | async-start | bytes 4718592 | tf_op jit(solution)/shard_map/all_gather | solution.py:219
  103.3 1.3 copy-start
  226.7 24.4 %collective-permute-start = (bf16[256,1536]{1,0:T(8,128)(2,1)}, bf16[256,1536]{1,0:T(8,128)(2,1)S(1)}, u32[]{:S(2)}, u32[]{:S(2)}) collective-permute-start(bf16[256,1536]{1,0:T(8,128)(2,1)} %bitcast.84), channel_id=1, source_target_pairs={{0,16},{16,32},{32,48},{48,64},{64,80},{80,96},{96,112},{112,0},{1... | collective-permute-start | bytes 2359304 | tf_op jit(solution)/shard_map/ppermute | solution.py:163
  227.9 24.7 %collective-permute-start.1 = (bf16[256,1536]{1,0:T(8,128)(2,1)}, bf16[256,1536]{1,0:T(8,128)(2,1)S(1)}, u32[]{:S(2)}, u32[]{:S(2)}) collective-permute-start(bf16[256,1536]{1,0:T(8,128)(2,1)} %bitcast.83), channel_id=1, source_target_pairs={{0,32},{16,48},{32,64},{48,80},{64,96},{80,112},{96,0},{112,16},{1... | collective-permute-start | bytes 2359304 | tf_op jit(solution)/shard_map/ppermute | solution.py:163
  229.7 40.5 %all-to-all-start.3 = ((bf16[16,128,384]{2,1,0:T(8,128)(2,1)}), bf16[16,128,384]{2,1,0:T(8,128)(2,1)}, u32[]{:S(2)}, u32[]{:S(2)}) async-start(bf16[16,128,384]{2,1,0:T(8,128)(2,1)} %bitcast.74), calls=%async_computation.3 | async-start | bytes 3145728 | tf_op jit(solution)/shard_map/all_to_all | solution.py:208
  234.1 123.0 %reduce-scatter.3.cloned.1.call-start = ((), (), s32[]{:S(2)}) async-start(), calls=%async_computation.10 | async-start | bytes 3932160 | tf_op jit(solution)/shard_map/reduce_scatter | solution.py:173
  235.3 49.9 %collective-permute-start.2 = (bf16[256,1536]{1,0:T(8,128)(2,1)}, bf16[256,1536]{1,0:T(8,128)(2,1)S(1)}, u32[]{:S(2)}, u32[]{:S(2)}) collective-permute-start(bf16[256,1536]{1,0:T(8,128)(2,1)} %bitcast.78), channel_id=1, source_target_pairs={{0,48},{16,64},{32,80},{48,96},{64,112},{80,0},{96,16},{112,32},{1... | collective-permute-start | bytes 2359304 | tf_op jit(solution)/shard_map/ppermute | solution.py:163
  240.4 45.9 %collective-permute-start.3 = (bf16[256,1536]{1,0:T(8,128)(2,1)}, bf16[256,1536]{1,0:T(8,128)(2,1)}, u32[]{:S(2)}, u32[]{:S(2)}) collective-permute-start(bf16[256,1536]{1,0:T(8,128)(2,1)} %bitcast.79), channel_id=1, source_target_pairs={{0,64},{16,80},{32,96},{48,112},{64,0},{80,16},{96,32},{112,48},{1... | collective-permute-start | bytes 2359304 | tf_op jit(solution)/shard_map/ppermute | solution.py:163
  244.0 55.3 %collective-permute-start.4 = (bf16[256,1536]{1,0:T(8,128)(2,1)}, bf16[256,1536]{1,0:T(8,128)(2,1)}, u32[]{:S(2)}, u32[]{:S(2)}) collective-permute-start(bf16[256,1536]{1,0:T(8,128)(2,1)} %bitcast.80), channel_id=1, source_target_pairs={{0,80},{16,96},{32,112},{48,0},{64,16},{80,32},{96,48},{112,64},{1... | collective-permute-start | bytes 2359304 | tf_op jit(solution)/shard_map/ppermute | solution.py:163
  251.1 48.2 %collective-permute-start.5 = (bf16[256,1536]{1,0:T(8,128)(2,1)}, bf16[256,1536]{1,0:T(8,128)(2,1)}, u32[]{:S(2)}, u32[]{:S(2)}) collective-permute-start(bf16[256,1536]{1,0:T(8,128)(2,1)} %bitcast.82), channel_id=1, source_target_pairs={{0,96},{16,112},{32,0},{48,16},{64,32},{80,48},{96,64},{112,80},{1... | collective-permute-start | bytes 2359304 | tf_op jit(solution)/shard_map/ppermute | solution.py:163
  252.6 53.6 %collective-permute-start.6 = (bf16[256,1536]{1,0:T(8,128)(2,1)}, bf16[256,1536]{1,0:T(8,128)(2,1)}, u32[]{:S(2)}, u32[]{:S(2)}) collective-permute-start(bf16[256,1536]{1,0:T(8,128)(2,1)} %bitcast.81), channel_id=1, source_target_pairs={{0,112},{16,0},{32,16},{48,32},{64,48},{80,64},{96,80},{112,96},{1... | collective-permute-start | bytes 2359304 | tf_op jit(solution)/shard_map/ppermute | solution.py:163
  316.9 75.1 %reduce-scatter.5.cloned.1.call-start = ((), (), s32[]{:S(2)}) async-start(), calls=%async_computation.11 | async-start | bytes 983040 | tf_op jit(solution)/shard_map/reduce_scatter | solution.py:176
  357.1 36.6 %all-to-all-start.5 = ((bf16[16,128,384]{2,1,0:T(8,128)(2,1)}), bf16[16,128,384]{2,1,0:T(8,128)(2,1)S(1)}, u32[]{:S(2)}, u32[]{:S(2)}) async-start(bf16[16,128,384]{2,1,0:T(8,128)(2,1)} %bitcast.31), calls=%async_computation.6 | async-start | bytes 3145728 | tf_op jit(solution)/shard_map/all_to_all | solution.py:175
  393.8 13.4 %all-to-all-start.6 = ((f32[96,8,128]{2,0,1:T(8,128)}), f32[96,8,128]{2,0,1:T(8,128)S(1)}, u32[]{:S(2)}, u32[]{:S(2)}) async-start(f32[96,8,128]{2,0,1:T(8,128)} %copy_bitcast_fusion.1), calls=%async_computation.8 | async-start | bytes 786432 | tf_op jit(solution)/shard_map/all_to_all | solution.py:177
Sparse Core Ops, SparseCore 0:
  205.8 34.1 all-gather.1
  317.1 39.9 reduce-scatter.2
  359.5 32.4 reduce-scatter.4
